TPU v7x, 128 devices: a whole 4x4x4 slice. The times are simulated.
128 devices in a mesh: expert: 8 (over z, core), ffn: 16 (over x, y).
Axes of the slice: x: 4, y: 4, z: 4, core: 2. Of those that a mesh axis runs over, the one named last changes fastest.
Arguments:
- queries: bfloat16 [512, 4096], P(('expert', 'ffn')), may hold values from -8 to 8
- new_keys: bfloat16 [512, 1024], P(('expert', 'ffn')), may hold values from -4 to 4
- new_values: bfloat16 [512, 1024], P(('expert', 'ffn')), may hold values from -5 to 5
- key_cache: bfloat16 [512, 512, 1024], P(('expert', 'ffn')), may hold values from -4 to 4
- value_cache: bfloat16 [512, 512, 1024], P(('expert', 'ffn')), may hold values from -5 to 5
- lengths: int32 [512], P(('expert', 'ffn')), may hold values from 1 to 512, 65536 in all
- residual: bfloat16 [512, 4096], P('expert', 'ffn'), may hold values from -16 to 16
- out_weight: bfloat16 [4096, 4096], P(None, 'ffn'), may hold values from -0.1875 to 0.1875
- norm_gain: float32 [4096], P('ffn'), may hold values from 0.25 to 1.75
- router: float32 [4096, 8], P('ffn'), may hold values from -0.09375 to 0.09375
- gate_weight: bfloat16 [8, 4096, 8192], P('expert', None, 'ffn'), may hold values from -0.09375 to 0.09375
- up_weight: bfloat16 [8, 4096, 8192], P('expert', None, 'ffn'), may hold values from -0.09375 to 0.09375
- down_weight: bfloat16 [8, 8192, 4096], P('expert', 'ffn'), may hold values from -0.09375 to 0.09375
- routes: int32 [512, 2], P('expert'), may hold values from 0 to 7, all different within a row; in each aligned block of 64 rows (0 to 63, 64 to 127, ...) at most 32 rows name the same one
Outputs:
- layer_out: bfloat16 [512, 4096], P('expert', 'ffn')
Inputs may be any that keep to these rules, and one draw needn't show every extreme that they name: The lengths of all 512 requests sum to 65536, and some request has exactly 512. `routes`: A request names two different experts. In each aligned block of 64 requests (the requests of one index of expert) no expert is named by more than 32 requests, a bound that some block reaches.
All inputs are finite; a program needn't handle non-finite values. No bound on the sum of `lengths` on one device may be relied on, other than what follows from the above.
Results may differ from a plain program's by a relative error of at most 0.0065.
Values may be sent and summed in bfloat16 or wider, within the bound.
No kernel may reach another device: no remote copies, remote signals or barrier semaphores. Data moves between devices by JAX's collectives and lax.ppermute only.
A program may use at most 128 MiB of HBM per device.

v0:
```python
import math

import jax
import jax.numpy as jnp
from jax import lax
from jax.sharding import PartitionSpec as P

D = 4096
QH = 32
KVH = 8
HD = 128
CACHE = 512


EPSILON = 1e-05
FLOOR = -1e30


def attend_local(queries, new_keys, new_values, key_cache, value_cache, lengths):
    request_count = queries.shape[0]
    group_size = QH // KVH
    score_scale = 1.0 / math.sqrt(HD)
    block_size = math.gcd(CACHE, 256)
    query_heads = queries.reshape(request_count, KVH, group_size, HD)
    key_view = key_cache.reshape(request_count, CACHE, KVH, HD)
    value_view = value_cache.reshape(request_count, CACHE, KVH, HD)
    score_new = (
        jnp.einsum(
            "rkgd,rkd->rkg",
            query_heads,
            new_keys.reshape(request_count, KVH, HD),
            preferred_element_type=jnp.float32,
        )
        * score_scale
    )
    value_start = jnp.broadcast_to(
        new_values.reshape(request_count, KVH, 1, HD).astype(jnp.float32),
        (request_count, KVH, group_size, HD),
    )
    initial = (score_new, jnp.ones_like(score_new), value_start)

    def block_step(block_index, carried):
        running_max, running_den, running_tot = carried
        offset = block_index * block_size
        keys_part = lax.dynamic_slice_in_dim(key_view, offset, block_size, 1)
        values_part = lax.dynamic_slice_in_dim(value_view, offset, block_size, 1)
        scores = (
            jnp.einsum(
                "rkgd,rpkd->rkgp", query_heads, keys_part, preferred_element_type=jnp.float32
            )
            * score_scale
        )
        positions = offset + jnp.arange(block_size, dtype=jnp.int32)
        live_mask = (positions[None, :] < lengths[:, None])[:, None, None, :]
        masked = jnp.where(live_mask, scores, FLOOR)
        new_max = jnp.maximum(running_max, jnp.max(masked, axis=-1))
        weights = jnp.where(live_mask, jnp.exp(masked - new_max[..., None]), 0.0)
        shrink = jnp.exp(running_max - new_max)
        new_den = running_den * shrink + jnp.sum(weights, axis=-1)
        new_tot = running_tot * shrink[..., None] + jnp.einsum(
            "rkgp,rpkd->rkgd",
            weights.astype(jnp.bfloat16),
            values_part,
            preferred_element_type=jnp.float32,
        )
        return (new_max, new_den, new_tot)

    block_total = (jnp.max(lengths) + block_size - 1) // block_size
    final_max, final_den, final_tot = lax.fori_loop(0, block_total, block_step, initial)
    return (final_tot / final_den[..., None]).astype(jnp.bfloat16).reshape(request_count, QH * HD)


def local(
    queries,
    new_keys,
    new_values,
    key_cache,
    value_cache,
    lengths,
    residual,
    out_weight,
    norm_gain,
    router,
    gate_weight,
    up_weight,
    down_weight,
    routes,
):
    attended = attend_local(queries, new_keys, new_values, key_cache, value_cache, lengths)
    hidden = residual.astype(jnp.float32) + jnp.dot(
        lax.all_gather(attended, "ffn", axis=0, tiled=True),
        out_weight,
        preferred_element_type=jnp.float32,
    )
    scaled = hidden * norm_gain
    square_part = jnp.sum(hidden * hidden, axis=-1)
    square_sum = lax.psum(square_part, "ffn")
    inverse = lax.rsqrt(square_sum / D + EPSILON)[:, None]
    logits = lax.psum(jnp.dot(scaled * inverse, router, precision=lax.Precision.HIGHEST), "ffn")
    normed = (scaled * inverse).astype(jnp.bfloat16)
    expert_count = lax.axis_size("expert")
    row_count = routes.shape[0]
    capacity = row_count // 2
    expert_ids = jnp.arange(expert_count, dtype=jnp.int32)
    chosen = routes[:, :, None] == expert_ids[None, None, :]
    picked = jnp.sum(jnp.where(chosen, logits[:, None, :], 0.0), axis=-1)
    first_weight = jax.nn.sigmoid(picked[:, 0] - picked[:, 1])
    route_weights = jnp.stack([first_weight, 1.0 - first_weight], axis=1)
    flat_hits = chosen.astype(jnp.int32).reshape(row_count * 2, expert_count)
    earlier = jnp.cumsum(flat_hits, axis=0) - flat_hits
    slots = jnp.sum(earlier * flat_hits, axis=-1).reshape(row_count, 2)
    targets = routes * capacity + slots
    slot_ids = jnp.arange(expert_count * capacity, dtype=jnp.int32)
    slot_hits = slot_ids[:, None, None] == targets[None, :, :]
    dispatch = jnp.sum(slot_hits.astype(jnp.float32), axis=-1).astype(jnp.bfloat16)
    combine = jnp.sum(jnp.where(slot_hits, route_weights[None, :, :], 0.0), axis=-1).T
    gate_local = gate_weight[0]
    up_local = up_weight[0]
    down_local = down_weight[0]
    share_rows = (
        jnp.dot(dispatch, normed, preferred_element_type=jnp.float32)
        .astype(jnp.bfloat16)
        .reshape(expert_count, capacity, normed.shape[1])
    )
    part_rows = lax.all_gather(
        lax.all_to_all(share_rows, "expert", split_axis=0, concat_axis=0, tiled=True),
        "ffn",
        axis=2,
        tiled=True,
    )
    gate_next = jnp.einsum("eck,kf->ecf", part_rows, gate_local, preferred_element_type=jnp.float32)
    up_next = jnp.einsum("eck,kf->ecf", part_rows, up_local, preferred_element_type=jnp.float32)
    inner = (jax.nn.silu(gate_next) * up_next).astype(jnp.bfloat16)
    partial_out = jnp.einsum("ecf,fd->ecd", inner, down_local, preferred_element_type=jnp.float32)
    summed = lax.psum_scatter(
        partial_out.astype(jnp.bfloat16), "ffn", scatter_dimension=2, tiled=True
    )
    returned = lax.all_to_all(summed, "expert", split_axis=0, concat_axis=0, tiled=True)
    mixed = jnp.dot(
        combine,
        returned.reshape(expert_count * capacity, -1).astype(jnp.float32),
        precision=lax.Precision.HIGHEST,
    )
    return (hidden + mixed).astype(jnp.bfloat16)


def solution(mesh):
    placed = (
        P(("expert", "ffn"), None),
        P(("expert", "ffn"), None),
        P(("expert", "ffn"), None),
        P(("expert", "ffn"), None, None),
        P(("expert", "ffn"), None, None),
        P(("expert", "ffn")),
        P("expert", "ffn"),
        P(None, "ffn"),
        P("ffn"),
        P("ffn", None),
        P("expert", None, "ffn"),
        P("expert", None, "ffn"),
        P("expert", "ffn", None),
        P("expert", None),
    )
    return jax.shard_map(
        local, mesh=mesh, in_specs=placed, out_specs=P("expert", "ffn"), check_vma=False
    )
```

profile of v0, /device:TPU:1, one launch (start us, length us, event | category | flops | bytes accessed | tf_op | source)
XLA Modules:
  0.0 292.2 jit_solution(4091025188030923789)
XLA Ops:
  6.5 1.4 reduce_max.18
  8.6 0.8 reshape.73
  9.5 0.7 reshape.91
  10.3 6.2 %copy.47 = bf16[4,512,1024]{1,2,0:T(8,128)(2,1)} copy(bf16[4,512,1024]{2,1,0:T(8,128)(2,1)} %param.19) | data formatting | bytes 8388608 | tf_op args[3]
  16.5 6.2 %copy.48 = bf16[4,512,1024]{1,2,0:T(8,128)(2,1)} copy(bf16[4,512,1024]{2,1,0:T(8,128)(2,1)} %param.20) | data formatting | bytes 8388608 | tf_op args[4]
  22.9 9.4 %while.14 = (s32[]{:T(128)}, f32[4,8,4]{2,1,0:T(8,128)S(1)}, f32[4,8,4]{2,1,0:T(8,128)S(1)}, f32[4,8,4,128]{3,2,1,0:T(4,128)S(1)}, s32[]{:T(128)}, /*index=5*/s3...) while((s32[]{:T(128)}, f32[4,8,4]{2,1,0:T(8,128)S(1)}, ...), condition=%wide.region_4.5_spmd, body=%wide.region_1.4_spmd.sunk | while | flops 17106436 | bytes 4765895 | solution.py:69
  23.0 2.1 fusion.77
  25.0 0.2 fusion.78
  25.3 2.3 fusion.79
  27.7 2.1 fusion.77
  30.0 2.3 fusion.79
  32.5 19.0 %all-gather = bf16[16,4,4096]{2,1,0:T(4,128)(2,1)S(1)} all-gather(bf16[1,4,4096]{2,1,0:T(4,128)(2,1)S(1)} %reshape.82), channel_id=1, replica_groups=mesh['expert'=8,'ffn'=16] {'ffn'}, dimensions={0}, use_global_device_ids=true | all-gather | bytes 557056 | tf_op jit(solution)/shard_map/all_gather | solution.py:91
  51.6 0.6 multiply_reduce_fusion
  52.2 31.1 %psum.14 = f32[64]{0:T(128)S(1)} all-reduce(f32[64]{0:T(128)S(1)} %get-tuple-element.118), channel_id=1, replica_groups=mesh['expert'=8,'ffn'=16] {'ffn'}, use_global_device_ids=true, to_apply=%region_8.9 | all-reduce | flops 64 | bytes 512 | tf_op jit(solution)/shard_map/psum | solution.py:97
  83.3 0.2 fusion.47
  83.5 28.8 %psum.15 = f32[64,8]{0,1:T(8,128)S(1)} all-reduce(f32[64,8]{0,1:T(8,128)S(1)} %fusion.47), channel_id=1, replica_groups=mesh['expert'=8,'ffn'=16] {'ffn'}, use_global_device_ids=true, to_apply=%region_9.10 | all-reduce | flops 512 | bytes 4096 | tf_op jit(solution)/shard_map/psum | solution.py:99
  113.4 0.2 convolution_convert_fusion.1
  113.6 30.9 %all_to_all.10 = bf16[8,32,256]{2,1,0:T(8,128)(2,1)} all-to-all(bf16[8,32,256]{2,1,0:T(8,128)(2,1)S(1)} %bitcast.46), channel_id=1, replica_groups=mesh['expert'=8,'ffn'=16] {'expert'}, dimensions={0} | all-to-all | bytes 262144 | tf_op jit(solution)/shard_map/all_to_all | solution.py:126
  144.6 41.4 %all-gather.3.cloned.1.call-done = bf16[8,32,4096]{2,1,0:T(8,128)(2,1)} async-done(((bf16[8,32,256]{2,1,0:T(8,128)(2,1)}), bf16[8,32,4096]{2,1,0:T(8,128)(2,1)}) %all-gather.3.cloned.1.call-update) | async-done | bytes 2097168 | tf_op jit(solution)/shard_map/all_gather | solution.py:125
  186.0 4.1 %fusion.28 = f32[8,32,512]{2,1,0:T(8,128)S(1)} fusion(bf16[8,32,4096]{2,1,0:T(8,128)(2,1)} %all-gather.3.cloned.1.call-done, bf16[1,4096,512]{2,1,0:T(8,128)(2,1)} %param.26), kind=kOutput, calls=%fused_computation.25 | convolution fusion | flops 1073741824 | bytes 6815744 | tf_op jit(solution)/shard_map/eck,kf->ecf/dot_general | solution.py:131
  190.1 7.8 %convolution_convert_fusion = bf16[8,32,4096]{2,1,0:T(8,128)(2,1)} fusion(bf16[1,512,4096]{2,1,0:T(8,128)(2,1)} %param.28, bf16[8,32,4096]{2,1,0:T(8,128)(2,1)} %all-gather.3.cloned.1.call-done, bf16[1,4096,512]{2,1,0:T(8,128)(2,1)} %param.27, f32[8,32,512]{2,1,0:T(8,128)S(1)} %fusion.28), kind=kOutput, calls=%fused_computation.21 | convolution fusion | flops 2149318656 | bytes 13107200 | tf_op jit(solution)/shard_map/ecf,fd->ecd/dot_general | solution.py:134
  197.9 74.6 %reduce-scatter.2.cloned.1.call-done = bf16[8,32,256]{2,1,0:T(8,128)(2,1)} async-done(((bf16[8,32,4096]{2,1,0:T(8,128)(2,1)}), bf16[8,32,256]{2,1,0:T(8,128)(2,1)}) %reduce-scatter.2.cloned.1.call-update) | async-done | bytes 131088 | tf_op jit(solution)/shard_map/reduce_scatter | solution.py:135
  272.6 12.0 %all_to_all.11 = bf16[8,32,256]{2,1,0:T(8,128)(2,1)S(1)} all-to-all(bf16[8,32,256]{2,1,0:T(8,128)(2,1)} %reduce-scatter.2.cloned.1.call-done), channel_id=1, replica_groups=mesh['expert'=8,'ffn'=16] {'expert'}, dimensions={0} | all-to-all | bytes 262144 | tf_op jit(solution)/shard_map/all_to_all | solution.py:138
  284.5 0.8 fusion.36
  (51 shorter events, 2.0 us)
Async XLA Ops:
  6.5 45.1 %copy-start = (bf16[4096,256]{1,0:T(8,128)(2,1)S(1)}, bf16[4096,256]{1,0:T(8,128)(2,1)}, u32[]{:S(2)}) copy-start(bf16[4096,256]{1,0:T(8,128)(2,1)} %param.23) | copy-start | bytes 6291460
  6.5 179.5 %all-gather.3.cloned.1.call-start = ((), (), s32[]{:S(2)}) async-start(), calls=%async_computation.3 | async-start | bytes 2228224 | tf_op jit(solution)/shard_map/all_gather | solution.py:125
  16.5 6.2 %copy-start.4 = (bf16[4,1024]{1,0:T(4,128)(2,1)S(1)}, bf16[4,1024]{1,0:T(4,128)(2,1)}, u32[]{:S(2)}) copy-start(bf16[4,1024]{1,0:T(4,128)(2,1)} %param.18) | copy-start | bytes 24580
  16.5 6.3 %copy-start.2 = (s32[4]{0:T(128)S(1)}, s32[4]{0:T(128)}, u32[]{:S(2)}) copy-start(s32[4]{0:T(128)} %param.21) | copy-start | bytes 52
  22.8 28.8 %copy-start.1 = (bf16[64,256]{1,0:T(8,128)(2,1)S(1)}, bf16[64,256]{1,0:T(8,128)(2,1)}, u32[]{:S(2)}) copy-start(bf16[64,256]{1,0:T(8,128)(2,1)} %param.22) | copy-start | bytes 98308
  32.3 51.0 %copy-start.5 = (f32[256,8]{0,1:T(8,128)S(1)}, f32[256,8]{0,1:T(8,128)}, u32[]{:S(2)}) copy-start(f32[256,8]{0,1:T(8,128)} %param.25) | copy-start | bytes 24580
  32.3 51.0 %copy-start.6 = (f32[256]{0:T(256)S(1)}, f32[256]{0:T(256)}, u32[]{:S(2)}) copy-start(f32[256]{0:T(256)} %param.24) | copy-start | bytes 3076
  32.3 80.0 %copy-start.3 = (s32[64,2]{0,1:T(2,128)S(1)}, s32[64,2]{0,1:T(2,128)}, u32[]{:S(2)}) copy-start(s32[64,2]{0,1:T(2,128)} %param.29) | copy-start | bytes 1540
  144.6 128.0 %reduce-scatter.2.cloned.1.call-start = ((), (), s32[]{:S(2)}) async-start(), calls=%async_computation.4 | async-start | bytes 2228224 | tf_op jit(solution)/shard_map/reduce_scatter | solution.py:135
Sparse Core Ops, SparseCore 0:
  144.7 41.3 all-gather.2
  198.1 74.4 reduce-scatter.1
where the time goes:
time: 293 us; the launch traced here: 292 us
  blocking collectives  122 us (42%)
  waiting for transfers between devices  116 us (40%)
  matrix products  22.6 us (8%)
  local copies, waits for them, and re-layouts  14.6 us (5%)
  between operations  14.3 us (5%)
    reduce_scatter x1, waiting for transfers between devices, local(): lax.psum_scatter(partial_out.astype(jnp.bfloat16), 'ffn', scatter_dimensi...  74.6 us
    all_gather x1, waiting for transfers between devices, local(): lax.all_gather(lax.all_to_all(share_rows, 'expert', split_axis=0, concat_...  41.4 us
    psum x1, blocking collectives, local(): square_sum = lax.psum(square_part, 'ffn')  31.1 us
    all_to_all x1, blocking collectives, local(): lax.all_to_all(share_rows, 'expert', split_axis=0, concat_axis=0, tiled=T...  30.9 us
    psum x1, blocking collectives, local(): lax.psum(jnp.dot(scaled * inverse, router, precision=lax.Precision.HIGHES...  28.8 us
    all_gather x1, blocking collectives, local(): lax.all_gather(attended, 'ffn', axis=0, tiled=True)  19 us
    unnamed x20, local copies, waits for them, and re-layouts  12.7 us
    all_to_all x1, blocking collectives, local(): lax.all_to_all(summed, 'expert', split_axis=0, concat_axis=0, tiled=True)  12 us
  transfers between devices with their start and end apart: 2, of which 2 were waited for; matrix products, arithmetic and copies ran while one was open for 0% of the time, Pallas kernels for 0%

commit v1 on v0

--- a/solution.py
+++ b/solution.py
@@ -93,10 +93,11 @@
         preferred_element_type=jnp.float32,
     )
     scaled = hidden * norm_gain
-    square_part = jnp.sum(hidden * hidden, axis=-1)
-    square_sum = lax.psum(square_part, "ffn")
-    inverse = lax.rsqrt(square_sum / D + EPSILON)[:, None]
-    logits = lax.psum(jnp.dot(scaled * inverse, router, precision=lax.Precision.HIGHEST), "ffn")
+    square_part = jnp.sum(hidden * hidden, axis=-1, keepdims=True)
+    logit_part = jnp.dot(scaled, router, precision=lax.Precision.HIGHEST)
+    stats = lax.psum(jnp.concatenate([square_part, logit_part], axis=1), "ffn")
+    inverse = lax.rsqrt(stats[:, :1] / D + EPSILON)
+    logits = stats[:, 1:] * inverse
     normed = (scaled * inverse).astype(jnp.bfloat16)
     expert_count = lax.axis_size("expert")
     row_count = routes.shape[0]
@@ -122,19 +123,20 @@
         .astype(jnp.bfloat16)
         .reshape(expert_count, capacity, normed.shape[1])
     )
+    feature_blocks = lax.axis_size("ffn")
+    received = lax.all_to_all(share_rows, "expert", split_axis=0, concat_axis=0, tiled=True)
     part_rows = lax.all_gather(
-        lax.all_to_all(share_rows, "expert", split_axis=0, concat_axis=0, tiled=True),
-        "ffn",
-        axis=2,
-        tiled=True,
+        received.reshape(expert_count * capacity, normed.shape[1]), "ffn", axis=0, tiled=False
     )
-    gate_next = jnp.einsum("eck,kf->ecf", part_rows, gate_local, preferred_element_type=jnp.float32)
-    up_next = jnp.einsum("eck,kf->ecf", part_rows, up_local, preferred_element_type=jnp.float32)
+    part_rows = part_rows.transpose(1, 0, 2).reshape(expert_count * capacity, -1)
+    gate_next = jnp.dot(part_rows, gate_local, preferred_element_type=jnp.float32)
+    up_next = jnp.dot(part_rows, up_local, preferred_element_type=jnp.float32)
     inner = (jax.nn.silu(gate_next) * up_next).astype(jnp.bfloat16)
-    partial_out = jnp.einsum("ecf,fd->ecd", inner, down_local, preferred_element_type=jnp.float32)
+    partial_out = jnp.dot(inner, down_local, preferred_element_type=jnp.float32)
+    partial_out = partial_out.reshape(-1, feature_blocks, normed.shape[1]).transpose(1, 0, 2)
     summed = lax.psum_scatter(
-        partial_out.astype(jnp.bfloat16), "ffn", scatter_dimension=2, tiled=True
-    )
+        partial_out.astype(jnp.bfloat16), "ffn", scatter_dimension=0, tiled=True
+    ).reshape(expert_count, capacity, normed.shape[1])
     returned = lax.all_to_all(summed, "expert", split_axis=0, concat_axis=0, tiled=True)
     mixed = jnp.dot(
         combine,

time: 293 us -> 261 us (0.89)
  blocking collectives: 122 us -> 91.5 us
  local copies, waits for them, and re-layouts: 14.6 us -> 25.6 us
  waiting for transfers between devices: 116 us -> 106 us
  matrix products: 22.6 us -> 18.2 us
    reduce_scatter x1 -> x0, waiting for transfers between devices: 74.6 us -> none  [local(): lax.psum_scatter(partial_out.astype(jnp.bfloat16), 'ffn', scatter_dimensi...]
    unnamed x2 -> x3, waiting for transfers between devices: 0.03 us -> 74.6 us
    psum x2 -> x1, blocking collectives: 59.8 us -> 31.4 us  [local(): stats = lax.psum(jnp.concatenate([square_part, logit_part], axis=1), 'ffn')]
    all_gather x1, waiting for transfers between devices: 41.4 us -> 31.4 us  [local(): lax.all_gather(received.reshape(expert_count * capacity, normed.shape[1])...]
    all_to_all x1, blocking collectives: 30.9 us -> 23.5 us  [local(): lax.all_to_all(share_rows, 'expert', split_axis=0, concat_axis=0, tiled=T...]
    dot_general x0 -> x1, local copies, waits for them, and re-layouts: none -> 6.49 us  [local(): partial_out = jnp.dot(inner, down_local, preferred_element_type=jnp.float32)]
    all_gather x1, blocking collectives: 19 us -> 24.7 us  [local(): lax.all_gather(attended, 'ffn', axis=0, tiled=True)]
    all_gather x0 -> x1, local copies, waits for them, and re-layouts: none -> 3.92 us  [local(): lax.all_gather(received.reshape(expert_count * capacity, normed.shape[1])...]
  transfers between devices with their start and end apart: 2 -> 2, of which waited for: 2 -> 2; matrix products, arithmetic and copies ran while one was open for 0% -> 3% of each run, Pallas kernels for 0% -> 0%
where the time goes in v1:
time: 261 us; the launch traced here: 260 us
  waiting for transfers between devices  106 us (41%)
  blocking collectives  91.5 us (35%)
  local copies, waits for them, and re-layouts  25.6 us (10%)
  matrix products  18.2 us (7%)
  between operations  14.3 us (5%)
  other arithmetic  3.95 us (2%)
    unnamed x3, waiting for transfers between devices  74.6 us
    all_gather x1, waiting for transfers between devices, local(): lax.all_gather(received.reshape(expert_count * capacity, normed.shape[1])...  31.4 us
    psum x1, blocking collectives, local(): stats = lax.psum(jnp.concatenate([square_part, logit_part], axis=1), 'ffn')  31.4 us
    all_gather x1, blocking collectives, local(): lax.all_gather(attended, 'ffn', axis=0, tiled=True)  24.7 us
    all_to_all x1, blocking collectives, local(): lax.all_to_all(share_rows, 'expert', split_axis=0, concat_axis=0, tiled=T...  23.5 us
    unnamed x18, local copies, waits for them, and re-layouts  13.4 us
    all_to_all x1, blocking collectives, local(): lax.all_to_all(summed, 'expert', split_axis=0, concat_axis=0, tiled=True)  12 us
    dot_general x1, matrix products, local(): partial_out = jnp.dot(inner, down_local, preferred_element_type=jnp.float32)  7.86 us
  transfers between devices with their start and end apart: 2, of which 2 were waited for; matrix products, arithmetic and copies ran while one was open for 3% of the time, Pallas kernels for 0%

profile of v1, /device:TPU:1, one launch (start us, length us, event | category | flops | bytes accessed | tf_op | source)
XLA Modules:
  0.0 259.7 jit_solution(12332257299404146861)
XLA Ops:
  6.5 1.5 reduce_max.18
  8.8 0.7 reshape.98
  9.5 0.7 convert_bitcast_fusion.1
  10.2 0.8 reshape.80
  11.2 0.8 copy.69
  12.7 0.7 multiply_add_fusion.1
  13.4 6.2 %copy.65 = bf16[4,512,1024]{1,2,0:T(8,128)(2,1)} copy(bf16[4,512,1024]{2,1,0:T(8,128)(2,1)} %param.19) | data formatting | bytes 8388608 | tf_op args[3]
  19.6 6.2 %copy.66 = bf16[4,512,1024]{1,2,0:T(8,128)(2,1)} copy(bf16[4,512,1024]{2,1,0:T(8,128)(2,1)} %param.20) | data formatting | bytes 8388608 | tf_op args[4]
  25.9 4.7 %while.14 = (s32[]{:T(128)}, f32[4,8,4]{2,1,0:T(8,128)S(1)}, f32[4,8,4]{2,1,0:T(8,128)S(1)}, f32[4,8,4,128]{3,2,1,0:T(4,128)S(1)}, s32[]{:T(128)}, /*index=5*/s3...) while((s32[]{:T(128)}, f32[4,8,4]{2,1,0:T(8,128)S(1)}, ...), condition=%wide.region_4.5_spmd, body=%wide.region_1.4_spmd.sunk | while | flops 17106436 | bytes 4765895 | solution.py:69
  26.0 2.1 fusion.81
  28.3 2.3 fusion.83
  30.8 24.7 %all-gather = bf16[16,4,4096]{2,1,0:T(4,128)(2,1)S(1)} all-gather(bf16[1,4,4096]{2,1,0:T(4,128)(2,1)S(1)} %reshape.91), channel_id=1, replica_groups=mesh['expert'=8,'ffn'=16] {'ffn'}, dimensions={0}, use_global_device_ids=true | all-gather | bytes 557056 | tf_op jit(solution)/shard_map/all_gather | solution.py:91
  55.6 0.6 multiply_reduce_fusion
  56.4 31.4 %psum.7 = f32[64,9]{0,1:T(8,128)S(1)} all-reduce(f32[64,9]{0,1:T(8,128)S(1)} %pad_maximum_fusion), channel_id=1, replica_groups=mesh['expert'=8,'ffn'=16] {'ffn'}, use_global_device_ids=true, to_apply=%region_8.9 | all-reduce | flops 576 | bytes 4608 | tf_op jit(solution)/shard_map/psum | solution.py:98
  88.0 0.2 convolution_convert_fusion
  88.2 23.5 %all_to_all.10 = bf16[8,32,256]{2,1,0:T(8,128)(2,1)} all-to-all(bf16[8,32,256]{2,1,0:T(8,128)(2,1)S(1)} %bitcast.66), channel_id=1, replica_groups=mesh['expert'=8,'ffn'=16] {'expert'}, dimensions={0} | all-to-all | bytes 262144 | tf_op jit(solution)/shard_map/all_to_all | solution.py:127
  111.8 6.5 %copy.75 = bf16[4096,512]{1,0:T(8,128)(2,1)} copy(bf16[4096,512]{0,1:T(8,128)(2,1)} %bitcast.62) | data formatting | bytes 8388608 | tf_op jit(solution)/shard_map/dot_general | solution.py:135
  118.3 31.4 %all-gather.3.cloned.1.call-done = bf16[16,256,256]{2,1,0:T(8,128)(2,1)} async-done(((bf16[1,256,256]{2,1,0:T(8,128)(2,1)}), bf16[16,256,256]{2,1,0:T(8,128)(2,1)}) %all-gather.3.cloned.1.call-update) | async-done | bytes 2097168 | tf_op jit(solution)/shard_map/all_gather | solution.py:128
  149.7 3.9 %copy.71 = bf16[16,256,256]{1,2,0:T(8,128)(2,1)} copy(bf16[16,256,256]{2,1,0:T(8,128)(2,1)} %all-gather.3.cloned.1.call-done) | data formatting | bytes 4194304 | tf_op jit(solution)/shard_map/all_gather | solution.py:128
  153.6 4.1 %fusion.27 = f32[256,512]{1,0:T(8,128)S(1)} fusion(bf16[256,4096]{0,1:T(8,128)(2,1)} %bitcast.64, bf16[1,4096,512]{2,1,0:T(8,128)(2,1)} %param.26), kind=kOutput, calls=%fused_computation.23 | convolution fusion | flops 1073741824 | bytes 6815744 | tf_op jit(solution)/shard_map/dot_general | solution.py:132
  157.7 7.9 %convert_bitcast_fusion = bf16[16,256,256]{2,1,0:T(8,128)(2,1)} fusion(bf16[16,256,512]{2,1,0:T(8,128)(2,1)} %bitcast.63, bf16[256,4096]{0,1:T(8,128)(2,1)} %bitcast.65, bf16[1,4096,512]{2,1,0:T(8,128)(2,1)} %param.27, f32[256,512]{1,0:T(8,128)S(1)} %fusion.27), kind=kOutput, calls=%fused_computation.25 | convolution fusion | flops 2149318656 | bytes 13107200 | tf_op jit(solution)/shard_map/dot_general | solution.py:135
  165.6 74.5 %reduce-scatter.4.cloned.1.call-done = bf16[1,256,256]{2,1,0:T(8,128)(2,1)} async-done(((bf16[16,256,256]{2,1,0:T(8,128)(2,1)}), bf16[1,256,256]{2,1,0:T(8,128)(2,1)}) %reduce-scatter.4.cloned.1.call-update) | async-done | bytes 131088
  240.1 12.0 %all_to_all.11 = bf16[8,32,256]{2,1,0:T(8,128)(2,1)S(1)} all-to-all(bf16[8,32,256]{2,1,0:T(8,128)(2,1)} %bitcast.69), channel_id=1, replica_groups=mesh['expert'=8,'ffn'=16] {'expert'}, dimensions={0} | all-to-all | bytes 262144 | tf_op jit(solution)/shard_map/all_to_all | solution.py:140
  252.1 0.8 fusion.38
  (44 shorter events, 1.9 us)
Async XLA Ops:
  6.5 49.0 %copy-start = (bf16[4096,256]{1,0:T(8,128)(2,1)S(1)}, bf16[4096,256]{1,0:T(8,128)(2,1)}, u32[]{:S(2)}) copy-start(bf16[4096,256]{1,0:T(8,128)(2,1)} %param.23) | copy-start | bytes 6291460
  6.5 143.1 %all-gather.3.cloned.1.call-start = ((), (), s32[]{:S(2)}) async-start(), calls=%async_computation.3 | async-start | bytes 2228224 | tf_op jit(solution)/shard_map/all_gather | solution.py:128
  19.6 6.2 %copy-start.2 = (s32[4]{0:T(128)S(1)}, s32[4]{0:T(128)}, u32[]{:S(2)}) copy-start(s32[4]{0:T(128)} %param.21) | copy-start | bytes 52
  25.9 29.7 %copy-start.1 = (bf16[64,256]{1,0:T(8,128)(2,1)S(1)}, bf16[64,256]{1,0:T(8,128)(2,1)}, u32[]{:S(2)}) copy-start(bf16[64,256]{1,0:T(8,128)(2,1)} %param.22) | copy-start | bytes 98308
  30.6 25.5 %copy-start.4 = (f32[256,8]{0,1:T(8,128)S(1)}, f32[256,8]{0,1:T(8,128)}, u32[]{:S(2)}) copy-start(f32[256,8]{0,1:T(8,128)} %param.25) | copy-start | bytes 24580
  30.6 25.5 %copy-start.5 = (f32[256]{0:T(256)S(1)}, f32[256]{0:T(256)}, u32[]{:S(2)}) copy-start(f32[256]{0:T(256)} %param.24) | copy-start | bytes 3076
  30.6 57.1 %copy-start.3 = (s32[64,2]{0,1:T(2,128)S(1)}, s32[64,2]{0,1:T(2,128)}, u32[]{:S(2)}) copy-start(s32[64,2]{0,1:T(2,128)} %param.29) | copy-start | bytes 1540
  111.7 128.4 %reduce-scatter.4.cloned.1.call-start = ((), (), s32[]{:S(2)}) async-start(), calls=%async_computation.4 | async-start | bytes 2228224
Sparse Core Ops, SparseCore 0:
  111.8 37.7 all-gather.2
  165.7 74.3 reduce-scatter.3

commit v2 on v1

--- a/solution.py
+++ b/solution.py
@@ -14,6 +14,22 @@
 
 EPSILON = 1e-05
 FLOOR = -1e30
+
+
+def butterfly_sum(value, axis_name):
+    size = lax.axis_size(axis_name)
+    step = 1
+    while step < size:
+        pairs = [(j, j ^ step) for j in range(size)]
+        value = value + lax.ppermute(value, axis_name, pairs)
+        step *= 2
+    return value
+
+
+def gather_by_exchange(value, axis_name):
+    size = lax.axis_size(axis_name)
+    copies = jnp.broadcast_to(value[None], (size,) + value.shape)
+    return lax.all_to_all(copies, axis_name, 0, 0, tiled=True)
 
 
 def attend_local(queries, new_keys, new_values, key_cache, value_cache, lengths):
@@ -87,15 +103,16 @@
     routes,
 ):
     attended = attend_local(queries, new_keys, new_values, key_cache, value_cache, lengths)
+    gathered = gather_by_exchange(attended, "ffn").reshape(-1, attended.shape[1])
     hidden = residual.astype(jnp.float32) + jnp.dot(
-        lax.all_gather(attended, "ffn", axis=0, tiled=True),
+        gathered,
         out_weight,
         preferred_element_type=jnp.float32,
     )
     scaled = hidden * norm_gain
     square_part = jnp.sum(hidden * hidden, axis=-1, keepdims=True)
     logit_part = jnp.dot(scaled, router, precision=lax.Precision.HIGHEST)
-    stats = lax.psum(jnp.concatenate([square_part, logit_part], axis=1), "ffn")
+    stats = butterfly_sum(jnp.concatenate([square_part, logit_part], axis=1), "ffn")
     inverse = lax.rsqrt(stats[:, :1] / D + EPSILON)
     logits = stats[:, 1:] * inverse
     normed = (scaled * inverse).astype(jnp.bfloat16)
@@ -125,8 +142,8 @@
     )
     feature_blocks = lax.axis_size("ffn")
     received = lax.all_to_all(share_rows, "expert", split_axis=0, concat_axis=0, tiled=True)
-    part_rows = lax.all_gather(
-        received.reshape(expert_count * capacity, normed.shape[1]), "ffn", axis=0, tiled=False
+    part_rows = gather_by_exchange(
+        received.reshape(expert_count * capacity, normed.shape[1]), "ffn"
     )
     part_rows = part_rows.transpose(1, 0, 2).reshape(expert_count * capacity, -1)
     gate_next = jnp.dot(part_rows, gate_local, preferred_element_type=jnp.float32)
@@ -134,9 +151,12 @@
     inner = (jax.nn.silu(gate_next) * up_next).astype(jnp.bfloat16)
     partial_out = jnp.dot(inner, down_local, preferred_element_type=jnp.float32)
     partial_out = partial_out.reshape(-1, feature_blocks, normed.shape[1]).transpose(1, 0, 2)
-    summed = lax.psum_scatter(
-        partial_out.astype(jnp.bfloat16), "ffn", scatter_dimension=0, tiled=True
-    ).reshape(expert_count, capacity, normed.shape[1])
+    pieces = lax.all_to_all(partial_out.astype(jnp.bfloat16), "ffn", 0, 0, tiled=True)
+    summed = (
+        jnp.sum(pieces.astype(jnp.float32), axis=0)
+        .astype(jnp.bfloat16)
+        .reshape(expert_count, capacity, normed.shape[1])
+    )
     returned = lax.all_to_all(summed, "expert", split_axis=0, concat_axis=0, tiled=True)
     mixed = jnp.dot(
         combine,

time: 261 us -> 168 us (0.64)
  waiting for transfers between devices: 106 us -> 31.3 us
  between operations: 14.3 us -> 0.94 us
  blocking collectives: 91.5 us -> 81 us
  starting transfers between devices: 0.04 us -> 7.47 us
  local copies, waits for them, and re-layouts: 25.6 us -> 22.9 us
    unnamed x3 -> x0, waiting for transfers between devices: 74.6 us -> none
    all_to_all x0 -> x2, blocking collectives: none -> 51.4 us  [the longest x1 29.1 us: local(): lax.all_to_all(partial_out.astype(jnp.bfloat16), 'ffn', 0, 0, tiled=True)]
    all_gather x1 -> x0, waiting for transfers between devices: 31.4 us -> none  [local(): lax.all_gather(received.reshape(expert_count * capacity, normed.shape[1])...]
    psum x1 -> x0, blocking collectives: 31.4 us -> none  [local(): stats = lax.psum(jnp.concatenate([square_part, logit_part], axis=1), 'ffn')]
    all_gather x1 -> x0, blocking collectives: 24.7 us -> none  [local(): lax.all_gather(attended, 'ffn', axis=0, tiled=True)]
    all_to_all x0 -> x1, waiting for transfers between devices: none -> 22.1 us  [gather_by_exchange(): return lax.all_to_all(copies, axis_name, 0, 0, tiled=True)]
    ppermute x0 -> x4, waiting for transfers between devices: none -> 9.15 us  [butterfly_sum(): value = value + lax.ppermute(value, axis_name, pairs)]
    all_to_all x1, blocking collectives: 23.5 us -> 16.9 us  [local(): lax.all_to_all(share_rows, 'expert', split_axis=0, concat_axis=0, tiled=T...]
  transfers between devices with their start and end apart: 2 -> 5, of which waited for: 2 -> 5; matrix products, arithmetic and copies ran while one was open for 3% -> 4% of each run, Pallas kernels for 0% -> 0%
where the time goes in v2:
time: 168 us; the launch traced here: 167 us
  blocking collectives  81 us (48%)
  waiting for transfers between devices  31.3 us (19%)
  local copies, waits for them, and re-layouts  22.9 us (14%)
  matrix products  18.2 us (11%)
  starting transfers between devices  7.47 us (4%)
  other arithmetic  5.16 us (3%)
    all_to_all x1, blocking collectives, local(): lax.all_to_all(partial_out.astype(jnp.bfloat16), 'ffn', 0, 0, tiled=True)  29.1 us
    all_to_all x1, blocking collectives, gather_by_exchange(): return lax.all_to_all(copies, axis_name, 0, 0, tiled=True)  22.3 us
    all_to_all x1, waiting for transfers between devices, gather_by_exchange(): return lax.all_to_all(copies, axis_name, 0, 0, tiled=True)  22.1 us
    all_to_all x1, blocking collectives, local(): lax.all_to_all(share_rows, 'expert', split_axis=0, concat_axis=0, tiled=T...  16.9 us
    all_to_all x1, blocking collectives, local(): lax.all_to_all(summed, 'expert', split_axis=0, concat_axis=0, tiled=True)  12.7 us
    unnamed x16, local copies, waits for them, and re-layouts  12.6 us
    ppermute x4, waiting for transfers between devices, butterfly_sum(): value = value + lax.ppermute(value, axis_name, pairs)  9.15 us
    dot_general x1, matrix products, local(): partial_out = jnp.dot(inner, down_local, preferred_element_type=jnp.float32)  7.88 us
  transfers between devices with their start and end apart: 5, of which 5 were waited for; matrix products, arithmetic and copies ran while one was open for 4% of the time, Pallas kernels for 0%

profile of v2, /device:TPU:1, one launch (start us, length us, event | category | flops | bytes accessed | tf_op | source)
XLA Modules:
  0.0 167.0 jit_solution(17823797884747397665)
XLA Ops:
  0.0 1.5 reduce_max.18
  4.6 6.2 %copy.54 = bf16[4,512,1024]{1,2,0:T(8,128)(2,1)} copy(bf16[4,512,1024]{2,1,0:T(8,128)(2,1)} %param.19) | data formatting | bytes 8388608 | tf_op args[3]
  10.8 6.2 %copy.55 = bf16[4,512,1024]{1,2,0:T(8,128)(2,1)} copy(bf16[4,512,1024]{2,1,0:T(8,128)(2,1)} %param.20) | data formatting | bytes 8388608 | tf_op args[4]
  17.1 4.7 %while.14 = (s32[]{:T(128)}, f32[4,8,4]{2,1,0:T(8,128)S(1)}, f32[4,8,4]{2,1,0:T(8,128)S(1)}, f32[4,8,4,128]{3,2,1,0:T(4,128)S(1)}, s32[]{:T(128)}, /*index=5*/s3...) while((s32[]{:T(128)}, f32[4,8,4]{2,1,0:T(8,128)S(1)}, ...), condition=%wide.region_4.5_spmd, body=%wide.region_1.4_spmd.sunk | while | flops 17106436 | bytes 4765895 | solution.py:85
  17.2 2.1 %fusion.82 = (f32[4,8,4]{2,1,0:T(8,128)S(1)}, f32[4,8,4,256]{3,2,1,0:T(4,128)S(1)}) fusion(bf16[4,8,4,128]{3,2,1,0:T(4,128)(2,1)S(1)} %get-tuple-element.217, bf16[4,512,8,128]{1,3,2,0:T(8,128)(2,1)} %get-tuple-element.216, s32[]{:T(128)S(6)} %select_n.46, pred[4,256]{1,0:T(4,128)(4,1)S(1)} %broadcast_compare_fusion.2), kind=kOutput, calls=%fused_computation.71.clone.1 | convolution fusion | flops 8486784 | bytes 2262532 | tf_op jit(solution)/shard_map/while/body/rkgd,rpkd->rkgp/dot_general | solution.py:64
  19.5 2.3 %fusion.84 = f32[4,8,4,128]{3,2,1,0:T(4,128)S(1)} fusion(bf16[4,512,8,128]{1,3,2,0:T(8,128)(2,1)} %get-tuple-element.218, s32[]{:T(128)S(6)} %select_n.46, f32[4,8,4,256]{3,2,1,0:T(4,128)S(1)} %get-tuple-element.181, f32[4,8,4,128]{3,2,1,0:T(4,128)S(1)} %get-tuple-element.200, f32[4,8,4]{2,1,0:T(8,128)S(1)} %max.4, ...), kind=kOutput, calls=%fused_computation.7.clone.1 | convolution fusion | flops 8519680 | bytes 2361348 | tf_op jit(solution)/shard_map/while/body/rkgp,rpkd->rkgd/dot_general | solution.py:76
  22.2 22.3 %all_to_all.25 = bf16[16,4,4096]{2,1,0:T(4,128)(2,1)S(1)} all-to-all(bf16[16,4,4096]{2,1,0:T(4,128)(2,1)S(1)} %broadcast_in_dim.85), channel_id=1, replica_groups=mesh['expert'=8,'ffn'=16] {'ffn'}, dimensions={0} | all-to-all | bytes 1048576 | tf_op jit(solution)/shard_map/all_to_all | solution.py:32
  46.1 1.9 %collective-permute-done = f32[64,9]{0,1:T(8,128)S(1)} collective-permute-done((f32[64,9]{0,1:T(8,128)S(1)}, f32[64,9]{0,1:T(8,128)S(1)}, u32[]{:S(2)}, u32[]{:S(2)}) %collective-permute-start) | collective-permute-done | bytes 2336 | tf_op jit(solution)/shard_map/ppermute | solution.py:24
  48.0 1.2 collective-permute-start.1
  49.4 2.6 %collective-permute-done.1 = f32[64,9]{0,1:T(8,128)S(1)} collective-permute-done((f32[64,9]{0,1:T(8,128)S(1)}, f32[64,9]{0,1:T(8,128)S(1)}, u32[]{:S(2)}, u32[]{:S(2)}) %collective-permute-start.1) | collective-permute-done | bytes 2336 | tf_op jit(solution)/shard_map/ppermute | solution.py:24
  52.4 2.1 %collective-permute-done.2 = f32[64,9]{0,1:T(8,128)S(1)} collective-permute-done((f32[64,9]{0,1:T(8,128)S(1)}, f32[64,9]{0,1:T(8,128)S(1)}, u32[]{:S(2)}, u32[]{:S(2)}) %collective-permute-start.2) | collective-permute-done | bytes 2336 | tf_op jit(solution)/shard_map/ppermute | solution.py:24
  54.5 1.4 collective-permute-start.3
  55.9 2.6 %collective-permute-done.3 = f32[64,9]{0,1:T(8,128)S(1)} collective-permute-done((f32[64,9]{0,1:T(8,128)S(1)}, f32[64,9]{0,1:T(8,128)S(1)}, u32[]{:S(2)}, u32[]{:S(2)}) %collective-permute-start.3) | collective-permute-done | bytes 2336 | tf_op jit(solution)/shard_map/ppermute | solution.py:24
  58.9 16.9 %all_to_all.26 = bf16[8,32,256]{2,1,0:T(8,128)(2,1)S(1)} all-to-all(bf16[8,32,256]{2,1,0:T(8,128)(2,1)S(1)} %bitcast.64), channel_id=1, replica_groups=mesh['expert'=8,'ffn'=16] {'expert'}, dimensions={0} | all-to-all | bytes 262144 | tf_op jit(solution)/shard_map/all_to_all | solution.py:144
  76.0 1.5 broadcast_in_dim.92
  77.5 4.4 %all-to-all-start.2 = ((bf16[16,256,256]{1,2,0:T(8,128)(2,1)}), bf16[16,256,256]{1,2,0:T(8,128)(2,1)}, u32[]{:S(2)}, u32[]{:S(2)}) async-start(bf16[16,256,256]{1,2,0:T(8,128)(2,1)} %broadcast_in_dim.92), calls=%async_computation.2 | async-start | bytes 4194304 | tf_op jit(solution)/shard_map/all_to_all | solution.py:32
  81.9 6.5 %copy.64 = bf16[4096,512]{1,0:T(8,128)(2,1)} copy(bf16[4096,512]{0,1:T(8,128)(2,1)} %bitcast.61) | data formatting | bytes 8388608 | tf_op jit(solution)/shard_map/dot_general | solution.py:152
  88.4 22.1 %all-to-all-done.2 = bf16[16,256,256]{1,2,0:T(8,128)(2,1)} async-done(((bf16[16,256,256]{1,2,0:T(8,128)(2,1)}), bf16[16,256,256]{1,2,0:T(8,128)(2,1)}, u32[]{:S(2)}, u32[]{:S(2)}) %all-to-all-start.2) | async-done | bytes 2097184 | tf_op jit(solution)/shard_map/all_to_all | solution.py:32
  110.6 4.1 %fusion.27 = f32[256,512]{1,0:T(8,128)S(1)} fusion(bf16[256,4096]{0,1:T(8,128)(2,1)} %bitcast.10, bf16[1,4096,512]{2,1,0:T(8,128)(2,1)} %param.26), kind=kOutput, calls=%fused_computation.23 | convolution fusion | flops 1073741824 | bytes 6815744 | tf_op jit(solution)/shard_map/dot_general | solution.py:149
  114.7 7.9 %convert_bitcast_fusion = bf16[16,256,256]{2,1,0:T(8,128)(2,1)} fusion(bf16[16,256,512]{2,1,0:T(8,128)(2,1)} %bitcast.62, bf16[256,4096]{0,1:T(8,128)(2,1)} %bitcast.10, bf16[1,4096,512]{2,1,0:T(8,128)(2,1)} %param.27, f32[256,512]{1,0:T(8,128)S(1)} %fusion.27), kind=kOutput, calls=%fused_computation.25 | convolution fusion | flops 2149318656 | bytes 13107200 | tf_op jit(solution)/shard_map/dot_general | solution.py:152
  122.5 29.1 %all_to_all.27 = bf16[16,256,256]{2,1,0:T(8,128)(2,1)} all-to-all(bf16[16,256,256]{2,1,0:T(8,128)(2,1)} %convert_bitcast_fusion), channel_id=1, replica_groups=mesh['expert'=8,'ffn'=16] {'ffn'}, dimensions={0} | all-to-all | bytes 4194304 | tf_op jit(solution)/shard_map/all_to_all | solution.py:154
  151.6 1.9 %reduce_sum.71 = bf16[256,256]{1,0:T(8,128)(2,1)S(1)} reduce(bf16[16,256,256]{2,1,0:T(8,128)(2,1)} %all_to_all.27, bf16[]{:T(256)} %constant.59.clone.1), dimensions={0}, to_apply=%region_11.12 | reduce | flops 983040 | bytes 2228226 | tf_op jit(solution)/shard_map/reduce_sum | solution.py:156
  153.5 12.7 %all_to_all.28 = bf16[8,32,256]{2,1,0:T(8,128)(2,1)S(1)} all-to-all(bf16[8,32,256]{2,1,0:T(8,128)(2,1)S(1)} %bitcast.63), channel_id=1, replica_groups=mesh['expert'=8,'ffn'=16] {'expert'}, dimensions={0} | all-to-all | bytes 262144 | tf_op jit(solution)/shard_map/all_to_all | solution.py:160
  166.2 0.8 fusion.38
  (55 shorter events, 5.8 us)
Async XLA Ops:
  0.0 44.6 %copy-start = (bf16[4096,256]{1,0:T(8,128)(2,1)S(1)}, bf16[4096,256]{1,0:T(8,128)(2,1)}, u32[]{:S(2)}) copy-start(bf16[4096,256]{1,0:T(8,128)(2,1)} %param.23) | copy-start | bytes 6291460
  10.8 6.2 %copy-start.2 = (s32[4]{0:T(128)S(1)}, s32[4]{0:T(128)}, u32[]{:S(2)}) copy-start(s32[4]{0:T(128)} %param.21) | copy-start | bytes 52
  17.1 27.5 %copy-start.1 = (bf16[64,256]{1,0:T(8,128)(2,1)S(1)}, bf16[64,256]{1,0:T(8,128)(2,1)}, u32[]{:S(2)}) copy-start(bf16[64,256]{1,0:T(8,128)(2,1)} %param.22) | copy-start | bytes 98308
  21.8 23.4 %copy-start.4 = (f32[256,8]{0,1:T(8,128)S(1)}, f32[256,8]{0,1:T(8,128)}, u32[]{:S(2)}) copy-start(f32[256,8]{0,1:T(8,128)} %param.25) | copy-start | bytes 24580
  21.8 23.4 %copy-start.5 = (f32[256]{0:T(256)S(1)}, f32[256]{0:T(256)}, u32[]{:S(2)}) copy-start(f32[256]{0:T(256)} %param.24) | copy-start | bytes 3076
  21.8 24.0 %copy-start.3 = (s32[64,2]{0,1:T(2,128)S(1)}, s32[64,2]{0,1:T(2,128)}, u32[]{:S(2)}) copy-start(s32[64,2]{0,1:T(2,128)} %param.29) | copy-start | bytes 1540
  45.4 2.6 %collective-permute-start = (f32[64,9]{0,1:T(8,128)S(1)}, f32[64,9]{0,1:T(8,128)S(1)}, u32[]{:S(2)}, u32[]{:S(2)}) collective-permute-start(f32[64,9]{0,1:T(8,128)S(1)} %pad_maximum_fusion), channel_id=1, source_target_pairs={{0,1},{1,0},{2,3},{3,2},{4,5},{5,4},{6,7},{7,6},{8,9},{9,8},{10,11... | collective-permute-start | bytes 6920 | tf_op jit(solution)/shard_map/ppermute | solution.py:24
  48.0 4.0 %collective-permute-start.1 = (f32[64,9]{0,1:T(8,128)S(1)}, f32[64,9]{0,1:T(8,128)S(1)}, u32[]{:S(2)}, u32[]{:S(2)}) collective-permute-start(f32[64,9]{0,1:T(8,128)S(1)} %fusion.57), channel_id=1, source_target_pairs={{0,2},{1,3},{2,0},{3,1},{4,6},{5,7},{6,4},{7,5},{8,10},{9,11},{10,... | collective-permute-start | bytes 6920 | tf_op jit(solution)/shard_map/ppermute | solution.py:24
  52.0 2.5 %collective-permute-start.2 = (f32[64,9]{0,1:T(8,128)S(1)}, f32[64,9]{0,1:T(8,128)S(1)}, u32[]{:S(2)}, u32[]{:S(2)}) collective-permute-start(f32[64,9]{0,1:T(8,128)S(1)} %add.67), channel_id=1, source_target_pairs={{0,4},{1,5},{2,6},{3,7},{4,0},{5,1},{6,2},{7,3},{8,12},{9,13},{10,... | collective-permute-start | bytes 6920 | tf_op jit(solution)/shard_map/ppermute | solution.py:24
  54.5 4.0 %collective-permute-start.3 = (f32[64,9]{0,1:T(8,128)S(1)}, f32[64,9]{0,1:T(8,128)S(1)}, u32[]{:S(2)}, u32[]{:S(2)}) collective-permute-start(f32[64,9]{0,1:T(8,128)S(1)} %add.68), channel_id=1, source_target_pairs={{0,8},{1,9},{2,10},{3,11},{4,12},{5,13},{6,14},{7,15},{8,0},{9,1},... | collective-permute-start | bytes 6920 | tf_op jit(solution)/shard_map/ppermute | solution.py:24
  77.5 33.1 %all-to-all-start.2 = ((bf16[16,256,256]{1,2,0:T(8,128)(2,1)}), bf16[16,256,256]{1,2,0:T(8,128)(2,1)}, u32[]{:S(2)}, u32[]{:S(2)}) async-start(bf16[16,256,256]{1,2,0:T(8,128)(2,1)} %broadcast_in_dim.92), calls=%async_computation.2 | async-start | bytes 4194304 | tf_op jit(solution)/shard_map/all_to_all | solution.py:32

commit v3 on v2

--- a/solution.py
+++ b/solution.py
@@ -36,10 +36,13 @@
     request_count = queries.shape[0]
     group_size = QH // KVH
     score_scale = 1.0 / math.sqrt(HD)
-    block_size = math.gcd(CACHE, 256)
     query_heads = queries.reshape(request_count, KVH, group_size, HD)
-    key_view = key_cache.reshape(request_count, CACHE, KVH, HD)
-    value_view = value_cache.reshape(request_count, CACHE, KVH, HD)
+    head_eye = jnp.eye(KVH, dtype=queries.dtype)[None, :, None, :, None]
+    spread_queries = (query_heads[:, :, :, None, :] * head_eye).reshape(request_count, QH, KVH * HD)
+    scores = (
+        jnp.einsum("rhc,rpc->rhp", spread_queries, key_cache, preferred_element_type=jnp.float32)
+        * score_scale
+    )
     score_new = (
         jnp.einsum(
             "rkgd,rkd->rkg",
@@ -48,42 +51,22 @@
             preferred_element_type=jnp.float32,
         )
         * score_scale
-    )
-    value_start = jnp.broadcast_to(
-        new_values.reshape(request_count, KVH, 1, HD).astype(jnp.float32),
-        (request_count, KVH, group_size, HD),
-    )
-    initial = (score_new, jnp.ones_like(score_new), value_start)
-
-    def block_step(block_index, carried):
-        running_max, running_den, running_tot = carried
-        offset = block_index * block_size
-        keys_part = lax.dynamic_slice_in_dim(key_view, offset, block_size, 1)
-        values_part = lax.dynamic_slice_in_dim(value_view, offset, block_size, 1)
-        scores = (
-            jnp.einsum(
-                "rkgd,rpkd->rkgp", query_heads, keys_part, preferred_element_type=jnp.float32
-            )
-            * score_scale
-        )
-        positions = offset + jnp.arange(block_size, dtype=jnp.int32)
-        live_mask = (positions[None, :] < lengths[:, None])[:, None, None, :]
-        masked = jnp.where(live_mask, scores, FLOOR)
-        new_max = jnp.maximum(running_max, jnp.max(masked, axis=-1))
-        weights = jnp.where(live_mask, jnp.exp(masked - new_max[..., None]), 0.0)
-        shrink = jnp.exp(running_max - new_max)
-        new_den = running_den * shrink + jnp.sum(weights, axis=-1)
-        new_tot = running_tot * shrink[..., None] + jnp.einsum(
-            "rkgp,rpkd->rkgd",
-            weights.astype(jnp.bfloat16),
-            values_part,
-            preferred_element_type=jnp.float32,
-        )
-        return (new_max, new_den, new_tot)
-
-    block_total = (jnp.max(lengths) + block_size - 1) // block_size
-    final_max, final_den, final_tot = lax.fori_loop(0, block_total, block_step, initial)
-    return (final_tot / final_den[..., None]).astype(jnp.bfloat16).reshape(request_count, QH * HD)
+    ).reshape(request_count, QH)
+    positions = jnp.arange(key_cache.shape[1], dtype=jnp.int32)
+    live_mask = (positions[None, :] < lengths[:, None])[:, None, :]
+    masked = jnp.where(live_mask, scores, FLOOR)
+    largest = jnp.maximum(jnp.max(masked, axis=-1), score_new)
+    weights = jnp.where(live_mask, jnp.exp(masked - largest[..., None]), 0.0)
+    weight_new = jnp.exp(score_new - largest)
+    denoms = jnp.sum(weights, axis=-1) + weight_new
+    spread_totals = jnp.einsum(
+        "rhp,rpc->rhc", weights.astype(jnp.bfloat16), value_cache, preferred_element_type=jnp.float32
+    ).reshape(request_count, KVH, group_size, KVH, HD)
+    totals = jnp.sum(spread_totals * head_eye.astype(jnp.float32), axis=3)
+    rounded_new = weight_new.astype(jnp.bfloat16).astype(jnp.float32).reshape(request_count, KVH, group_size)
+    totals = totals + rounded_new[..., None] * new_values.reshape(request_count, KVH, 1, HD).astype(jnp.float32)
+    denoms = denoms.reshape(request_count, KVH, group_size)
+    return (totals / denoms[..., None]).astype(jnp.bfloat16).reshape(request_count, QH * HD)
 
 
 def local(
@@ -141,23 +124,30 @@
         .reshape(expert_count, capacity, normed.shape[1])
     )
     feature_blocks = lax.axis_size("ffn")
-    received = lax.all_to_all(share_rows, "expert", split_axis=0, concat_axis=0, tiled=True)
-    part_rows = gather_by_exchange(
-        received.reshape(expert_count * capacity, normed.shape[1]), "ffn"
+    width = normed.shape[1]
+    outgoing = jnp.broadcast_to(
+        share_rows[:, None], (expert_count, feature_blocks, capacity, width)
+    ).reshape(expert_count * feature_blocks, capacity, width)
+    incoming = lax.all_to_all(outgoing, ("expert", "ffn"), 0, 0, tiled=True)
+    part_rows = (
+        incoming.reshape(expert_count, feature_blocks, capacity, width)
+        .transpose(0, 2, 1, 3)
+        .reshape(expert_count * capacity, feature_blocks * width)
     )
-    part_rows = part_rows.transpose(1, 0, 2).reshape(expert_count * capacity, -1)
     gate_next = jnp.dot(part_rows, gate_local, preferred_element_type=jnp.float32)
     up_next = jnp.dot(part_rows, up_local, preferred_element_type=jnp.float32)
     inner = (jax.nn.silu(gate_next) * up_next).astype(jnp.bfloat16)
     partial_out = jnp.dot(inner, down_local, preferred_element_type=jnp.float32)
-    partial_out = partial_out.reshape(-1, feature_blocks, normed.shape[1]).transpose(1, 0, 2)
-    pieces = lax.all_to_all(partial_out.astype(jnp.bfloat16), "ffn", 0, 0, tiled=True)
-    summed = (
-        jnp.sum(pieces.astype(jnp.float32), axis=0)
+    partial_out = (
+        partial_out.reshape(expert_count, capacity, feature_blocks, width)
+        .transpose(0, 2, 1, 3)
+        .reshape(expert_count * feature_blocks, capacity, width)
+    )
+    pieces = lax.all_to_all(partial_out.astype(jnp.bfloat16), ("expert", "ffn"), 0, 0, tiled=True)
+    returned = (
+        jnp.sum(pieces.reshape(expert_count, feature_blocks, capacity, width).astype(jnp.float32), axis=1)
         .astype(jnp.bfloat16)
-        .reshape(expert_count, capacity, normed.shape[1])
     )
-    returned = lax.all_to_all(summed, "expert", split_axis=0, concat_axis=0, tiled=True)
     mixed = jnp.dot(
         combine,
         returned.reshape(expert_count * capacity, -1).astype(jnp.float32),

time: 168 us -> 134 us (0.80)
  blocking collectives: 81 us -> 51.8 us
  starting transfers between devices: 7.47 us -> 16.1 us
  local copies, waits for them, and re-layouts: 22.9 us -> 16.7 us
  matrix products: 18.2 us -> 12.4 us
  other arithmetic: 5.16 us -> 3.16 us
    all_to_all x3 -> x1, blocking collectives: 58.7 us -> 34 us  [local(): lax.all_to_all(partial_out.astype(jnp.bfloat16), ('expert', 'ffn'), 0, 0,...]
    unnamed x16 -> x21, local copies, waits for them, and re-layouts: 12.6 us -> 2.97 us
    all_to_all x1, starting transfers between devices: 4.43 us -> 13.6 us  [local(): incoming = lax.all_to_all(outgoing, ('expert', 'ffn'), 0, 0, tiled=True)]
    dot_general x1, matrix products: 7.88 us -> 1.28 us  [local(): partial_out = jnp.dot(inner, down_local, preferred_element_type=jnp.float32)]
    all_to_all x1, blocking collectives: 22.3 us -> 17.7 us  [gather_by_exchange(): return lax.all_to_all(copies, axis_name, 0, 0, tiled=True)]
    dot_general x2 -> x3, matrix products: 4.36 us -> 8.02 us  [the longest x1 3.62 us: attend_local(): jnp.einsum('rhc,rpc->rhp', spread_queries, key_cache, preferred_element_t...]
    transpose x0 -> x1, local copies, waits for them, and re-layouts: none -> 3.01 us  [local(): part_rows = incoming.reshape(expert_count, feature_blocks, capacity, widt...]
    dot_general x1, matrix products: 4.08 us -> 1.24 us  [local(): jnp.dot(part_rows, gate_local, preferred_element_type=jnp.float32)]
  transfers between devices with their start and end apart: 5 -> 5, of which waited for: 5 -> 5; matrix products, arithmetic and copies ran while one was open for 4% -> 6% of each run, Pallas kernels for 0% -> 0%
where the time goes in v3:
time: 134 us; the launch traced here: 133 us
  blocking collectives  51.8 us (39%)
  waiting for transfers between devices  32.6 us (24%)
  local copies, waits for them, and re-layouts  16.7 us (12%)
  starting transfers between devices  16.1 us (12%)
  matrix products  12.4 us (9%)
  other arithmetic  3.16 us (2%)
    all_to_all x1, blocking collectives, local(): lax.all_to_all(partial_out.astype(jnp.bfloat16), ('expert', 'ffn'), 0, 0,...  34 us
    all_to_all x1, waiting for transfers between devices, local(): incoming = lax.all_to_all(outgoing, ('expert', 'ffn'), 0, 0, tiled=True)  22.9 us
    all_to_all x1, blocking collectives, gather_by_exchange(): return lax.all_to_all(copies, axis_name, 0, 0, tiled=True)  17.7 us
    all_to_all x1, starting transfers between devices, local(): incoming = lax.all_to_all(outgoing, ('expert', 'ffn'), 0, 0, tiled=True)  13.6 us
    ppermute x4, waiting for transfers between devices, butterfly_sum(): value = value + lax.ppermute(value, axis_name, pairs)  9.72 us
    dot_general x1, local copies, waits for them, and re-layouts, local(): partial_out = jnp.dot(inner, down_local, preferred_element_type=jnp.float32)  6.48 us
    dot_general x1, matrix products, attend_local(): jnp.einsum('rhc,rpc->rhp', spread_queries, key_cache, preferred_element_t...  3.62 us
    dot_general x1, matrix products, attend_local(): jnp.einsum('rhp,rpc->rhc', weights.astype(jnp.bfloat16), value_cache, pre...  3.08 us
  transfers between devices with their start and end apart: 5, of which 5 were waited for; matrix products, arithmetic and copies ran while one was open for 6% of the time, Pallas kernels for 0%

profile of v3, /device:TPU:1, one launch (start us, length us, event | category | flops | bytes accessed | tf_op | source)
XLA Modules:
  0.0 133.1 jit_solution(1137156874554283040)
XLA Ops:
  0.0 0.9 iota_compare_fusion.3
  2.3 0.8 mul.105
  3.6 3.6 %fusion.38 = (f32[4,32]{1,0:T(4,128)S(1)}, f32[4,32,512]{2,1,0:T(8,128)S(1)}) fusion(bf16[4,512,1024]{2,1,0:T(8,128)(2,1)} %param.17, bf16[4,32,1024]{2,1,0:T(8,128)(2,1)S(1)} %mul.107, bf16[32,1024]{1,0:T(8,128)(2,1)S(1)} %bitcast.81, pred[4,512]{1,0:T(4,128)(4,1)S(1)} %iota_compare_fusion.3), kind=kOutput, calls=%fused_computation.66 | convolution fusion | flops 134545280 | bytes 4786688 | tf_op jit(solution)/shard_map/rhc,rpc->rhp/dot_general | solution.py:43
  7.6 3.1 %fusion.15 = f32[4,32,1024]{2,1,0:T(8,128)S(1)} fusion(bf16[4,512,1024]{2,1,0:T(8,128)(2,1)} %param.18, f32[4,32,512]{2,1,0:T(8,128)S(1)} %get-tuple-element.12, f32[4,32]{1,0:T(4,128)S(1)} %max.12, pred[4,512]{1,0:T(4,128)(4,1)S(1)} %iota_compare_fusion.3), kind=kOutput, calls=%fused_computation.19 | convolution fusion | flops 134414336 | bytes 4983296 | tf_op jit(solution)/shard_map/rhp,rpc->rhc/dot_general | solution.py:62
  11.5 17.7 %all_to_all.15 = bf16[16,4,4096]{2,1,0:T(4,128)(2,1)S(1)} all-to-all(bf16[16,4,4096]{2,1,0:T(4,128)(2,1)S(1)} %broadcast_in_dim.72), channel_id=1, replica_groups=mesh['expert'=8,'ffn'=16] {'ffn'}, dimensions={0} | all-to-all | bytes 1048576 | tf_op jit(solution)/shard_map/all_to_all | solution.py:32
  30.9 1.8 %collective-permute-done = f32[64,9]{0,1:T(8,128)S(1)} collective-permute-done((f32[64,9]{0,1:T(8,128)S(1)}, f32[64,9]{0,1:T(8,128)S(1)}, u32[]{:S(2)}, u32[]{:S(2)}) %collective-permute-start) | collective-permute-done | bytes 2336 | tf_op jit(solution)/shard_map/ppermute | solution.py:24
  32.7 1.0 collective-permute-start.1
  34.0 2.7 %collective-permute-done.1 = f32[64,9]{0,1:T(8,128)S(1)} collective-permute-done((f32[64,9]{0,1:T(8,128)S(1)}, f32[64,9]{0,1:T(8,128)S(1)}, u32[]{:S(2)}, u32[]{:S(2)}) %collective-permute-start.1) | collective-permute-done | bytes 2336 | tf_op jit(solution)/shard_map/ppermute | solution.py:24
  37.1 2.1 %collective-permute-done.2 = f32[64,9]{0,1:T(8,128)S(1)} collective-permute-done((f32[64,9]{0,1:T(8,128)S(1)}, f32[64,9]{0,1:T(8,128)S(1)}, u32[]{:S(2)}, u32[]{:S(2)}) %collective-permute-start.2) | collective-permute-done | bytes 2336 | tf_op jit(solution)/shard_map/ppermute | solution.py:24
  39.2 0.9 collective-permute-start.3
  40.1 3.1 %collective-permute-done.3 = f32[64,9]{0,1:T(8,128)S(1)} collective-permute-done((f32[64,9]{0,1:T(8,128)S(1)}, f32[64,9]{0,1:T(8,128)S(1)}, u32[]{:S(2)}, u32[]{:S(2)}) %collective-permute-start.3) | collective-permute-done | bytes 2336 | tf_op jit(solution)/shard_map/ppermute | solution.py:24
  43.6 1.6 %broadcast_in_dim.79 = bf16[8,16,32,256]{3,2,1,0:T(8,128)(2,1)} broadcast(bf16[8,32,256]{2,1,0:T(8,128)(2,1)S(1)} %bitcast.79), dimensions={0,2,3} | broadcast | bytes 2228224 | tf_op jit(solution)/shard_map/broadcast_in_dim | solution.py:128
  45.3 13.6 %all-to-all-start.1 = ((bf16[128,32,256]{2,1,0:T(8,128)(2,1)}), bf16[128,32,256]{2,1,0:T(8,128)(2,1)}, u32[]{:S(2)}, u32[]{:S(2)}) async-start(bf16[128,32,256]{2,1,0:T(8,128)(2,1)} %bitcast.70), calls=%async_computation.1 | async-start | bytes 4194304 | tf_op jit(solution)/shard_map/all_to_all | solution.py:131
  58.9 6.5 %copy.55 = bf16[4096,512]{1,0:T(8,128)(2,1)} copy(bf16[4096,512]{0,1:T(8,128)(2,1)} %bitcast.72) | data formatting | bytes 8388608 | tf_op jit(solution)/shard_map/dot_general | solution.py:140
  65.3 22.9 %all-to-all-done.1 = bf16[128,32,256]{2,1,0:T(8,128)(2,1)} async-done(((bf16[128,32,256]{2,1,0:T(8,128)(2,1)}), bf16[128,32,256]{2,1,0:T(8,128)(2,1)}, u32[]{:S(2)}, u32[]{:S(2)}) %all-to-all-start.1) | async-done | bytes 2097184 | tf_op jit(solution)/shard_map/all_to_all | solution.py:131
  88.2 3.0 %copy.50 = bf16[8,32,16,256]{3,2,1,0:T(8,128)(2,1)S(1)} copy(bf16[8,32,16,256]{3,1,2,0:T(8,128)(2,1)} %bitcast.7) | data formatting | bytes 4194304 | tf_op jit(solution)/shard_map/transpose | solution.py:134
  91.2 0.9 copy.59
  92.2 1.2 fusion.2
  93.5 0.9 copy-done.7
  94.4 1.3 fusion.7
  95.7 0.9 copy-done.1
  96.6 1.3 convolution_convert_fusion
  97.9 34.0 %all_to_all.16 = bf16[128,32,256]{2,1,0:T(8,128)(2,1)S(1)} all-to-all(bf16[128,32,256]{2,1,0:T(8,128)(2,1)S(1)} %bitcast.76), channel_id=1, replica_groups=mesh['expert'=8,'ffn'=16] {'expert','ffn'}, dimensions={0} | all-to-all | bytes 4194304 | tf_op jit(solution)/shard_map/all_to_all | solution.py:146
  132.2 0.8 fusion.11
  (62 shorter events, 6.0 us)
Async XLA Ops:
  0.0 29.3 %copy-start = (bf16[4096,256]{1,0:T(8,128)(2,1)S(1)}, bf16[4096,256]{1,0:T(8,128)(2,1)}, u32[]{:S(2)}) copy-start(bf16[4096,256]{1,0:T(8,128)(2,1)} %param.21) | copy-start | bytes 6291460
  7.6 21.7 %copy-start.2 = (bf16[64,256]{1,0:T(8,128)(2,1)S(1)}, bf16[64,256]{1,0:T(8,128)(2,1)}, u32[]{:S(2)}) copy-start(bf16[64,256]{1,0:T(8,128)(2,1)} %param.20) | copy-start | bytes 98308
  10.7 19.2 %copy-start.4 = (f32[256,8]{0,1:T(8,128)S(1)}, f32[256,8]{0,1:T(8,128)}, u32[]{:S(2)}) copy-start(f32[256,8]{0,1:T(8,128)} %param.23) | copy-start | bytes 24580
  10.7 19.2 %copy-start.5 = (f32[256]{0:T(256)S(1)}, f32[256]{0:T(256)}, u32[]{:S(2)}) copy-start(f32[256]{0:T(256)} %param.22) | copy-start | bytes 3076
  10.7 19.9 %copy-start.3 = (s32[64,2]{0,1:T(2,128)S(1)}, s32[64,2]{0,1:T(2,128)}, u32[]{:S(2)}) copy-start(s32[64,2]{0,1:T(2,128)} %param.27) | copy-start | bytes 1540
  30.1 2.6 %collective-permute-start = (f32[64,9]{0,1:T(8,128)S(1)}, f32[64,9]{0,1:T(8,128)S(1)}, u32[]{:S(2)}, u32[]{:S(2)}) collective-permute-start(f32[64,9]{0,1:T(8,128)S(1)} %pad_maximum_fusion), channel_id=1, source_target_pairs={{0,1},{1,0},{2,3},{3,2},{4,5},{5,4},{6,7},{7,6},{8,9},{9,8},{10,11... | collective-permute-start | bytes 6920 | tf_op jit(solution)/shard_map/ppermute | solution.py:24
  32.7 4.0 %collective-permute-start.1 = (f32[64,9]{0,1:T(8,128)S(1)}, f32[64,9]{0,1:T(8,128)S(1)}, u32[]{:S(2)}, u32[]{:S(2)}) collective-permute-start(f32[64,9]{0,1:T(8,128)S(1)} %fusion.36), channel_id=1, source_target_pairs={{0,2},{1,3},{2,0},{3,1},{4,6},{5,7},{6,4},{7,5},{8,10},{9,11},{10,... | collective-permute-start | bytes 6920 | tf_op jit(solution)/shard_map/ppermute | solution.py:24
  36.7 2.5 %collective-permute-start.2 = (f32[64,9]{0,1:T(8,128)S(1)}, f32[64,9]{0,1:T(8,128)S(1)}, u32[]{:S(2)}, u32[]{:S(2)}) collective-permute-start(f32[64,9]{0,1:T(8,128)S(1)} %add.54), channel_id=1, source_target_pairs={{0,4},{1,5},{2,6},{3,7},{4,0},{5,1},{6,2},{7,3},{8,12},{9,13},{10,... | collective-permute-start | bytes 6920 | tf_op jit(solution)/shard_map/ppermute | solution.py:24
  39.2 4.0 %collective-permute-start.3 = (f32[64,9]{0,1:T(8,128)S(1)}, f32[64,9]{0,1:T(8,128)S(1)}, u32[]{:S(2)}, u32[]{:S(2)}) collective-permute-start(f32[64,9]{0,1:T(8,128)S(1)} %add.55), channel_id=1, source_target_pairs={{0,8},{1,9},{2,10},{3,11},{4,12},{5,13},{6,14},{7,15},{8,0},{9,1},... | collective-permute-start | bytes 6920 | tf_op jit(solution)/shard_map/ppermute | solution.py:24
  45.3 43.0 %all-to-all-start.1 = ((bf16[128,32,256]{2,1,0:T(8,128)(2,1)}), bf16[128,32,256]{2,1,0:T(8,128)(2,1)}, u32[]{:S(2)}, u32[]{:S(2)}) async-start(bf16[128,32,256]{2,1,0:T(8,128)(2,1)} %bitcast.70), calls=%async_computation.1 | async-start | bytes 4194304 | tf_op jit(solution)/shard_map/all_to_all | solution.py:131
  88.2 4.0 %copy-start.6 = (bf16[1,4096,512]{2,1,0:T(8,128)(2,1)S(1)}, bf16[1,4096,512]{2,1,0:T(8,128)(2,1)}, u32[]{:S(2)}) copy-start(bf16[1,4096,512]{2,1,0:T(8,128)(2,1)} %param.24) | copy-start | bytes 12582916
  92.2 2.2 %copy-start.7 = (bf16[1,4096,512]{2,1,0:T(8,128)(2,1)S(1)}, bf16[1,4096,512]{2,1,0:T(8,128)(2,1)}, u32[]{:S(2)}) copy-start(bf16[1,4096,512]{2,1,0:T(8,128)(2,1)} %param.25) | copy-start | bytes 12582916
  94.4 2.2 %copy-start.1 = (bf16[4096,512]{1,0:T(8,128)(2,1)S(1)}, bf16[4096,512]{1,0:T(8,128)(2,1)}, u32[]{:S(2)}) copy-start(bf16[4096,512]{1,0:T(8,128)(2,1)} %copy.55) | copy-start | bytes 12582916

commit v4 on v3

--- a/solution.py
+++ b/solution.py
@@ -5,11 +5,11 @@
 from jax import lax
 from jax.sharding import PartitionSpec as P
 
+
 D = 4096
 QH = 32
 KVH = 8
 HD = 128
-CACHE = 512
 
 
 EPSILON = 1e-05
@@ -86,7 +86,16 @@
     routes,
 ):
     attended = attend_local(queries, new_keys, new_values, key_cache, value_cache, lengths)
-    gathered = gather_by_exchange(attended, "ffn").reshape(-1, attended.shape[1])
+    gain_high = norm_gain.astype(jnp.bfloat16)
+    gain_low = (norm_gain - gain_high.astype(jnp.float32)).astype(jnp.bfloat16)
+    gain_width = norm_gain.shape[0]
+    gain_row = jnp.concatenate(
+        [gain_high, gain_low, jnp.zeros((attended.shape[1] - 2 * gain_width,), jnp.bfloat16)]
+    )[None]
+    exchanged = gather_by_exchange(jnp.concatenate([attended, gain_row], axis=0), "ffn")
+    gathered = exchanged[:, :-1].reshape(-1, attended.shape[1])
+    gain_parts = exchanged[:, -1, : 2 * gain_width].reshape(-1, 2, gain_width).astype(jnp.float32)
+    gain_full = (gain_parts[:, 0] + gain_parts[:, 1]).reshape(-1)
     hidden = residual.astype(jnp.float32) + jnp.dot(
         gathered,
         out_weight,
@@ -98,7 +107,7 @@
     stats = butterfly_sum(jnp.concatenate([square_part, logit_part], axis=1), "ffn")
     inverse = lax.rsqrt(stats[:, :1] / D + EPSILON)
     logits = stats[:, 1:] * inverse
-    normed = (scaled * inverse).astype(jnp.bfloat16)
+    scaled_rows = scaled.astype(jnp.bfloat16)
     expert_count = lax.axis_size("expert")
     row_count = routes.shape[0]
     capacity = row_count // 2
@@ -114,17 +123,19 @@
     slot_ids = jnp.arange(expert_count * capacity, dtype=jnp.int32)
     slot_hits = slot_ids[:, None, None] == targets[None, :, :]
     dispatch = jnp.sum(slot_hits.astype(jnp.float32), axis=-1).astype(jnp.bfloat16)
+    dispatch, targets = lax.optimization_barrier((dispatch, targets))
+    slot_hits = slot_ids[:, None, None] == targets[None, :, :]
     combine = jnp.sum(jnp.where(slot_hits, route_weights[None, :, :], 0.0), axis=-1).T
     gate_local = gate_weight[0]
     up_local = up_weight[0]
     down_local = down_weight[0]
     share_rows = (
-        jnp.dot(dispatch, normed, preferred_element_type=jnp.float32)
+        jnp.dot(dispatch, scaled_rows, preferred_element_type=jnp.float32)
         .astype(jnp.bfloat16)
-        .reshape(expert_count, capacity, normed.shape[1])
+        .reshape(expert_count, capacity, scaled_rows.shape[1])
     )
     feature_blocks = lax.axis_size("ffn")
-    width = normed.shape[1]
+    width = scaled_rows.shape[1]
     outgoing = jnp.broadcast_to(
         share_rows[:, None], (expert_count, feature_blocks, capacity, width)
     ).reshape(expert_count * feature_blocks, capacity, width)
@@ -134,8 +145,12 @@
         .transpose(0, 2, 1, 3)
         .reshape(expert_count * capacity, feature_blocks * width)
     )
-    gate_next = jnp.dot(part_rows, gate_local, preferred_element_type=jnp.float32)
-    up_next = jnp.dot(part_rows, up_local, preferred_element_type=jnp.float32)
+    rows_f = part_rows.astype(jnp.float32)
+    rows_hidden = rows_f / gain_full
+    row_inverse = lax.rsqrt(jnp.sum(rows_hidden * rows_hidden, axis=-1, keepdims=True) / D + EPSILON)
+    normed_rows = (rows_f * row_inverse).astype(jnp.bfloat16)
+    gate_next = jnp.dot(normed_rows, gate_local, preferred_element_type=jnp.float32)
+    up_next = jnp.dot(normed_rows, up_local, preferred_element_type=jnp.float32)
     inner = (jax.nn.silu(gate_next) * up_next).astype(jnp.bfloat16)
     partial_out = jnp.dot(inner, down_local, preferred_element_type=jnp.float32)
     partial_out = (
@@ -173,6 +188,4 @@
         P("expert", "ffn", None),
         P("expert", None),
     )
-    return jax.shard_map(
-        local, mesh=mesh, in_specs=placed, out_specs=P("expert", "ffn"), check_vma=False
-    )
+    return jax.shard_map(local, mesh=mesh, in_specs=placed, out_specs=P("expert", "ffn"), check_vma=False)

time: 134 us -> 141 us (1.052)
  the two profiles are of different devices: /device:TPU:1 before, /device:TPU:4 now
where the time goes in v4:
time: 141 us; the launch traced here: 140 us
  waiting for transfers between devices  69.3 us (49%)
  starting transfers between devices  27.9 us (20%)
  local copies, waits for them, and re-layouts  18.8 us (13%)
  matrix products  14.8 us (10%)
  other arithmetic  9.04 us (6%)
    ppermute x4, waiting for transfers between devices, butterfly_sum(): value = value + lax.ppermute(value, axis_name, pairs)  33.5 us
    all_to_all x1, waiting for transfers between devices, local(): incoming = lax.all_to_all(outgoing, ('expert', 'ffn'), 0, 0, tiled=True)  21.8 us
    all_to_all x1, waiting for transfers between devices, gather_by_exchange(): return lax.all_to_all(copies, axis_name, 0, 0, tiled=True)  13.9 us
    all_to_all x1, starting transfers between devices, local(): incoming = lax.all_to_all(outgoing, ('expert', 'ffn'), 0, 0, tiled=True)  9.58 us
    all_to_all x1, starting transfers between devices, gather_by_exchange(): return lax.all_to_all(copies, axis_name, 0, 0, tiled=True)  7.45 us
    all_to_all x1, starting transfers between devices, local(): lax.all_to_all(partial_out.astype(jnp.bfloat16), ('expert', 'ffn'), 0, 0,...  6.64 us
    dot_general x1, local copies, waits for them, and re-layouts, local(): partial_out = jnp.dot(inner, down_local, preferred_element_type=jnp.float32)  6.48 us
    ppermute x4, starting transfers between devices, butterfly_sum(): value = value + lax.ppermute(value, axis_name, pairs)  4.23 us
  transfers between devices with their start and end apart: 7, of which 6 were waited for; matrix products, arithmetic and copies ran while one was open for 6% of the time, Pallas kernels for 0%

profile of v4, /device:TPU:4, one launch (start us, length us, event | category | flops | bytes accessed | tf_op | source)
XLA Modules:
  0.0 140.2 jit_solution(18402172942687121934)
XLA Ops:
  2.9 3.6 %fusion.41 = (f32[4,32]{1,0:T(4,128)S(1)}, f32[4,32,512]{2,1,0:T(8,128)S(1)}) fusion(bf16[4,512,1024]{2,1,0:T(8,128)(2,1)} %param.17, bf16[4,32,1024]{2,1,0:T(8,128)(2,1)S(1)} %mul.112, bf16[32,1024]{1,0:T(8,128)(2,1)S(1)} %bitcast.86, pred[4,512]{1,0:T(4,128)(4,1)S(1)} %iota_compare_fusion.4), kind=kOutput, calls=%fused_computation.79 | convolution fusion | flops 134545280 | bytes 4786688 | tf_op jit(solution)/shard_map/rhc,rpc->rhp/dot_general | solution.py:43
  6.9 3.1 %fusion.19 = f32[4,32,1024]{2,1,0:T(8,128)S(1)} fusion(bf16[4,512,1024]{2,1,0:T(8,128)(2,1)} %param.18, f32[4,32,512]{2,1,0:T(8,128)S(1)} %get-tuple-element.16, f32[4,32]{1,0:T(4,128)S(1)} %max.12, pred[4,512]{1,0:T(4,128)(4,1)S(1)} %iota_compare_fusion.4), kind=kOutput, calls=%fused_computation.25 | convolution fusion | flops 134414336 | bytes 4983296 | tf_op jit(solution)/shard_map/rhp,rpc->rhc/dot_general | solution.py:62
  11.8 7.5 %all-to-all-start = ((bf16[16,5,4096]{2,1,0:T(8,128)(2,1)}), bf16[16,5,4096]{2,1,0:T(8,128)(2,1)S(1)}, u32[]{:S(2)}, u32[]{:S(2)}) async-start(bf16[16,5,4096]{2,1,0:T(8,128)(2,1)} %broadcast_in_dim.84), calls=%async_computation | async-start | bytes 2097152 | tf_op jit(solution)/shard_map/all_to_all | solution.py:32
  20.3 13.9 %all-to-all-done = bf16[16,5,4096]{2,1,0:T(8,128)(2,1)S(1)} async-done(((bf16[16,5,4096]{2,1,0:T(8,128)(2,1)}), bf16[16,5,4096]{2,1,0:T(8,128)(2,1)S(1)}, u32[]{:S(2)}, u32[]{:S(2)}) %all-to-all-start) | async-done | bytes 655392 | tf_op jit(solution)/shard_map/all_to_all | solution.py:32
  35.2 2.0 %reshape.164 = bf16[64,4096]{1,0:T(8,128)(2,1)} reshape(bf16[16,4,4096]{2,1,0:T(4,128)(2,1)} %slice.32) | data formatting | bytes 1048576 | tf_op jit(solution)/shard_map/reshape | solution.py:96
  37.1 1.6 %multiply_reduce_fusion.1 = (f32[64]{0:T(128)S(1)}, f32[64,256]{1,0:T(8,128)S(1)}) fusion(bf16[64,4096]{1,0:T(8,128)(2,1)} %reshape.164, bf16[4096,256]{1,0:T(8,128)(2,1)S(1)} %copy-done, bf16[64,256]{1,0:T(8,128)(2,1)S(1)} %copy-done.2), kind=kOutput, calls=%fused_computation.36 | convolution fusion | flops 134283200 | bytes 2720000 | tf_op jit(solution)/shard_map/dot_general | solution.py:99
  39.0 1.6 %broadcast_in_dim.91 = bf16[8,16,32,256]{3,2,1,0:T(8,128)(2,1)} broadcast(bf16[8,32,256]{2,1,0:T(8,128)(2,1)S(1)} %bitcast.84), dimensions={0,2,3} | broadcast | bytes 2228224 | tf_op jit(solution)/shard_map/broadcast_in_dim | solution.py:139
  40.6 9.6 %all-to-all-start.1 = ((bf16[128,32,256]{2,1,0:T(8,128)(2,1)}), bf16[128,32,256]{2,1,0:T(8,128)(2,1)}, u32[]{:S(2)}, u32[]{:S(2)}) async-start(bf16[128,32,256]{2,1,0:T(8,128)(2,1)} %bitcast.75), calls=%async_computation.1 | async-start | bytes 4194304 | tf_op jit(solution)/shard_map/all_to_all | solution.py:142
  50.2 6.5 %copy.64 = bf16[4096,512]{1,0:T(8,128)(2,1)} copy(bf16[4096,512]{0,1:T(8,128)(2,1)} %bitcast.77) | data formatting | bytes 8388608 | tf_op jit(solution)/shard_map/dot_general | solution.py:155
  56.8 21.8 %all-to-all-done.1 = bf16[128,32,256]{2,1,0:T(8,128)(2,1)} async-done(((bf16[128,32,256]{2,1,0:T(8,128)(2,1)}), bf16[128,32,256]{2,1,0:T(8,128)(2,1)}, u32[]{:S(2)}, u32[]{:S(2)}) %all-to-all-start.1) | async-done | bytes 2097184 | tf_op jit(solution)/shard_map/all_to_all | solution.py:142
  78.7 2.2 %fusion.6 = f32[8,32]{1,0:T(8,128)S(1)} fusion(bf16[8,16,32,256]{3,2,1,0:T(8,128)(2,1)} %bitcast.7, f32[16,256]{1,0:T(8,128)S(1)} %bitcast.88), kind=kLoop, calls=%fused_computation.8 | loop fusion | flops 4194048 | bytes 2114560 | tf_op jit(solution)/shard_map/reduce_sum | solution.py:150
  80.9 2.5 %fusion.7 = bf16[8,32,16,256]{3,1,2,0:T(8,128)(2,1)S(1)} fusion(f32[8,32]{1,0:T(8,128)S(1)} %add_rsqrt_fusion, bf16[128,32,256]{2,1,0:T(8,128)(2,1)} %all-to-all-done.1), kind=kLoop, calls=%fused_computation.9 | loop fusion | flops 3145728 | bytes 4195328 | tf_op jit(solution)/shard_map/convert_element_type | solution.py:151
  83.4 1.3 copy.59
  85.6 1.2 fusion.4
  87.8 1.3 fusion.11
  90.0 2.6 %convolution_convert_fusion = bf16[8,32,16,256]{3,1,2,0:T(8,128)(2,1)} fusion(bf16[8,32,512,1]{2,1,3,0:T(8,128)(2,1)S(1)} %bitcast.94, bf16[16,256,512,1]{2,1,0,3:T(8,128)(2,1)S(1)} %bitcast.78), kind=kOutput, calls=%fused_computation.11 | convolution fusion | flops 1074790400 | bytes 6553600 | tf_op jit(solution)/shard_map/dot_general | solution.py:155
  92.6 6.6 %all-to-all-start.2 = ((bf16[128,32,256]{2,1,0:T(8,128)(2,1)}), bf16[128,32,256]{2,1,0:T(8,128)(2,1)}, u32[]{:S(2)}, u32[]{:S(2)}) async-start(bf16[128,32,256]{2,1,0:T(8,128)(2,1)} %bitcast.79), calls=%async_computation.2 | async-start | bytes 4194304 | tf_op jit(solution)/shard_map/all_to_all | solution.py:161
  99.4 1.6 %collective-permute-start = (f32[64,9]{0,1:T(8,128)S(1)}, f32[64,9]{0,1:T(8,128)S(1)}, u32[]{:S(2)}, u32[]{:S(2)}) collective-permute-start(f32[64,9]{0,1:T(8,128)S(1)} %pad_maximum_fusion.2), channel_id=1, source_target_pairs={{0,1},{1,0},{2,3},{3,2},{4,5},{5,4},{6,7},{7,6},{8,9},{9,8},{10,11... | collective-permute-start | bytes 6920 | tf_op jit(solution)/shard_map/ppermute | solution.py:24
  101.0 22.2 %collective-permute-done = f32[64,9]{0,1:T(8,128)S(1)} collective-permute-done((f32[64,9]{0,1:T(8,128)S(1)}, f32[64,9]{0,1:T(8,128)S(1)}, u32[]{:S(2)}, u32[]{:S(2)}) %collective-permute-start) | collective-permute-done | bytes 2336 | tf_op jit(solution)/shard_map/ppermute | solution.py:24
  123.2 2.1 %collective-permute-start.1 = (f32[64,9]{0,1:T(8,128)S(1)}, f32[64,9]{0,1:T(8,128)S(1)}, u32[]{:S(2)}, u32[]{:S(2)}) collective-permute-start(f32[64,9]{0,1:T(8,128)S(1)} %fusion.39), channel_id=1, source_target_pairs={{0,2},{1,3},{2,0},{3,1},{4,6},{5,7},{6,4},{7,5},{8,10},{9,11},{10,... | collective-permute-start | bytes 6920 | tf_op jit(solution)/shard_map/ppermute | solution.py:24
  125.3 3.1 %collective-permute-done.1 = f32[64,9]{0,1:T(8,128)S(1)} collective-permute-done((f32[64,9]{0,1:T(8,128)S(1)}, f32[64,9]{0,1:T(8,128)S(1)}, u32[]{:S(2)}, u32[]{:S(2)}) %collective-permute-start.1) | collective-permute-done | bytes 2336 | tf_op jit(solution)/shard_map/ppermute | solution.py:24
  129.0 3.1 %collective-permute-done.2 = f32[64,9]{0,1:T(8,128)S(1)} collective-permute-done((f32[64,9]{0,1:T(8,128)S(1)}, f32[64,9]{0,1:T(8,128)S(1)}, u32[]{:S(2)}, u32[]{:S(2)}) %collective-permute-start.2) | collective-permute-done | bytes 2336 | tf_op jit(solution)/shard_map/ppermute | solution.py:24
  132.1 5.2 %collective-permute-done.3 = f32[64,9]{0,1:T(8,128)S(1)} collective-permute-done((f32[64,9]{0,1:T(8,128)S(1)}, f32[64,9]{0,1:T(8,128)S(1)}, u32[]{:S(2)}, u32[]{:S(2)}) %collective-permute-start.3) | collective-permute-done | bytes 2336 | tf_op jit(solution)/shard_map/ppermute | solution.py:24
  137.4 1.9 %bitcast_reduce_fusion = bf16[8,32,256]{2,1,0:T(8,128)(2,1)S(1)} fusion(bf16[128,32,256]{2,1,0:T(8,128)(2,1)} %all-to-all-done.2), kind=kLoop, calls=%fused_computation.10 | loop fusion | flops 983040 | bytes 2228224 | tf_op jit(solution)/shard_map/reduce_sum | solution.py:163
  (80 shorter events, 11.8 us)
Async XLA Ops:
  0.0 37.1 %copy-start = (bf16[4096,256]{1,0:T(8,128)(2,1)S(1)}, bf16[4096,256]{1,0:T(8,128)(2,1)}, u32[]{:S(2)}) copy-start(bf16[4096,256]{1,0:T(8,128)(2,1)} %param.21) | copy-start | bytes 6291460
  6.5 3.6 %copy-start.5 = (bf16[4,1024]{1,0:T(4,128)(2,1)S(1)}, bf16[4,1024]{1,0:T(4,128)(2,1)}, u32[]{:S(2)}) copy-start(bf16[4,1024]{1,0:T(4,128)(2,1)} %param.16) | copy-start | bytes 24580
  6.6 4.0 %copy-start.3 = (f32[256]{0:T(256)S(1)}, f32[256]{0:T(256)}, u32[]{:S(2)}) copy-start(f32[256]{0:T(256)} %param.22) | copy-start | bytes 3076
  6.9 12.3 %copy-start.4 = (s32[64,2]{0,1:T(2,128)S(1)}, s32[64,2]{0,1:T(2,128)}, u32[]{:S(2)}) copy-start(s32[64,2]{0,1:T(2,128)} %param.27) | copy-start | bytes 1540
  10.0 27.1 %copy-start.2 = (bf16[64,256]{1,0:T(8,128)(2,1)S(1)}, bf16[64,256]{1,0:T(8,128)(2,1)}, u32[]{:S(2)}) copy-start(bf16[64,256]{1,0:T(8,128)(2,1)} %param.20) | copy-start | bytes 98308
  11.8 22.4 %all-to-all-start = ((bf16[16,5,4096]{2,1,0:T(8,128)(2,1)}), bf16[16,5,4096]{2,1,0:T(8,128)(2,1)S(1)}, u32[]{:S(2)}, u32[]{:S(2)}) async-start(bf16[16,5,4096]{2,1,0:T(8,128)(2,1)} %broadcast_in_dim.84), calls=%async_computation | async-start | bytes 2097152 | tf_op jit(solution)/shard_map/all_to_all | solution.py:32
  40.6 38.1 %all-to-all-start.1 = ((bf16[128,32,256]{2,1,0:T(8,128)(2,1)}), bf16[128,32,256]{2,1,0:T(8,128)(2,1)}, u32[]{:S(2)}, u32[]{:S(2)}) async-start(bf16[128,32,256]{2,1,0:T(8,128)(2,1)} %bitcast.75), calls=%async_computation.1 | async-start | bytes 4194304 | tf_op jit(solution)/shard_map/all_to_all | solution.py:142
  83.4 2.3 %copy-start.7 = (bf16[1,4096,512]{2,1,0:T(8,128)(2,1)S(1)}, bf16[1,4096,512]{2,1,0:T(8,128)(2,1)}, u32[]{:S(2)}) copy-start(bf16[1,4096,512]{2,1,0:T(8,128)(2,1)} %param.24) | copy-start | bytes 12582916
  85.6 2.2 %copy-start.8 = (bf16[1,4096,512]{2,1,0:T(8,128)(2,1)S(1)}, bf16[1,4096,512]{2,1,0:T(8,128)(2,1)}, u32[]{:S(2)}) copy-start(bf16[1,4096,512]{2,1,0:T(8,128)(2,1)} %param.25) | copy-start | bytes 12582916
  87.8 2.2 %copy-start.1 = (bf16[4096,512]{1,0:T(8,128)(2,1)S(1)}, bf16[4096,512]{1,0:T(8,128)(2,1)}, u32[]{:S(2)}) copy-start(bf16[4096,512]{1,0:T(8,128)(2,1)} %copy.64) | copy-start | bytes 12582916
  92.6 6.7 %copy-start.6 = (f32[256,8]{0,1:T(8,128)S(1)}, f32[256,8]{0,1:T(8,128)}, u32[]{:S(2)}) copy-start(f32[256,8]{0,1:T(8,128)} %param.23) | copy-start | bytes 24580
  92.6 44.8 %all-to-all-start.2 = ((bf16[128,32,256]{2,1,0:T(8,128)(2,1)}), bf16[128,32,256]{2,1,0:T(8,128)(2,1)}, u32[]{:S(2)}, u32[]{:S(2)}) async-start(bf16[128,32,256]{2,1,0:T(8,128)(2,1)} %bitcast.79), calls=%async_computation.2 | async-start | bytes 4194304 | tf_op jit(solution)/shard_map/all_to_all | solution.py:161
  99.4 23.8 %collective-permute-start = (f32[64,9]{0,1:T(8,128)S(1)}, f32[64,9]{0,1:T(8,128)S(1)}, u32[]{:S(2)}, u32[]{:S(2)}) collective-permute-start(f32[64,9]{0,1:T(8,128)S(1)} %pad_maximum_fusion.2), channel_id=1, source_target_pairs={{0,1},{1,0},{2,3},{3,2},{4,5},{5,4},{6,7},{7,6},{8,9},{9,8},{10,11... | collective-permute-start | bytes 6920 | tf_op jit(solution)/shard_map/ppermute | solution.py:24
  123.2 5.2 %collective-permute-start.1 = (f32[64,9]{0,1:T(8,128)S(1)}, f32[64,9]{0,1:T(8,128)S(1)}, u32[]{:S(2)}, u32[]{:S(2)}) collective-permute-start(f32[64,9]{0,1:T(8,128)S(1)} %fusion.39), channel_id=1, source_target_pairs={{0,2},{1,3},{2,0},{3,1},{4,6},{5,7},{6,4},{7,5},{8,10},{9,11},{10,... | collective-permute-start | bytes 6920 | tf_op jit(solution)/shard_map/ppermute | solution.py:24
  128.4 3.7 %collective-permute-start.2 = (f32[64,9]{0,1:T(8,128)S(1)}, f32[64,9]{0,1:T(8,128)S(1)}, u32[]{:S(2)}, u32[]{:S(2)}) collective-permute-start(f32[64,9]{0,1:T(8,128)S(1)} %add.72), channel_id=1, source_target_pairs={{0,4},{1,5},{2,6},{3,7},{4,0},{5,1},{6,2},{7,3},{8,12},{9,13},{10,... | collective-permute-start | bytes 6920 | tf_op jit(solution)/shard_map/ppermute | solution.py:24
  132.1 5.2 %collective-permute-start.3 = (f32[64,9]{0,1:T(8,128)S(1)}, f32[64,9]{0,1:T(8,128)S(1)}, u32[]{:S(2)}, u32[]{:S(2)}) collective-permute-start(f32[64,9]{0,1:T(8,128)S(1)} %add.73), channel_id=1, source_target_pairs={{0,8},{1,9},{2,10},{3,11},{4,12},{5,13},{6,14},{7,15},{8,0},{9,1},... | collective-permute-start | bytes 6920 | tf_op jit(solution)/shard_map/ppermute | solution.py:24

commit v5 on v3

--- a/solution.py
+++ b/solution.py
@@ -44,14 +44,9 @@
         * score_scale
     )
     score_new = (
-        jnp.einsum(
-            "rkgd,rkd->rkg",
-            query_heads,
-            new_keys.reshape(request_count, KVH, HD),
-            preferred_element_type=jnp.float32,
-        )
+        jnp.einsum("rhc,rc->rh", spread_queries, new_keys, preferred_element_type=jnp.float32)
         * score_scale
-    ).reshape(request_count, QH)
+    )
     positions = jnp.arange(key_cache.shape[1], dtype=jnp.int32)
     live_mask = (positions[None, :] < lengths[:, None])[:, None, :]
     masked = jnp.where(live_mask, scores, FLOOR)
@@ -59,14 +54,16 @@
     weights = jnp.where(live_mask, jnp.exp(masked - largest[..., None]), 0.0)
     weight_new = jnp.exp(score_new - largest)
     denoms = jnp.sum(weights, axis=-1) + weight_new
+    rounded_new = weight_new.astype(jnp.bfloat16).astype(jnp.float32)
     spread_totals = jnp.einsum(
         "rhp,rpc->rhc", weights.astype(jnp.bfloat16), value_cache, preferred_element_type=jnp.float32
-    ).reshape(request_count, KVH, group_size, KVH, HD)
-    totals = jnp.sum(spread_totals * head_eye.astype(jnp.float32), axis=3)
-    rounded_new = weight_new.astype(jnp.bfloat16).astype(jnp.float32).reshape(request_count, KVH, group_size)
-    totals = totals + rounded_new[..., None] * new_values.reshape(request_count, KVH, 1, HD).astype(jnp.float32)
-    denoms = denoms.reshape(request_count, KVH, group_size)
-    return (totals / denoms[..., None]).astype(jnp.bfloat16).reshape(request_count, QH * HD)
+    ) + rounded_new[..., None] * new_values[:, None, :].astype(jnp.float32)
+    spread_totals = spread_totals / denoms[..., None]
+    totals = jnp.sum(
+        spread_totals.reshape(request_count, KVH, group_size, KVH, HD) * head_eye.astype(jnp.float32),
+        axis=3,
+    )
+    return totals.astype(jnp.bfloat16).reshape(request_count, QH * HD)
 
 
 def local(
@@ -95,7 +92,9 @@
     scaled = hidden * norm_gain
     square_part = jnp.sum(hidden * hidden, axis=-1, keepdims=True)
     logit_part = jnp.dot(scaled, router, precision=lax.Precision.HIGHEST)
-    stats = butterfly_sum(jnp.concatenate([square_part, logit_part], axis=1), "ffn")
+    stats = jnp.sum(
+        gather_by_exchange(jnp.concatenate([square_part, logit_part], axis=1), "ffn"), axis=0
+    )
     inverse = lax.rsqrt(stats[:, :1] / D + EPSILON)
     logits = stats[:, 1:] * inverse
     normed = (scaled * inverse).astype(jnp.bfloat16)

time: 134 us -> 128 us (0.955)
  blocking collectives: 51.8 us -> 34 us
  waiting for transfers between devices: 32.6 us -> 38.8 us
  starting transfers between devices: 16.1 us -> 21 us
    all_to_all x1 -> x0, blocking collectives: 17.7 us -> none  [gather_by_exchange(): return lax.all_to_all(copies, axis_name, 0, 0, tiled=True)]
    all_to_all x0 -> x2, waiting for transfers between devices: none -> 15.9 us  [gather_by_exchange(): return lax.all_to_all(copies, axis_name, 0, 0, tiled=True)]
    all_to_all x0 -> x2, starting transfers between devices: none -> 11.1 us  [gather_by_exchange(): return lax.all_to_all(copies, axis_name, 0, 0, tiled=True)]
    ppermute x4 -> x0, waiting for transfers between devices: 9.72 us -> none  [butterfly_sum(): value = value + lax.ppermute(value, axis_name, pairs)]
    all_to_all x1, starting transfers between devices: 13.6 us -> 9.97 us  [local(): incoming = lax.all_to_all(outgoing, ('expert', 'ffn'), 0, 0, tiled=True)]
    ppermute x4 -> x0, starting transfers between devices: 2.47 us -> none  [butterfly_sum(): value = value + lax.ppermute(value, axis_name, pairs)]
    dot_general x1, matrix products: 3.08 us -> 0.89 us  [attend_local(): jnp.einsum('rhp,rpc->rhc', weights.astype(jnp.bfloat16), value_cache, pre...]
    unnamed x21 -> x25, local copies, waits for them, and re-layouts: 2.97 us -> 3.78 us
  transfers between devices with their start and end apart: 5 -> 3, of which waited for: 5 -> 3; matrix products, arithmetic and copies ran while one was open for 6% -> 6% of each run, Pallas kernels for 0% -> 0%
where the time goes in v5:
time: 128 us; the launch traced here: 127 us
  waiting for transfers between devices  38.8 us (30%)
  blocking collectives  34 us (27%)
  starting transfers between devices  21 us (16%)
  local copies, waits for them, and re-layouts  17.9 us (14%)
  matrix products  11.4 us (9%)
  other arithmetic  3.75 us (3%)
    all_to_all x1, blocking collectives, local(): lax.all_to_all(partial_out.astype(jnp.bfloat16), ('expert', 'ffn'), 0, 0,...  34 us
    all_to_all x1, waiting for transfers between devices, local(): incoming = lax.all_to_all(outgoing, ('expert', 'ffn'), 0, 0, tiled=True)  22.9 us
    all_to_all x2, waiting for transfers between devices, gather_by_exchange(): return lax.all_to_all(copies, axis_name, 0, 0, tiled=True)  15.9 us
    all_to_all x2, starting transfers between devices, gather_by_exchange(): return lax.all_to_all(copies, axis_name, 0, 0, tiled=True)  11.1 us
    all_to_all x1, starting transfers between devices, local(): incoming = lax.all_to_all(outgoing, ('expert', 'ffn'), 0, 0, tiled=True)  9.97 us
    dot_general x1, local copies, waits for them, and re-layouts, local(): partial_out = jnp.dot(inner, down_local, preferred_element_type=jnp.float32)  6.48 us
    dot_general x1, matrix products, attend_local(): jnp.einsum('rhc,rpc->rhp', spread_queries, key_cache, preferred_element_t...  3.86 us
    unnamed x25, local copies, waits for them, and re-layouts  3.78 us
  transfers between devices with their start and end apart: 3, of which 3 were waited for; matrix products, arithmetic and copies ran while one was open for 6% of the time, Pallas kernels for 0%

profile of v5, /device:TPU:1, one launch (start us, length us, event | category | flops | bytes accessed | tf_op | source)
XLA Modules:
  0.0 127.2 jit_solution(6843381554972893146)
XLA Ops:
  0.0 0.9 iota_compare_fusion.3
  1.6 0.8 mul.100
  2.7 1.0 fusion.13
  3.7 3.9 %fusion.39 = (f32[4,32]{1,0:T(4,128)S(1)}, f32[4,32,512]{2,1,0:T(8,128)S(1)}) fusion(bf16[4,512,1024]{2,1,0:T(8,128)(2,1)} %param.17, bf16[4,32,1024]{2,1,0:T(8,128)(2,1)S(1)} %mul.102, bf16[32,1024]{1,0:T(8,128)(2,1)S(1)} %bitcast.80, pred[4,512]{1,0:T(4,128)(4,1)S(1)} %iota_compare_fusion.3), kind=kOutput, calls=%fused_computation.65 | convolution fusion | flops 134545280 | bytes 4786688 | tf_op jit(solution)/shard_map/rhc,rpc->rhp/dot_general | solution.py:43
  7.8 0.9 fusion.7
  9.1 1.0 broadcast_in_dim.81
  10.1 7.6 %all-to-all-start = ((bf16[16,4,4096]{2,1,0:T(4,128)(2,1)}), bf16[16,4,4096]{2,1,0:T(4,128)(2,1)S(1)}, u32[]{:S(2)}, u32[]{:S(2)}) async-start(bf16[16,4,4096]{2,1,0:T(4,128)(2,1)} %broadcast_in_dim.81), calls=%async_computation | async-start | bytes 1048576 | tf_op jit(solution)/shard_map/all_to_all | solution.py:32
  18.6 9.5 %all-to-all-done = bf16[16,4,4096]{2,1,0:T(4,128)(2,1)S(1)} async-done(((bf16[16,4,4096]{2,1,0:T(4,128)(2,1)}), bf16[16,4,4096]{2,1,0:T(4,128)(2,1)S(1)}, u32[]{:S(2)}, u32[]{:S(2)}) %all-to-all-start) | async-done | bytes 524320 | tf_op jit(solution)/shard_map/all_to_all | solution.py:32
  29.7 3.5 %all-to-all-start.1 = ((f32[16,1,576]{2,1,0:T(1,128)}), f32[16,1,576]{2,1,0:T(1,128)S(1)}, u32[]{:S(2)}, u32[]{:S(2)}) async-start(f32[16,1,576]{2,1,0:T(1,128)} %reshape.97), calls=%async_computation.1 | async-start | bytes 81920 | tf_op jit(solution)/shard_map/all_to_all | solution.py:32
  33.2 6.5 %all-to-all-done.1 = f32[16,1,576]{2,1,0:T(1,128)S(1)} async-done(((f32[16,1,576]{2,1,0:T(1,128)}), f32[16,1,576]{2,1,0:T(1,128)S(1)}, u32[]{:S(2)}, u32[]{:S(2)}) %all-to-all-start.1) | async-done | bytes 36896 | tf_op jit(solution)/shard_map/all_to_all | solution.py:32
  40.2 0.7 reduce.1
  41.4 1.6 %broadcast_in_dim.89 = bf16[8,16,32,256]{3,2,1,0:T(8,128)(2,1)} broadcast(bf16[8,32,256]{2,1,0:T(8,128)(2,1)S(1)} %bitcast.77), dimensions={0,2,3} | broadcast | bytes 2228224 | tf_op jit(solution)/shard_map/broadcast_in_dim | solution.py:127
  43.0 10.0 %all-to-all-start.2 = ((bf16[128,32,256]{2,1,0:T(8,128)(2,1)}), bf16[128,32,256]{2,1,0:T(8,128)(2,1)}, u32[]{:S(2)}, u32[]{:S(2)}) async-start(bf16[128,32,256]{2,1,0:T(8,128)(2,1)} %bitcast.68), calls=%async_computation.2 | async-start | bytes 4194304 | tf_op jit(solution)/shard_map/all_to_all | solution.py:130
  53.0 6.5 %copy.58 = bf16[4096,512]{1,0:T(8,128)(2,1)} copy(bf16[4096,512]{0,1:T(8,128)(2,1)} %bitcast.70) | data formatting | bytes 8388608 | tf_op jit(solution)/shard_map/dot_general | solution.py:139
  59.5 22.9 %all-to-all-done.2 = bf16[128,32,256]{2,1,0:T(8,128)(2,1)} async-done(((bf16[128,32,256]{2,1,0:T(8,128)(2,1)}), bf16[128,32,256]{2,1,0:T(8,128)(2,1)}, u32[]{:S(2)}, u32[]{:S(2)}) %all-to-all-start.2) | async-done | bytes 2097184 | tf_op jit(solution)/shard_map/all_to_all | solution.py:130
  82.4 3.0 %copy.53 = bf16[8,32,16,256]{3,2,1,0:T(8,128)(2,1)S(1)} copy(bf16[8,32,16,256]{3,1,2,0:T(8,128)(2,1)} %bitcast.8) | data formatting | bytes 4194304 | tf_op jit(solution)/shard_map/transpose | solution.py:133
  85.4 0.9 copy.61
  86.4 1.2 fusion.2
  87.6 0.9 copy-done.8
  88.6 1.3 %fusion.8 = bf16[256,512]{1,0:T(8,128)(2,1)S(1)} fusion(bf16[256,4096]{1,0:T(8,128)(2,1)S(1)} %bitcast.74, bf16[1,4096,512]{2,1,0:T(8,128)(2,1)S(1)} %copy-done.8, f32[256,512]{1,0:T(8,128)S(1)} %fusion.2), kind=kOutput, calls=%fused_computation.9 | convolution fusion | flops 1074528256 | bytes 7077888 | tf_op jit(solution)/shard_map/dot_general | solution.py:137
  89.9 0.9 copy-done.2
  90.7 1.3 %convolution_convert_fusion = bf16[8,32,16,256]{3,1,2,0:T(8,128)(2,1)S(1)} fusion(bf16[8,32,512,1]{2,1,3,0:T(8,128)(2,1)S(1)} %bitcast.86, bf16[16,256,512,1]{2,1,0,3:T(8,128)(2,1)S(1)} %bitcast.71), kind=kOutput, calls=%fused_computation.5 | convolution fusion | flops 1074790400 | bytes 6553600 | tf_op jit(solution)/shard_map/dot_general | solution.py:139
  92.0 34.0 %all_to_all.20 = bf16[128,32,256]{2,1,0:T(8,128)(2,1)S(1)} all-to-all(bf16[128,32,256]{2,1,0:T(8,128)(2,1)S(1)} %bitcast.75), channel_id=1, replica_groups=mesh['expert'=8,'ffn'=16] {'expert','ffn'}, dimensions={0} | all-to-all | bytes 4194304 | tf_op jit(solution)/shard_map/all_to_all | solution.py:145
  126.4 0.8 fusion.12
  (54 shorter events, 5.3 us)
Async XLA Ops:
  0.0 28.2 %copy-start = (bf16[4096,256]{1,0:T(8,128)(2,1)S(1)}, bf16[4096,256]{1,0:T(8,128)(2,1)}, u32[]{:S(2)}) copy-start(bf16[4096,256]{1,0:T(8,128)(2,1)} %param.21) | copy-start | bytes 6291460
  2.7 5.1 %copy-start.1 = (bf16[4,512,1024]{2,1,0:T(8,128)(2,1)S(1)}, bf16[4,512,1024]{2,1,0:T(8,128)(2,1)}, u32[]{:S(2)}) copy-start(bf16[4,512,1024]{2,1,0:T(8,128)(2,1)} %param.18) | copy-start | bytes 12582916
  7.8 9.9 %copy-start.4 = (s32[64,2]{0,1:T(2,128)S(1)}, s32[64,2]{0,1:T(2,128)}, u32[]{:S(2)}) copy-start(s32[64,2]{0,1:T(2,128)} %param.27) | copy-start | bytes 1540
  7.8 20.4 %copy-start.3 = (bf16[64,256]{1,0:T(8,128)(2,1)S(1)}, bf16[64,256]{1,0:T(8,128)(2,1)}, u32[]{:S(2)}) copy-start(bf16[64,256]{1,0:T(8,128)(2,1)} %param.20) | copy-start | bytes 98308
  8.7 20.0 %copy-start.5 = (f32[256,8]{0,1:T(8,128)S(1)}, f32[256,8]{0,1:T(8,128)}, u32[]{:S(2)}) copy-start(f32[256,8]{0,1:T(8,128)} %param.23) | copy-start | bytes 24580
  8.7 20.0 %copy-start.6 = (f32[256]{0:T(256)S(1)}, f32[256]{0:T(256)}, u32[]{:S(2)}) copy-start(f32[256]{0:T(256)} %param.22) | copy-start | bytes 3076
  10.1 17.9 %all-to-all-start = ((bf16[16,4,4096]{2,1,0:T(4,128)(2,1)}), bf16[16,4,4096]{2,1,0:T(4,128)(2,1)S(1)}, u32[]{:S(2)}, u32[]{:S(2)}) async-start(bf16[16,4,4096]{2,1,0:T(4,128)(2,1)} %broadcast_in_dim.81), calls=%async_computation | async-start | bytes 1048576 | tf_op jit(solution)/shard_map/all_to_all | solution.py:32
  29.7 10.0 %all-to-all-start.1 = ((f32[16,1,576]{2,1,0:T(1,128)}), f32[16,1,576]{2,1,0:T(1,128)S(1)}, u32[]{:S(2)}, u32[]{:S(2)}) async-start(f32[16,1,576]{2,1,0:T(1,128)} %reshape.97), calls=%async_computation.1 | async-start | bytes 81920 | tf_op jit(solution)/shard_map/all_to_all | solution.py:32
  43.0 39.4 %all-to-all-start.2 = ((bf16[128,32,256]{2,1,0:T(8,128)(2,1)}), bf16[128,32,256]{2,1,0:T(8,128)(2,1)}, u32[]{:S(2)}, u32[]{:S(2)}) async-start(bf16[128,32,256]{2,1,0:T(8,128)(2,1)} %bitcast.68), calls=%async_computation.2 | async-start | bytes 4194304 | tf_op jit(solution)/shard_map/all_to_all | solution.py:130
  82.4 4.0 %copy-start.7 = (bf16[1,4096,512]{2,1,0:T(8,128)(2,1)S(1)}, bf16[1,4096,512]{2,1,0:T(8,128)(2,1)}, u32[]{:S(2)}) copy-start(bf16[1,4096,512]{2,1,0:T(8,128)(2,1)} %param.24) | copy-start | bytes 12582916
  86.4 2.2 %copy-start.8 = (bf16[1,4096,512]{2,1,0:T(8,128)(2,1)S(1)}, bf16[1,4096,512]{2,1,0:T(8,128)(2,1)}, u32[]{:S(2)}) copy-start(bf16[1,4096,512]{2,1,0:T(8,128)(2,1)} %param.25) | copy-start | bytes 12582916
  88.5 2.2 %copy-start.2 = (bf16[4096,512]{1,0:T(8,128)(2,1)S(1)}, bf16[4096,512]{1,0:T(8,128)(2,1)}, u32[]{:S(2)}) copy-start(bf16[4096,512]{1,0:T(8,128)(2,1)} %copy.58) | copy-start | bytes 12582916

commit v6 on v5

--- a/solution.py
+++ b/solution.py
@@ -3,6 +3,8 @@
 import jax
 import jax.numpy as jnp
 from jax import lax
+from jax.experimental import pallas as pl
+from jax.experimental.pallas import tpu as pltpu
 from jax.sharding import PartitionSpec as P
 
 D = 4096
@@ -30,6 +32,58 @@
     size = lax.axis_size(axis_name)
     copies = jnp.broadcast_to(value[None], (size,) + value.shape)
     return lax.all_to_all(copies, axis_name, 0, 0, tiled=True)
+
+
+def gate_up_kernel(rows_ref, gate_ref, up_ref, out_ref, gate_acc, up_acc):
+    step = pl.program_id(0)
+    groups, blocks, capacity, width = rows_ref.shape
+
+    @pl.when(step == 0)
+    def _():
+        gate_acc[...] = jnp.zeros_like(gate_acc)
+        up_acc[...] = jnp.zeros_like(up_acc)
+
+    for block in range(blocks):
+        rows = rows_ref[:, block].reshape(groups * capacity, width)
+        gate_acc[...] += jnp.dot(
+            rows, gate_ref[block * width:(block + 1) * width, :], preferred_element_type=jnp.float32
+        )
+        up_acc[...] += jnp.dot(
+            rows, up_ref[block * width:(block + 1) * width, :], preferred_element_type=jnp.float32
+        )
+
+    @pl.when(step == pl.num_programs(0) - 1)
+    def _():
+        gate_sum = gate_acc[...]
+        out_ref[...] = (gate_sum / (1.0 + jnp.exp(-gate_sum)) * up_acc[...]).astype(out_ref.dtype)
+
+
+def gate_up(rows, gate_local, up_local):
+    groups, blocks, capacity, width = rows.shape
+    per_step = 4
+    hidden_units = gate_local.shape[1]
+    row_count = groups * capacity
+    return pl.pallas_call(
+        gate_up_kernel,
+        out_shape=jax.ShapeDtypeStruct((row_count, hidden_units), jnp.bfloat16),
+        grid=(blocks // per_step,),
+        in_specs=[
+            pl.BlockSpec((groups, per_step, capacity, width), lambda j: (0, j, 0, 0)),
+            pl.BlockSpec((per_step * width, hidden_units), lambda j: (j, 0)),
+            pl.BlockSpec((per_step * width, hidden_units), lambda j: (j, 0)),
+        ],
+        out_specs=pl.BlockSpec((row_count, hidden_units), lambda j: (0, 0)),
+        scratch_shapes=[
+            pltpu.VMEM((row_count, hidden_units), jnp.float32),
+            pltpu.VMEM((row_count, hidden_units), jnp.float32),
+        ],
+        compiler_params=pltpu.CompilerParams(dimension_semantics=("arbitrary",)),
+        cost_estimate=pl.CostEstimate(
+            flops=4 * row_count * blocks * width * hidden_units,
+            transcendentals=row_count * hidden_units,
+            bytes_accessed=2 * (rows.size + gate_local.size + up_local.size + row_count * hidden_units),
+        ),
+    )(rows, gate_local, up_local)
 
 
 def attend_local(queries, new_keys, new_values, key_cache, value_cache, lengths):
@@ -128,14 +182,9 @@
         share_rows[:, None], (expert_count, feature_blocks, capacity, width)
     ).reshape(expert_count * feature_blocks, capacity, width)
     incoming = lax.all_to_all(outgoing, ("expert", "ffn"), 0, 0, tiled=True)
-    part_rows = (
-        incoming.reshape(expert_count, feature_blocks, capacity, width)
-        .transpose(0, 2, 1, 3)
-        .reshape(expert_count * capacity, feature_blocks * width)
-    )
-    gate_next = jnp.dot(part_rows, gate_local, preferred_element_type=jnp.float32)
-    up_next = jnp.dot(part_rows, up_local, preferred_element_type=jnp.float32)
-    inner = (jax.nn.silu(gate_next) * up_next).astype(jnp.bfloat16)
+    inner = gate_up(
+        incoming.reshape(expert_count, feature_blocks, capacity, width), gate_local, up_local
+    )
     partial_out = jnp.dot(inner, down_local, preferred_element_type=jnp.float32)
     partial_out = (
         partial_out.reshape(expert_count, capacity, feature_blocks, width)

time: 128 us -> 129 us (level)
  Pallas kernels: 0 us -> 6.72 us
  local copies, waits for them, and re-layouts: 17.9 us -> 12.2 us
    pallas_call x0 -> x1, Pallas kernels: none -> 6.72 us  [gate_up(): pl.pallas_call(gate_up_kernel, out_shape=jax.ShapeDtypeStruct((row_count,...]
    transpose x1 -> x0, local copies, waits for them, and re-layouts: 3.01 us -> none  [local(): part_rows = incoming.reshape(expert_count, feature_blocks, capacity, widt...]
    unnamed x25 -> x18, local copies, waits for them, and re-layouts: 3.78 us -> 1.05 us
    dot_general x2 -> x0, matrix products: 2.56 us -> none  [the longest x1 1.32 us: local(): up_next = jnp.dot(part_rows, up_local, preferred_element_type=jnp.float32)]
    dot_general x1, matrix products: 1.28 us -> 3.57 us  [local(): partial_out = jnp.dot(inner, down_local, preferred_element_type=jnp.float32)]
where the time goes in v6:
time: 129 us; the launch traced here: 128 us
  waiting for transfers between devices  38.8 us (30%)
  blocking collectives  34 us (26%)
  starting transfers between devices  21 us (16%)
  local copies, waits for them, and re-layouts  12.2 us (9%)
  matrix products  11.1 us (9%)
  Pallas kernels  6.72 us (5%)
  other arithmetic  3.75 us (3%)
    all_to_all x1, blocking collectives, local(): lax.all_to_all(partial_out.astype(jnp.bfloat16), ('expert', 'ffn'), 0, 0,...  34 us
    all_to_all x1, waiting for transfers between devices, local(): incoming = lax.all_to_all(outgoing, ('expert', 'ffn'), 0, 0, tiled=True)  22.9 us
    all_to_all x2, waiting for transfers between devices, gather_by_exchange(): return lax.all_to_all(copies, axis_name, 0, 0, tiled=True)  15.9 us
    all_to_all x2, starting transfers between devices, gather_by_exchange(): return lax.all_to_all(copies, axis_name, 0, 0, tiled=True)  11.1 us
    all_to_all x1, starting transfers between devices, local(): incoming = lax.all_to_all(outgoing, ('expert', 'ffn'), 0, 0, tiled=True)  9.97 us
    pallas_call x1, Pallas kernels, gate_up(): pl.pallas_call(gate_up_kernel, out_shape=jax.ShapeDtypeStruct((row_count,...  6.72 us
    dot_general x1, local copies, waits for them, and re-layouts, local(): partial_out = jnp.dot(inner, down_local, preferred_element_type=jnp.float32)  6.48 us
    dot_general x1, matrix products, attend_local(): jnp.einsum('rhc,rpc->rhp', spread_queries, key_cache, preferred_element_t...  3.86 us
  transfers between devices with their start and end apart: 3, of which 3 were waited for; matrix products, arithmetic and copies ran while one was open for 6% of the time, Pallas kernels for 0%

profile of v6, /device:TPU:1, one launch (start us, length us, event | category | flops | bytes accessed | tf_op | source)
XLA Modules:
  0.0 127.9 jit_solution(3537598372561326945)
XLA Ops:
  0.0 0.9 iota_compare_fusion.3
  0.9 0.7 convert_element_type.82
  1.6 0.8 mul.93
  2.7 1.0 fusion.3
  3.7 3.9 %fusion.29 = (f32[4,32]{1,0:T(4,128)S(1)}, f32[4,32,512]{2,1,0:T(8,128)S(1)}) fusion(bf16[4,512,1024]{2,1,0:T(8,128)(2,1)} %param.17, bf16[4,32,1024]{2,1,0:T(8,128)(2,1)S(1)} %mul.95, bf16[32,1024]{1,0:T(8,128)(2,1)S(1)} %bitcast.64, pred[4,512]{1,0:T(4,128)(4,1)S(1)} %iota_compare_fusion.3), kind=kOutput, calls=%fused_computation.59 | convolution fusion | flops 134545280 | bytes 4786688 | tf_op jit(solution)/shard_map/rhc,rpc->rhp/dot_general | solution.py:97
  7.8 0.9 fusion
  9.1 1.0 broadcast_in_dim.81
  10.1 7.6 %all-to-all-start = ((bf16[16,4,4096]{2,1,0:T(4,128)(2,1)}), bf16[16,4,4096]{2,1,0:T(4,128)(2,1)S(1)}, u32[]{:S(2)}, u32[]{:S(2)}) async-start(bf16[16,4,4096]{2,1,0:T(4,128)(2,1)} %broadcast_in_dim.81), calls=%async_computation | async-start | bytes 1048576 | tf_op jit(solution)/shard_map/all_to_all | solution.py:34
  18.6 9.5 %all-to-all-done = bf16[16,4,4096]{2,1,0:T(4,128)(2,1)S(1)} async-done(((bf16[16,4,4096]{2,1,0:T(4,128)(2,1)}), bf16[16,4,4096]{2,1,0:T(4,128)(2,1)S(1)}, u32[]{:S(2)}, u32[]{:S(2)}) %all-to-all-start) | async-done | bytes 524320 | tf_op jit(solution)/shard_map/all_to_all | solution.py:34
  28.2 0.6 multiply_reduce_fusion.1
  29.0 0.7 reshape.93
  29.7 3.5 %all-to-all-start.1 = ((f32[16,1,576]{2,1,0:T(1,128)}), f32[16,1,576]{2,1,0:T(1,128)S(1)}, u32[]{:S(2)}, u32[]{:S(2)}) async-start(f32[16,1,576]{2,1,0:T(1,128)} %reshape.93), calls=%async_computation.1 | async-start | bytes 81920 | tf_op jit(solution)/shard_map/all_to_all | solution.py:34
  33.2 6.5 %all-to-all-done.1 = f32[16,1,576]{2,1,0:T(1,128)S(1)} async-done(((f32[16,1,576]{2,1,0:T(1,128)}), f32[16,1,576]{2,1,0:T(1,128)S(1)}, u32[]{:S(2)}, u32[]{:S(2)}) %all-to-all-start.1) | async-done | bytes 36896 | tf_op jit(solution)/shard_map/all_to_all | solution.py:34
  39.7 0.5 broadcast.41
  40.2 0.7 reduce.1
  41.4 1.6 %broadcast_in_dim.89 = bf16[8,16,32,256]{3,2,1,0:T(8,128)(2,1)} broadcast(bf16[8,32,256]{2,1,0:T(8,128)(2,1)S(1)} %bitcast.61), dimensions={0,2,3} | broadcast | bytes 2228224 | tf_op jit(solution)/shard_map/broadcast_in_dim | solution.py:181
  43.0 10.0 %all-to-all-start.2 = ((bf16[128,32,256]{2,1,0:T(8,128)(2,1)}), bf16[128,32,256]{2,1,0:T(8,128)(2,1)}, u32[]{:S(2)}, u32[]{:S(2)}) async-start(bf16[128,32,256]{2,1,0:T(8,128)(2,1)} %bitcast.53), calls=%async_computation.2 | async-start | bytes 4194304 | tf_op jit(solution)/shard_map/all_to_all | solution.py:184
  53.0 6.5 %copy.47 = bf16[4096,512]{1,0:T(8,128)(2,1)} copy(bf16[4096,512]{0,1:T(8,128)(2,1)} %bitcast.54) | data formatting | bytes 8388608 | tf_op jit(solution)/shard_map/dot_general | solution.py:188
  59.5 22.9 %all-to-all-done.2 = bf16[128,32,256]{2,1,0:T(8,128)(2,1)} async-done(((bf16[128,32,256]{2,1,0:T(8,128)(2,1)}), bf16[128,32,256]{2,1,0:T(8,128)(2,1)}, u32[]{:S(2)}, u32[]{:S(2)}) %all-to-all-start.2) | async-done | bytes 2097184 | tf_op jit(solution)/shard_map/all_to_all | solution.py:184
  82.4 6.7 %shard_map.136 = bf16[256,512]{1,0:T(8,128)(2,1)} custom-call(bf16[8,16,32,256]{3,2,1,0:T(8,128)(2,1)} %bitcast.7.rows_ref, bf16[4096,512]{1,0:T(8,128)(2,1)} %bitcast.56, bf16[4096,512]{1,0:T(8,128)(2,1)} %bitcast.57), custom_call_target="tpu_custom_call" | custom-call | flops 2147483648 | bytes 10747904 | tf_op jit(solution)/shard_map/pallas_call | solution.py:66
  89.1 3.6 %convolution_convert_fusion = bf16[8,32,16,256]{3,1,2,0:T(8,128)(2,1)S(1)} fusion(bf16[8,32,512,1]{2,1,3,0:T(8,128)(2,1)} %bitcast.66, bf16[16,256,512,1]{2,1,0,3:T(8,128)(2,1)} %bitcast.55), kind=kOutput, calls=%fused_computation.1 | convolution fusion | flops 1074790400 | bytes 6553600 | tf_op jit(solution)/shard_map/dot_general | solution.py:188
  92.7 34.0 %all_to_all.20 = bf16[128,32,256]{2,1,0:T(8,128)(2,1)S(1)} all-to-all(bf16[128,32,256]{2,1,0:T(8,128)(2,1)S(1)} %bitcast.59), channel_id=1, replica_groups=mesh['expert'=8,'ffn'=16] {'expert','ffn'}, dimensions={0} | all-to-all | bytes 4194304 | tf_op jit(solution)/shard_map/all_to_all | solution.py:194
  126.7 0.3 bitcast_reduce_fusion
  127.1 0.8 fusion.2
  (45 shorter events, 2.5 us)
Async XLA Ops:
  0.0 28.2 %copy-start = (bf16[4096,256]{1,0:T(8,128)(2,1)S(1)}, bf16[4096,256]{1,0:T(8,128)(2,1)}, u32[]{:S(2)}) copy-start(bf16[4096,256]{1,0:T(8,128)(2,1)} %param.21) | copy-start | bytes 6291460
  2.7 5.1 %copy-start.1 = (bf16[4,512,1024]{2,1,0:T(8,128)(2,1)S(1)}, bf16[4,512,1024]{2,1,0:T(8,128)(2,1)}, u32[]{:S(2)}) copy-start(bf16[4,512,1024]{2,1,0:T(8,128)(2,1)} %param.18) | copy-start | bytes 12582916
  7.8 9.9 %copy-start.3 = (s32[64,2]{0,1:T(2,128)S(1)}, s32[64,2]{0,1:T(2,128)}, u32[]{:S(2)}) copy-start(s32[64,2]{0,1:T(2,128)} %param.27) | copy-start | bytes 1540
  7.8 20.4 %copy-start.2 = (bf16[64,256]{1,0:T(8,128)(2,1)S(1)}, bf16[64,256]{1,0:T(8,128)(2,1)}, u32[]{:S(2)}) copy-start(bf16[64,256]{1,0:T(8,128)(2,1)} %param.20) | copy-start | bytes 98308
  8.7 20.0 %copy-start.4 = (f32[256,8]{0,1:T(8,128)S(1)}, f32[256,8]{0,1:T(8,128)}, u32[]{:S(2)}) copy-start(f32[256,8]{0,1:T(8,128)} %param.23) | copy-start | bytes 24580
  8.7 20.0 %copy-start.5 = (f32[256]{0:T(256)S(1)}, f32[256]{0:T(256)}, u32[]{:S(2)}) copy-start(f32[256]{0:T(256)} %param.22) | copy-start | bytes 3076
  10.1 17.9 %all-to-all-start = ((bf16[16,4,4096]{2,1,0:T(4,128)(2,1)}), bf16[16,4,4096]{2,1,0:T(4,128)(2,1)S(1)}, u32[]{:S(2)}, u32[]{:S(2)}) async-start(bf16[16,4,4096]{2,1,0:T(4,128)(2,1)} %broadcast_in_dim.81), calls=%async_computation | async-start | bytes 1048576 | tf_op jit(solution)/shard_map/all_to_all | solution.py:34
  29.7 10.0 %all-to-all-start.1 = ((f32[16,1,576]{2,1,0:T(1,128)}), f32[16,1,576]{2,1,0:T(1,128)S(1)}, u32[]{:S(2)}, u32[]{:S(2)}) async-start(f32[16,1,576]{2,1,0:T(1,128)} %reshape.93), calls=%async_computation.1 | async-start | bytes 81920 | tf_op jit(solution)/shard_map/all_to_all | solution.py:34
  43.0 39.4 %all-to-all-start.2 = ((bf16[128,32,256]{2,1,0:T(8,128)(2,1)}), bf16[128,32,256]{2,1,0:T(8,128)(2,1)}, u32[]{:S(2)}, u32[]{:S(2)}) async-start(bf16[128,32,256]{2,1,0:T(8,128)(2,1)} %bitcast.53), calls=%async_computation.2 | async-start | bytes 4194304 | tf_op jit(solution)/shard_map/all_to_all | solution.py:184

commit v7 on v5

--- a/solution.py
+++ b/solution.py
@@ -3,6 +3,8 @@
 import jax
 import jax.numpy as jnp
 from jax import lax
+from jax.experimental import pallas as pl
+from jax.experimental.pallas import tpu as pltpu
 from jax.sharding import PartitionSpec as P
 
 D = 4096
@@ -30,6 +32,65 @@
     size = lax.axis_size(axis_name)
     copies = jnp.broadcast_to(value[None], (size,) + value.shape)
     return lax.all_to_all(copies, axis_name, 0, 0, tiled=True)
+
+
+def expert_kernel(rows_hbm, gate_hbm, up_hbm, down_hbm, out_ref, rows_v, gate_v, up_v, down_v, sems):
+    groups, blocks, capacity, width = rows_v.shape
+    row_count = groups * capacity
+    hidden_units = gate_v.shape[1]
+    copies = []
+    for block in range(blocks):
+        span = pl.ds(block * width, width)
+        trio = (
+            pltpu.make_async_copy(rows_hbm.at[:, block], rows_v.at[:, block], sems.at[0, block]),
+            pltpu.make_async_copy(gate_hbm.at[span], gate_v.at[span], sems.at[1, block]),
+            pltpu.make_async_copy(up_hbm.at[span], up_v.at[span], sems.at[2, block]),
+        )
+        for copy in trio:
+            copy.start()
+        copies.append(trio)
+    down_copy = pltpu.make_async_copy(down_hbm, down_v, sems.at[3, 0])
+    down_copy.start()
+    gate_sum = jnp.zeros((row_count, hidden_units), jnp.float32)
+    up_sum = jnp.zeros((row_count, hidden_units), jnp.float32)
+    for block in range(blocks):
+        for copy in copies[block]:
+            copy.wait()
+        rows = rows_v[:, block].reshape(row_count, width)
+        span = pl.ds(block * width, width)
+        gate_sum += jnp.dot(rows, gate_v[span, :], preferred_element_type=jnp.float32)
+        up_sum += jnp.dot(rows, up_v[span, :], preferred_element_type=jnp.float32)
+    inner = (gate_sum / (1.0 + jnp.exp(-gate_sum)) * up_sum).astype(jnp.bfloat16)
+    down_copy.wait()
+    for block in range(blocks):
+        part = jnp.dot(inner, down_v[:, pl.ds(block * width, width)], preferred_element_type=jnp.float32)
+        out_ref[:, block] = part.astype(out_ref.dtype).reshape(groups, capacity, width)
+
+
+def expert_block(rows, gate_local, up_local, down_local):
+    groups, blocks, capacity, width = rows.shape
+    hidden_units = gate_local.shape[1]
+    row_count = groups * capacity
+    anywhere = pl.BlockSpec(memory_space=pl.ANY)
+    return pl.pallas_call(
+        expert_kernel,
+        out_shape=jax.ShapeDtypeStruct(rows.shape, jnp.bfloat16),
+        in_specs=[anywhere, anywhere, anywhere, anywhere],
+        out_specs=pl.BlockSpec(memory_space=pltpu.VMEM),
+        scratch_shapes=[
+            pltpu.VMEM(rows.shape, rows.dtype),
+            pltpu.VMEM(gate_local.shape, gate_local.dtype),
+            pltpu.VMEM(up_local.shape, up_local.dtype),
+            pltpu.VMEM(down_local.shape, down_local.dtype),
+            pltpu.SemaphoreType.DMA((4, blocks)),
+        ],
+        compiler_params=pltpu.CompilerParams(vmem_limit_bytes=48 * 1024 * 1024),
+        cost_estimate=pl.CostEstimate(
+            flops=6 * row_count * blocks * width * hidden_units,
+            transcendentals=row_count * hidden_units,
+            bytes_accessed=2 * (2 * rows.size + gate_local.size + up_local.size + down_local.size),
+        ),
+    )(rows, gate_local, up_local, down_local)
 
 
 def attend_local(queries, new_keys, new_values, key_cache, value_cache, lengths):
@@ -128,21 +189,10 @@
         share_rows[:, None], (expert_count, feature_blocks, capacity, width)
     ).reshape(expert_count * feature_blocks, capacity, width)
     incoming = lax.all_to_all(outgoing, ("expert", "ffn"), 0, 0, tiled=True)
-    part_rows = (
-        incoming.reshape(expert_count, feature_blocks, capacity, width)
-        .transpose(0, 2, 1, 3)
-        .reshape(expert_count * capacity, feature_blocks * width)
-    )
-    gate_next = jnp.dot(part_rows, gate_local, preferred_element_type=jnp.float32)
-    up_next = jnp.dot(part_rows, up_local, preferred_element_type=jnp.float32)
-    inner = (jax.nn.silu(gate_next) * up_next).astype(jnp.bfloat16)
-    partial_out = jnp.dot(inner, down_local, preferred_element_type=jnp.float32)
-    partial_out = (
-        partial_out.reshape(expert_count, capacity, feature_blocks, width)
-        .transpose(0, 2, 1, 3)
-        .reshape(expert_count * feature_blocks, capacity, width)
-    )
-    pieces = lax.all_to_all(partial_out.astype(jnp.bfloat16), ("expert", "ffn"), 0, 0, tiled=True)
+    partial_out = expert_block(
+        incoming.reshape(expert_count, feature_blocks, capacity, width), gate_local, up_local, down_local
+    ).reshape(expert_count * feature_blocks, capacity, width)
+    pieces = lax.all_to_all(partial_out, ("expert", "ffn"), 0, 0, tiled=True)
     returned = (
         jnp.sum(pieces.reshape(expert_count, feature_blocks, capacity, width).astype(jnp.float32), axis=1)
         .astype(jnp.bfloat16)

time: 128 us -> 123 us (0.961)
  blocking collectives: 34 us -> 73.1 us
  waiting for transfers between devices: 38.8 us -> 15.9 us
  local copies, waits for them, and re-layouts: 17.9 us -> 4.32 us
  starting transfers between devices: 21 us -> 11.1 us
  Pallas kernels: 0 us -> 6.62 us
  matrix products: 11.4 us -> 7.53 us
    all_to_all x1 -> x2, blocking collectives: 34 us -> 73.1 us  [the longest x1 39.1 us: local(): incoming = lax.all_to_all(outgoing, ('expert', 'ffn'), 0, 0, tiled=True)]
    all_to_all x1 -> x0, waiting for transfers between devices: 22.9 us -> none  [local(): incoming = lax.all_to_all(outgoing, ('expert', 'ffn'), 0, 0, tiled=True)]
    all_to_all x1 -> x0, starting transfers between devices: 9.97 us -> none  [local(): incoming = lax.all_to_all(outgoing, ('expert', 'ffn'), 0, 0, tiled=True)]
    pallas_call x0 -> x1, Pallas kernels: none -> 6.62 us  [expert_block(): pl.pallas_call(expert_kernel, out_shape=jax.ShapeDtypeStruct(rows.shape,...]
    dot_general x1 -> x0, local copies, waits for them, and re-layouts: 6.48 us -> none  [local(): partial_out = jnp.dot(inner, down_local, preferred_element_type=jnp.float32)]
    dot_general x3 -> x0, matrix products: 3.84 us -> none  [the longest x1 1.32 us: local(): up_next = jnp.dot(part_rows, up_local, preferred_element_type=jnp.float32)]
    transpose x1 -> x0, local copies, waits for them, and re-layouts: 3.01 us -> none  [local(): part_rows = incoming.reshape(expert_count, feature_blocks, capacity, widt...]
    unnamed x25 -> x18, local copies, waits for them, and re-layouts: 3.78 us -> 1.05 us
  transfers between devices with their start and end apart: 3 -> 2, of which waited for: 3 -> 2; matrix products, arithmetic and copies ran while one was open for 6% -> 1% of each run, Pallas kernels for 0% -> 0%
where the time goes in v7:
time: 123 us
  blocking collectives  73.1 us (59%)
  waiting for transfers between devices  15.9 us (13%)
  starting transfers between devices  11.1 us (9%)
  matrix products  7.53 us (6%)
  Pallas kernels  6.62 us (5%)
  local copies, waits for them, and re-layouts  4.32 us (4%)
  other arithmetic  3.75 us (3%)
    all_to_all x1, blocking collectives, local(): incoming = lax.all_to_all(outgoing, ('expert', 'ffn'), 0, 0, tiled=True)  39.1 us
    all_to_all x1, blocking collectives, local(): pieces = lax.all_to_all(partial_out, ('expert', 'ffn'), 0, 0, tiled=True)  34 us
    all_to_all x2, waiting for transfers between devices, gather_by_exchange(): return lax.all_to_all(copies, axis_name, 0, 0, tiled=True)  15.9 us
    all_to_all x2, starting transfers between devices, gather_by_exchange(): return lax.all_to_all(copies, axis_name, 0, 0, tiled=True)  11.1 us
    pallas_call x1, Pallas kernels, expert_block(): pl.pallas_call(expert_kernel, out_shape=jax.ShapeDtypeStruct(rows.shape,...  6.62 us
    dot_general x1, matrix products, attend_local(): jnp.einsum('rhc,rpc->rhp', spread_queries, key_cache, preferred_element_t...  3.86 us
  transfers between devices with their start and end apart: 2, of which 2 were waited for; matrix products, arithmetic and copies ran while one was open for 1% of the time, Pallas kernels for 0%

profile of v7, /device:TPU:1, one launch (start us, length us, event | category | flops | bytes accessed | tf_op | source)
XLA Modules:
  0.0 122.6 jit_solution(9339086514060203166)
XLA Ops:
  0.0 0.9 iota_compare_fusion.3
  0.9 0.7 convert_element_type.73
  1.6 0.8 mul.93
  2.7 1.0 fusion.3
  3.7 3.9 %fusion.29 = (f32[4,32]{1,0:T(4,128)S(1)}, f32[4,32,512]{2,1,0:T(8,128)S(1)}) fusion(bf16[4,512,1024]{2,1,0:T(8,128)(2,1)} %param.17, bf16[4,32,1024]{2,1,0:T(8,128)(2,1)S(1)} %mul.95, bf16[32,1024]{1,0:T(8,128)(2,1)S(1)} %bitcast.50, pred[4,512]{1,0:T(4,128)(4,1)S(1)} %iota_compare_fusion.3), kind=kOutput, calls=%fused_computation.58 | convolution fusion | flops 134545280 | bytes 4786688 | tf_op jit(solution)/shard_map/rhc,rpc->rhp/dot_general | solution.py:104
  7.6 0.2 fusion.6
  7.8 0.9 fusion
  8.8 0.2 multiply_reduce_fusion
  9.1 1.0 broadcast_in_dim.81
  10.1 7.6 %all-to-all-start = ((bf16[16,4,4096]{2,1,0:T(4,128)(2,1)}), bf16[16,4,4096]{2,1,0:T(4,128)(2,1)S(1)}, u32[]{:S(2)}, u32[]{:S(2)}) async-start(bf16[16,4,4096]{2,1,0:T(4,128)(2,1)} %broadcast_in_dim.81), calls=%async_computation | async-start | bytes 1048576 | tf_op jit(solution)/shard_map/all_to_all | solution.py:34
  18.6 9.5 %all-to-all-done = bf16[16,4,4096]{2,1,0:T(4,128)(2,1)S(1)} async-done(((bf16[16,4,4096]{2,1,0:T(4,128)(2,1)}), bf16[16,4,4096]{2,1,0:T(4,128)(2,1)S(1)}, u32[]{:S(2)}, u32[]{:S(2)}) %all-to-all-start) | async-done | bytes 524320 | tf_op jit(solution)/shard_map/all_to_all | solution.py:34
  28.2 0.6 multiply_reduce_fusion.1
  29.0 0.7 reshape.90
  29.7 3.5 %all-to-all-start.1 = ((f32[16,1,576]{2,1,0:T(1,128)}), f32[16,1,576]{2,1,0:T(1,128)S(1)}, u32[]{:S(2)}, u32[]{:S(2)}) async-start(f32[16,1,576]{2,1,0:T(1,128)} %reshape.90), calls=%async_computation.1 | async-start | bytes 81920 | tf_op jit(solution)/shard_map/all_to_all | solution.py:34
  33.2 6.5 %all-to-all-done.1 = f32[16,1,576]{2,1,0:T(1,128)S(1)} async-done(((f32[16,1,576]{2,1,0:T(1,128)}), f32[16,1,576]{2,1,0:T(1,128)S(1)}, u32[]{:S(2)}, u32[]{:S(2)}) %all-to-all-start.1) | async-done | bytes 36896 | tf_op jit(solution)/shard_map/all_to_all | solution.py:34
  39.7 0.5 broadcast.41
  40.2 0.7 reduce.1
  41.2 0.2 convolution_convert_fusion
  41.4 0.3 broadcast_in_dim.89
  41.7 39.1 %all_to_all.20 = bf16[128,32,256]{2,1,0:T(8,128)(2,1)S(1)} all-to-all(bf16[128,32,256]{2,1,0:T(8,128)(2,1)S(1)} %bitcast.41), channel_id=1, replica_groups=mesh['expert'=8,'ffn'=16] {'expert','ffn'}, dimensions={0} | all-to-all | bytes 4194304 | tf_op jit(solution)/shard_map/all_to_all | solution.py:191
  80.8 6.6 %shard_map.136 = bf16[8,16,32,256]{3,2,1,0:T(8,128)(2,1)S(1)} custom-call(bf16[8,16,32,256]{3,2,1,0:T(8,128)(2,1)S(1)} %bitcast.39, bf16[4096,512]{1,0:T(8,128)(2,1)} %bitcast.42, bf16[4096,512]{1,0:T(8,128)(2,1)} %bitcast.43, bf16[512,4096]{1,0:T(8,128)(2,1)} %bitcast.44), custom_call_target="tpu_custom_call" | custom-call | flops 3221225472 | bytes 16777216 | tf_op jit(solution)/shard_map/pallas_call | solution.py:75
  87.4 34.0 %all_to_all.21 = bf16[128,32,256]{2,1,0:T(8,128)(2,1)S(1)} all-to-all(bf16[128,32,256]{2,1,0:T(8,128)(2,1)S(1)} %bitcast.40), channel_id=1, replica_groups=mesh['expert'=8,'ffn'=16] {'expert','ffn'}, dimensions={0} | all-to-all | bytes 4194304 | tf_op jit(solution)/shard_map/all_to_all | solution.py:195
  121.4 0.3 bitcast_reduce_fusion
  121.8 0.8 fusion.2
  (42 shorter events, 1.9 us)
Async XLA Ops:
  0.0 28.2 %copy-start = (bf16[4096,256]{1,0:T(8,128)(2,1)S(1)}, bf16[4096,256]{1,0:T(8,128)(2,1)}, u32[]{:S(2)}) copy-start(bf16[4096,256]{1,0:T(8,128)(2,1)} %param.21) | copy-start | bytes 6291460
  2.7 5.1 %copy-start.1 = (bf16[4,512,1024]{2,1,0:T(8,128)(2,1)S(1)}, bf16[4,512,1024]{2,1,0:T(8,128)(2,1)}, u32[]{:S(2)}) copy-start(bf16[4,512,1024]{2,1,0:T(8,128)(2,1)} %param.18) | copy-start | bytes 12582916
  7.8 9.9 %copy-start.3 = (s32[64,2]{0,1:T(2,128)S(1)}, s32[64,2]{0,1:T(2,128)}, u32[]{:S(2)}) copy-start(s32[64,2]{0,1:T(2,128)} %param.27) | copy-start | bytes 1540
  7.8 20.4 %copy-start.2 = (bf16[64,256]{1,0:T(8,128)(2,1)S(1)}, bf16[64,256]{1,0:T(8,128)(2,1)}, u32[]{:S(2)}) copy-start(bf16[64,256]{1,0:T(8,128)(2,1)} %param.20) | copy-start | bytes 98308
  8.7 20.0 %copy-start.4 = (f32[256,8]{0,1:T(8,128)S(1)}, f32[256,8]{0,1:T(8,128)}, u32[]{:S(2)}) copy-start(f32[256,8]{0,1:T(8,128)} %param.23) | copy-start | bytes 24580
  8.7 20.0 %copy-start.5 = (f32[256]{0:T(256)S(1)}, f32[256]{0:T(256)}, u32[]{:S(2)}) copy-start(f32[256]{0:T(256)} %param.22) | copy-start | bytes 3076
  10.1 17.9 %all-to-all-start = ((bf16[16,4,4096]{2,1,0:T(4,128)(2,1)}), bf16[16,4,4096]{2,1,0:T(4,128)(2,1)S(1)}, u32[]{:S(2)}, u32[]{:S(2)}) async-start(bf16[16,4,4096]{2,1,0:T(4,128)(2,1)} %broadcast_in_dim.81), calls=%async_computation | async-start | bytes 1048576 | tf_op jit(solution)/shard_map/all_to_all | solution.py:34
  29.7 10.0 %all-to-all-start.1 = ((f32[16,1,576]{2,1,0:T(1,128)}), f32[16,1,576]{2,1,0:T(1,128)S(1)}, u32[]{:S(2)}, u32[]{:S(2)}) async-start(f32[16,1,576]{2,1,0:T(1,128)} %reshape.90), calls=%async_computation.1 | async-start | bytes 81920 | tf_op jit(solution)/shard_map/all_to_all | solution.py:34

commit v8 on v7

--- a/solution.py
+++ b/solution.py
@@ -93,38 +93,74 @@
     )(rows, gate_local, up_local, down_local)
 
 
+def attend_kernel(
+    lengths_ref, queries_ref, new_keys_ref, new_values_ref, keys_hbm, values_hbm, out_ref, keys_v, values_v, sems
+):
+    request_count, heads, width = queries_ref.shape
+    group_size = heads // KVH
+    score_scale = 1.0 / math.sqrt(HD)
+    copies = []
+    for request in range(request_count):
+        pair = (
+            pltpu.make_async_copy(keys_hbm.at[request], keys_v.at[request], sems.at[0, request]),
+            pltpu.make_async_copy(values_hbm.at[request], values_v.at[request], sems.at[1, request]),
+        )
+        for copy in pair:
+            copy.start()
+        copies.append(pair)
+    head_group = lax.broadcasted_iota(jnp.int32, (heads, 1), 0) // group_size
+    for request in range(request_count):
+        for copy in copies[request]:
+            copy.wait()
+        spread = queries_ref[request]
+        scores = lax.dot_general(
+            spread, keys_v[request], (((1,), (1,)), ((), ())), preferred_element_type=jnp.float32
+        ) * score_scale
+        key_new = new_keys_ref[pl.ds(request, 1), :].astype(jnp.float32)
+        score_new = jnp.sum(spread.astype(jnp.float32) * key_new, axis=1, keepdims=True) * score_scale
+        positions = lax.broadcasted_iota(jnp.int32, scores.shape, 1)
+        live = positions < lengths_ref[request]
+        masked = jnp.where(live, scores, FLOOR)
+        largest = jnp.maximum(jnp.max(masked, axis=1, keepdims=True), score_new)
+        weights = jnp.where(live, jnp.exp(masked - largest), 0.0)
+        weight_new = jnp.exp(score_new - largest)
+        denoms = jnp.sum(weights, axis=1, keepdims=True) + weight_new
+        rounded_new = weight_new.astype(jnp.bfloat16).astype(jnp.float32)
+        totals = jnp.dot(weights.astype(jnp.bfloat16), values_v[request], preferred_element_type=jnp.float32)
+        totals = totals + rounded_new * new_values_ref[pl.ds(request, 1), :].astype(jnp.float32)
+        totals = totals / denoms
+        picked = jnp.zeros((heads, HD), jnp.float32)
+        for head in range(KVH):
+            picked = picked + jnp.where(head_group == head, totals[:, head * HD:(head + 1) * HD], 0.0)
+        out_ref[request] = picked.astype(out_ref.dtype)
+
+
 def attend_local(queries, new_keys, new_values, key_cache, value_cache, lengths):
     request_count = queries.shape[0]
     group_size = QH // KVH
-    score_scale = 1.0 / math.sqrt(HD)
     query_heads = queries.reshape(request_count, KVH, group_size, HD)
     head_eye = jnp.eye(KVH, dtype=queries.dtype)[None, :, None, :, None]
     spread_queries = (query_heads[:, :, :, None, :] * head_eye).reshape(request_count, QH, KVH * HD)
-    scores = (
-        jnp.einsum("rhc,rpc->rhp", spread_queries, key_cache, preferred_element_type=jnp.float32)
-        * score_scale
-    )
-    score_new = (
-        jnp.einsum("rhc,rc->rh", spread_queries, new_keys, preferred_element_type=jnp.float32)
-        * score_scale
-    )
-    positions = jnp.arange(key_cache.shape[1], dtype=jnp.int32)
-    live_mask = (positions[None, :] < lengths[:, None])[:, None, :]
-    masked = jnp.where(live_mask, scores, FLOOR)
-    largest = jnp.maximum(jnp.max(masked, axis=-1), score_new)
-    weights = jnp.where(live_mask, jnp.exp(masked - largest[..., None]), 0.0)
-    weight_new = jnp.exp(score_new - largest)
-    denoms = jnp.sum(weights, axis=-1) + weight_new
-    rounded_new = weight_new.astype(jnp.bfloat16).astype(jnp.float32)
-    spread_totals = jnp.einsum(
-        "rhp,rpc->rhc", weights.astype(jnp.bfloat16), value_cache, preferred_element_type=jnp.float32
-    ) + rounded_new[..., None] * new_values[:, None, :].astype(jnp.float32)
-    spread_totals = spread_totals / denoms[..., None]
-    totals = jnp.sum(
-        spread_totals.reshape(request_count, KVH, group_size, KVH, HD) * head_eye.astype(jnp.float32),
-        axis=3,
-    )
-    return totals.astype(jnp.bfloat16).reshape(request_count, QH * HD)
+    anywhere = pl.BlockSpec(memory_space=pl.ANY)
+    whole = pl.BlockSpec(memory_space=pltpu.VMEM)
+    attended = pl.pallas_call(
+        attend_kernel,
+        out_shape=jax.ShapeDtypeStruct((request_count, QH, HD), jnp.bfloat16),
+        in_specs=[pl.BlockSpec(memory_space=pltpu.SMEM), whole, whole, whole, anywhere, anywhere],
+        out_specs=whole,
+        scratch_shapes=[
+            pltpu.VMEM(key_cache.shape, key_cache.dtype),
+            pltpu.VMEM(value_cache.shape, value_cache.dtype),
+            pltpu.SemaphoreType.DMA((2, request_count)),
+        ],
+        compiler_params=pltpu.CompilerParams(vmem_limit_bytes=40 * 1024 * 1024),
+        cost_estimate=pl.CostEstimate(
+            flops=4 * request_count * QH * key_cache.shape[1] * key_cache.shape[2],
+            transcendentals=request_count * QH * key_cache.shape[1],
+            bytes_accessed=2 * (key_cache.size + value_cache.size),
+        ),
+    )(lengths, spread_queries, new_keys, new_values, key_cache, value_cache)
+    return attended.reshape(request_count, QH * HD)
 
 
 def local(

time: 123 us -> 126 us (1.024)
  local copies, waits for them, and re-layouts: 4.32 us -> 10.8 us
  matrix products: 7.53 us -> 1.76 us
  Pallas kernels: 6.62 us -> 10.9 us
  other arithmetic: 3.75 us -> 1.74 us
    unnamed x18 -> x26, local copies, waits for them, and re-layouts: 1.05 us -> 7.38 us
    dot_general x3 -> x0, matrix products: 5.77 us -> none  [the longest x1 3.86 us: attend_local(): jnp.einsum('rhc,rpc->rhp', spread_queries, key_cache, preferred_element_t...]
    pallas_call x0 -> x1, Pallas kernels: none -> 4.26 us  [attend_local(): pl.pallas_call(attend_kernel, out_shape=jax.ShapeDtypeStruct((request_cou...]
where the time goes in v8:
time: 126 us
  blocking collectives  73.1 us (58%)
  waiting for transfers between devices  15.9 us (13%)
  starting transfers between devices  11.1 us (9%)
  Pallas kernels  10.9 us (9%)
  local copies, waits for them, and re-layouts  10.8 us (9%)
  matrix products  1.76 us (1%)
  other arithmetic  1.74 us (1%)
    all_to_all x1, blocking collectives, local(): incoming = lax.all_to_all(outgoing, ('expert', 'ffn'), 0, 0, tiled=True)  39.1 us
    all_to_all x1, blocking collectives, local(): pieces = lax.all_to_all(partial_out, ('expert', 'ffn'), 0, 0, tiled=True)  34 us
    all_to_all x2, waiting for transfers between devices, gather_by_exchange(): return lax.all_to_all(copies, axis_name, 0, 0, tiled=True)  15.9 us
    all_to_all x2, starting transfers between devices, gather_by_exchange(): return lax.all_to_all(copies, axis_name, 0, 0, tiled=True)  11.1 us
    unnamed x26, local copies, waits for them, and re-layouts  7.38 us
    pallas_call x1, Pallas kernels, expert_block(): pl.pallas_call(expert_kernel, out_shape=jax.ShapeDtypeStruct(rows.shape,...  6.62 us
    pallas_call x1, Pallas kernels, attend_local(): pl.pallas_call(attend_kernel, out_shape=jax.ShapeDtypeStruct((request_cou...  4.26 us
  transfers between devices with their start and end apart: 2, of which 2 were waited for; matrix products, arithmetic and copies ran while one was open for 1% of the time, Pallas kernels for 0%

profile of v8, /device:TPU:1, one launch (start us, length us, event | category | flops | bytes accessed | tf_op | source)
XLA Modules:
  0.0 125.5 jit_solution(1107437060527760907)
XLA Ops:
  0.0 1.0 mul.60
  1.3 2.2 %copy-done.1 = bf16[4,512,1024]{2,1,0:T(8,128)(2,1)S(1)} copy-done((bf16[4,512,1024]{2,1,0:T(8,128)(2,1)S(1)}, bf16[4,512,1024]{2,1,0:T(8,128)(2,1)}, u32[]{:S(2)}) %copy-start.1) | copy-done | bytes 4194328
  3.5 2.2 %copy-done.2 = bf16[4,512,1024]{2,1,0:T(8,128)(2,1)S(1)} copy-done((bf16[4,512,1024]{2,1,0:T(8,128)(2,1)S(1)}, bf16[4,512,1024]{2,1,0:T(8,128)(2,1)}, u32[]{:S(2)}) %copy-start.2) | copy-done | bytes 4194328
  5.6 0.7 copy-done.3
  6.3 0.7 copy-done.4
  7.0 0.7 copy-done.5
  7.7 4.3 %shard_map.136 = bf16[4,32,128]{2,1,0:T(8,128)(2,1)S(1)} custom-call(s32[4]{0:T(128)S(1)} %copy-done.5, bf16[4,32,1024]{2,1,0:T(8,128)(2,1)S(1)} %broadcast_multiply_fusion.queries_ref, bf16[4,1024]{1,0:T(4,128)(2,1)S(1)} %copy-done.3, bf16[4,1024]{1,0:T(4,128)(2,1)S(1)} %copy-done.4, bf16[4,512,1024]{2,1,0:T(8,128)(2,1)S(1)} %copy-done.1, ...), custom_call_target="tpu_custom_call" | custom-call | flops 268435456 | bytes 8388608 | tf_op jit(solution)/shard_map/pallas_call | solution.py:146
  12.0 1.0 broadcast_in_dim.56
  13.0 7.6 %all-to-all-start = ((bf16[16,4,4096]{2,1,0:T(4,128)(2,1)}), bf16[16,4,4096]{2,1,0:T(4,128)(2,1)S(1)}, u32[]{:S(2)}, u32[]{:S(2)}) async-start(bf16[16,4,4096]{2,1,0:T(4,128)(2,1)} %broadcast_in_dim.56), calls=%async_computation | async-start | bytes 1048576 | tf_op jit(solution)/shard_map/all_to_all | solution.py:34
  20.9 0.2 reduce_window_sum.11
  21.5 9.4 %all-to-all-done = bf16[16,4,4096]{2,1,0:T(4,128)(2,1)S(1)} async-done(((bf16[16,4,4096]{2,1,0:T(4,128)(2,1)}), bf16[16,4,4096]{2,1,0:T(4,128)(2,1)S(1)}, u32[]{:S(2)}, u32[]{:S(2)}) %all-to-all-start) | async-done | bytes 524320 | tf_op jit(solution)/shard_map/all_to_all | solution.py:34
  31.1 0.6 multiply_reduce_fusion
  31.9 0.7 reshape.51
  32.6 3.5 %all-to-all-start.1 = ((f32[16,1,576]{2,1,0:T(1,128)}), f32[16,1,576]{2,1,0:T(1,128)S(1)}, u32[]{:S(2)}, u32[]{:S(2)}) async-start(f32[16,1,576]{2,1,0:T(1,128)} %reshape.51), calls=%async_computation.1 | async-start | bytes 81920 | tf_op jit(solution)/shard_map/all_to_all | solution.py:34
  36.1 6.5 %all-to-all-done.1 = f32[16,1,576]{2,1,0:T(1,128)S(1)} async-done(((f32[16,1,576]{2,1,0:T(1,128)}), f32[16,1,576]{2,1,0:T(1,128)S(1)}, u32[]{:S(2)}, u32[]{:S(2)}) %all-to-all-start.1) | async-done | bytes 36896 | tf_op jit(solution)/shard_map/all_to_all | solution.py:34
  42.5 0.5 broadcast.28
  43.1 0.7 reduce.1
  44.1 0.2 convolution_convert_fusion
  44.3 0.3 broadcast_in_dim.64
  44.6 39.1 %all_to_all.20 = bf16[128,32,256]{2,1,0:T(8,128)(2,1)S(1)} all-to-all(bf16[128,32,256]{2,1,0:T(8,128)(2,1)S(1)} %bitcast.37), channel_id=1, replica_groups=mesh['expert'=8,'ffn'=16] {'expert','ffn'}, dimensions={0} | all-to-all | bytes 4194304 | tf_op jit(solution)/shard_map/all_to_all | solution.py:227
  83.7 6.6 %shard_map.137 = bf16[8,16,32,256]{3,2,1,0:T(8,128)(2,1)S(1)} custom-call(bf16[8,16,32,256]{3,2,1,0:T(8,128)(2,1)S(1)} %bitcast.34, bf16[4096,512]{1,0:T(8,128)(2,1)} %bitcast.38, bf16[4096,512]{1,0:T(8,128)(2,1)} %bitcast.39, bf16[512,4096]{1,0:T(8,128)(2,1)} %bitcast.40), custom_call_target="tpu_custom_call" | custom-call | flops 3221225472 | bytes 16777216 | tf_op jit(solution)/shard_map/pallas_call | solution.py:75
  90.3 34.0 %all_to_all.21 = bf16[128,32,256]{2,1,0:T(8,128)(2,1)S(1)} all-to-all(bf16[128,32,256]{2,1,0:T(8,128)(2,1)S(1)} %bitcast.35), channel_id=1, replica_groups=mesh['expert'=8,'ffn'=16] {'expert','ffn'}, dimensions={0} | all-to-all | bytes 4194304 | tf_op jit(solution)/shard_map/all_to_all | solution.py:231
  124.3 0.3 bitcast_reduce_fusion
  124.7 0.8 fusion
  (41 shorter events, 1.6 us)
Async XLA Ops:
  0.0 31.1 %copy-start = (bf16[4096,256]{1,0:T(8,128)(2,1)S(1)}, bf16[4096,256]{1,0:T(8,128)(2,1)}, u32[]{:S(2)}) copy-start(bf16[4096,256]{1,0:T(8,128)(2,1)} %param.21) | copy-start | bytes 6291460
  1.3 2.2 %copy-start.1 = (bf16[4,512,1024]{2,1,0:T(8,128)(2,1)S(1)}, bf16[4,512,1024]{2,1,0:T(8,128)(2,1)}, u32[]{:S(2)}) copy-start(bf16[4,512,1024]{2,1,0:T(8,128)(2,1)} %keys_hbm.1) | copy-start | bytes 12582916
  3.5 2.2 %copy-start.2 = (bf16[4,512,1024]{2,1,0:T(8,128)(2,1)S(1)}, bf16[4,512,1024]{2,1,0:T(8,128)(2,1)}, u32[]{:S(2)}) copy-start(bf16[4,512,1024]{2,1,0:T(8,128)(2,1)} %values_hbm.1) | copy-start | bytes 12582916
  5.6 0.7 copy-start.3
  6.3 0.7 copy-start.4
  7.0 0.7 copy-start.5
  7.7 12.9 %copy-start.7 = (s32[64,2]{0,1:T(2,128)S(1)}, s32[64,2]{0,1:T(2,128)}, u32[]{:S(2)}) copy-start(s32[64,2]{0,1:T(2,128)} %param.27) | copy-start | bytes 1540
  12.0 19.1 %copy-start.6 = (bf16[64,256]{1,0:T(8,128)(2,1)S(1)}, bf16[64,256]{1,0:T(8,128)(2,1)}, u32[]{:S(2)}) copy-start(bf16[64,256]{1,0:T(8,128)(2,1)} %param.20) | copy-start | bytes 98308
  13.0 17.9 %all-to-all-start = ((bf16[16,4,4096]{2,1,0:T(4,128)(2,1)}), bf16[16,4,4096]{2,1,0:T(4,128)(2,1)S(1)}, u32[]{:S(2)}, u32[]{:S(2)}) async-start(bf16[16,4,4096]{2,1,0:T(4,128)(2,1)} %broadcast_in_dim.56), calls=%async_computation | async-start | bytes 1048576 | tf_op jit(solution)/shard_map/all_to_all | solution.py:34
  20.6 11.1 %copy-start.8 = (f32[256,8]{0,1:T(8,128)S(1)}, f32[256,8]{0,1:T(8,128)}, u32[]{:S(2)}) copy-start(f32[256,8]{0,1:T(8,128)} %param.23) | copy-start | bytes 24580
  20.6 11.1 %copy-start.9 = (f32[256]{0:T(256)S(1)}, f32[256]{0:T(256)}, u32[]{:S(2)}) copy-start(f32[256]{0:T(256)} %param.22) | copy-start | bytes 3076
  32.6 10.0 %all-to-all-start.1 = ((f32[16,1,576]{2,1,0:T(1,128)}), f32[16,1,576]{2,1,0:T(1,128)S(1)}, u32[]{:S(2)}, u32[]{:S(2)}) async-start(f32[16,1,576]{2,1,0:T(1,128)} %reshape.51), calls=%async_computation.1 | async-start | bytes 81920 | tf_op jit(solution)/shard_map/all_to_all | solution.py:34

commit v9 on v7

--- a/solution.py
+++ b/solution.py
@@ -71,7 +71,7 @@
     groups, blocks, capacity, width = rows.shape
     hidden_units = gate_local.shape[1]
     row_count = groups * capacity
-    anywhere = pl.BlockSpec(memory_space=pl.ANY)
+    anywhere = pl.BlockSpec(memory_space=pltpu.HBM)
     return pl.pallas_call(
         expert_kernel,
         out_shape=jax.ShapeDtypeStruct(rows.shape, jnp.bfloat16),
@@ -93,38 +93,67 @@
     )(rows, gate_local, up_local, down_local)
 
 
+def attend_kernel(length_ref, spread_ref, key_new_ref, value_new_ref, keys_ref, values_ref, out_ref):
+    heads = spread_ref.shape[0]
+    group_size = heads // KVH
+    score_scale = 1.0 / math.sqrt(HD)
+    head_group = lax.broadcasted_iota(jnp.int32, (heads, 1), 0) // group_size
+    spread = spread_ref[...]
+    scores = lax.dot_general(
+        spread, keys_ref[...], (((1,), (1,)), ((), ())), preferred_element_type=jnp.float32
+    ) * score_scale
+    key_new = key_new_ref[...].astype(jnp.float32)
+    score_new = jnp.sum(spread.astype(jnp.float32) * key_new, axis=1, keepdims=True) * score_scale
+    positions = lax.broadcasted_iota(jnp.int32, scores.shape, 1)
+    live = positions < length_ref[0]
+    masked = jnp.where(live, scores, FLOOR)
+    largest = jnp.maximum(jnp.max(masked, axis=1, keepdims=True), score_new)
+    weights = jnp.where(live, jnp.exp(masked - largest), 0.0)
+    weight_new = jnp.exp(score_new - largest)
+    denoms = jnp.sum(weights, axis=1, keepdims=True) + weight_new
+    rounded_new = weight_new.astype(jnp.bfloat16).astype(jnp.float32)
+    totals = jnp.dot(weights.astype(jnp.bfloat16), values_ref[...], preferred_element_type=jnp.float32)
+    totals = totals + rounded_new * value_new_ref[...].astype(jnp.float32)
+    totals = totals / denoms
+    picked = jnp.zeros((heads, HD), jnp.float32)
+    for head in range(KVH):
+        picked = picked + jnp.where(head_group == head, totals[:, head * HD:(head + 1) * HD], 0.0)
+    out_ref[...] = picked.astype(out_ref.dtype)
+
+
+def attend_one(length, spread, key_new, value_new, keys, values):
+    whole = pl.BlockSpec(memory_space=pltpu.VMEM)
+    return pl.pallas_call(
+        attend_kernel,
+        out_shape=jax.ShapeDtypeStruct((spread.shape[0], HD), jnp.bfloat16),
+        in_specs=[pl.BlockSpec(memory_space=pltpu.SMEM), whole, whole, whole, whole, whole],
+        out_specs=whole,
+        cost_estimate=pl.CostEstimate(
+            flops=4 * spread.shape[0] * keys.shape[0] * keys.shape[1],
+            transcendentals=spread.shape[0] * keys.shape[0],
+            bytes_accessed=2 * (keys.size + values.size),
+        ),
+    )(length, spread, key_new, value_new, keys, values)
+
+
 def attend_local(queries, new_keys, new_values, key_cache, value_cache, lengths):
     request_count = queries.shape[0]
     group_size = QH // KVH
-    score_scale = 1.0 / math.sqrt(HD)
     query_heads = queries.reshape(request_count, KVH, group_size, HD)
     head_eye = jnp.eye(KVH, dtype=queries.dtype)[None, :, None, :, None]
     spread_queries = (query_heads[:, :, :, None, :] * head_eye).reshape(request_count, QH, KVH * HD)
-    scores = (
-        jnp.einsum("rhc,rpc->rhp", spread_queries, key_cache, preferred_element_type=jnp.float32)
-        * score_scale
-    )
-    score_new = (
-        jnp.einsum("rhc,rc->rh", spread_queries, new_keys, preferred_element_type=jnp.float32)
-        * score_scale
-    )
-    positions = jnp.arange(key_cache.shape[1], dtype=jnp.int32)
-    live_mask = (positions[None, :] < lengths[:, None])[:, None, :]
-    masked = jnp.where(live_mask, scores, FLOOR)
-    largest = jnp.maximum(jnp.max(masked, axis=-1), score_new)
-    weights = jnp.where(live_mask, jnp.exp(masked - largest[..., None]), 0.0)
-    weight_new = jnp.exp(score_new - largest)
-    denoms = jnp.sum(weights, axis=-1) + weight_new
-    rounded_new = weight_new.astype(jnp.bfloat16).astype(jnp.float32)
-    spread_totals = jnp.einsum(
-        "rhp,rpc->rhc", weights.astype(jnp.bfloat16), value_cache, preferred_element_type=jnp.float32
-    ) + rounded_new[..., None] * new_values[:, None, :].astype(jnp.float32)
-    spread_totals = spread_totals / denoms[..., None]
-    totals = jnp.sum(
-        spread_totals.reshape(request_count, KVH, group_size, KVH, HD) * head_eye.astype(jnp.float32),
-        axis=3,
-    )
-    return totals.astype(jnp.bfloat16).reshape(request_count, QH * HD)
+    rows = [
+        attend_one(
+            lengths[request:request + 1],
+            spread_queries[request],
+            new_keys[request:request + 1],
+            new_values[request:request + 1],
+            key_cache[request],
+            value_cache[request],
+        )
+        for request in range(request_count)
+    ]
+    return jnp.stack(rows).reshape(request_count, QH * HD)
 
 
 def local(

time: 123 us -> 144 us (1.17)
  Pallas kernels: 6.62 us -> 20.8 us
  local copies, waits for them, and re-layouts: 4.32 us -> 18.4 us
  matrix products: 7.53 us -> 1.76 us
  other arithmetic: 3.75 us -> 1.89 us
    pallas_call x0 -> x4, Pallas kernels: none -> 14.2 us  [attend_one(): pl.pallas_call(attend_kernel, out_shape=jax.ShapeDtypeStruct((spread.shap...]
    squeeze x0 -> x1, local copies, waits for them, and re-layouts: none -> 6.09 us  [attend_local(): value_cache[request]]
    dot_general x3 -> x0, matrix products: 5.77 us -> none  [the longest x1 3.86 us: attend_local(): jnp.einsum('rhc,rpc->rhp', spread_queries, key_cache, preferred_element_t...]
    slice x0 -> x3, local copies, waits for them, and re-layouts: none -> 3.02 us  [the longest x1 1.52 us: attend_local(): lengths[request:request + 1]]
    another operation x0 -> x4, local copies, waits for them, and re-layouts: none -> 2.85 us  [attend_local(): return jnp.stack(rows).reshape(request_count, QH * HD)]
    unnamed x18, local copies, waits for them, and re-layouts: 1.05 us -> 3.47 us
where the time goes in v9:
time: 144 us; the launch traced here: 143 us
  blocking collectives  73.1 us (51%)
  Pallas kernels  20.8 us (14%)
  local copies, waits for them, and re-layouts  18.4 us (13%)
  waiting for transfers between devices  15.9 us (11%)
  starting transfers between devices  11.1 us (8%)
  other arithmetic  1.89 us (1%)
  matrix products  1.76 us (1%)
    all_to_all x1, blocking collectives, local(): incoming = lax.all_to_all(outgoing, ('expert', 'ffn'), 0, 0, tiled=True)  39.1 us
    all_to_all x1, blocking collectives, local(): pieces = lax.all_to_all(partial_out, ('expert', 'ffn'), 0, 0, tiled=True)  34 us
    all_to_all x2, waiting for transfers between devices, gather_by_exchange(): return lax.all_to_all(copies, axis_name, 0, 0, tiled=True)  15.9 us
    pallas_call x4, Pallas kernels, attend_one(): pl.pallas_call(attend_kernel, out_shape=jax.ShapeDtypeStruct((spread.shap...  14.2 us
    all_to_all x2, starting transfers between devices, gather_by_exchange(): return lax.all_to_all(copies, axis_name, 0, 0, tiled=True)  11.1 us
    pallas_call x1, Pallas kernels, expert_block(): pl.pallas_call(expert_kernel, out_shape=jax.ShapeDtypeStruct(rows.shape,...  6.62 us
    squeeze x1, local copies, waits for them, and re-layouts, attend_local(): value_cache[request]  6.09 us
    unnamed x18, local copies, waits for them, and re-layouts  3.47 us
  transfers between devices with their start and end apart: 2, of which 2 were waited for; matrix products, arithmetic and copies ran while one was open for 1% of the time, Pallas kernels for 0%

profile of v9, /device:TPU:1, one launch (start us, length us, event | category | flops | bytes accessed | tf_op | source)
XLA Modules:
  0.0 143.2 jit_solution(14753213183637643854)
XLA Ops:
  0.0 1.5 %fusion.15 = (s32[1]{0:T(128)}, s32[1]{0:T(128)}, s32[1]{0:T(128)}, s32[1]{0:T(128)}) fusion(s32[4]{0:T(128)} %param.19), kind=kLoop, calls=%fused_computation.50 | loop fusion | bytes 32 | tf_op jit(solution)/shard_map/slice | solution.py:147
  1.5 0.8 mul.53
  3.1 1.5 %fusion.13 = (bf16[1,1024]{1,0:T(2,128)(2,1)}, bf16[1,1024]{1,0:T(2,128)(2,1)}, bf16[1,1024]{1,0:T(2,128)(2,1)}, bf16[1,1024]{1,0:T(2,128)(2,1)}, bf16[1,1024]{1...) fusion(bf16[4,1024]{1,0:T(4,128)(2,1)} %param.16, ...), kind=kLoop, calls=%fused_computation.48 | loop fusion | bytes 32768 | tf_op jit(solution)/shard_map/slice | solution.py:150
  4.6 6.1 %slice_bitcast_fusion.6 = (bf16[512,1024]{1,0:T(8,128)(2,1)}, bf16[512,1024]{1,0:T(8,128)(2,1)}, bf16[512,1024]{1,0:T(8,128)(2,1)}, bf16[512,1024]{1,0:T(8,128)(...) fusion(bf16[4,512,1024]{2,1,0:T(8,128)(2,1)} %param.18, ...), kind=kLoop, calls=%fused_computation.11 | loop fusion | bytes 16777216 | tf_op jit(solution)/shard_map/squeeze | solution.py:152
  10.7 3.5 %shard_map.139 = bf16[32,128]{1,0:T(8,128)(2,1)} custom-call(s32[1]{0:T(128)} %get-tuple-element.31.length_ref, bf16[32,1024]{1,0:T(8,128)(2,1)} %bitcast.69, bf16[1,1024]{1,0:T(2,128)(2,1)} %get-tuple-element.40.key_new_ref, bf16[1,1024]{1,0:T(2,128)(2,1)} %get-tuple-element.23.value_new_ref, bf16[512,1024]{1,0:T(8,128)(2,1)} %get-tuple-element.36.keys_ref, ...), custom_call_target="tpu_custom_call" | custom-call | flops 67108864 | bytes 2097152 | tf_op jit(solution)/shard_map/pallas_call | solution.py:126
  14.2 0.7 stack.23
  15.5 3.6 %shard_map.138 = bf16[32,128]{1,0:T(8,128)(2,1)} custom-call(s32[1]{0:T(128)} %get-tuple-element.32.length_ref, bf16[32,1024]{1,0:T(8,128)(2,1)} %bitcast.71, bf16[1,1024]{1,0:T(2,128)(2,1)} %get-tuple-element.39.key_new_ref, bf16[1,1024]{1,0:T(2,128)(2,1)} %get-tuple-element.24.value_new_ref, bf16[512,1024]{1,0:T(8,128)(2,1)} %get-tuple-element.35.keys_ref, ...), custom_call_target="tpu_custom_call" | custom-call | flops 67108864 | bytes 2097152 | tf_op jit(solution)/shard_map/pallas_call | solution.py:126
  19.1 0.7 stack.22
  19.8 0.6 copy.49
  20.4 3.6 %shard_map.137 = bf16[32,128]{1,0:T(8,128)(2,1)} custom-call(s32[1]{0:T(128)} %get-tuple-element.30.length_ref, bf16[32,1024]{1,0:T(8,128)(2,1)} %bitcast.72, bf16[1,1024]{1,0:T(2,128)(2,1)} %get-tuple-element.41.key_new_ref, bf16[1,1024]{1,0:T(2,128)(2,1)} %get-tuple-element.22.value_new_ref, bf16[512,1024]{1,0:T(8,128)(2,1)} %get-tuple-element.37.keys_ref, ...), custom_call_target="tpu_custom_call" | custom-call | flops 67108864 | bytes 2097152 | tf_op jit(solution)/shard_map/pallas_call | solution.py:126
  24.0 0.7 stack.21
  25.4 3.5 %shard_map.136 = bf16[32,128]{1,0:T(8,128)(2,1)} custom-call(s32[1]{0:T(128)} %get-tuple-element.29.length_ref, bf16[32,1024]{1,0:T(8,128)(2,1)} %bitcast.70, bf16[1,1024]{1,0:T(2,128)(2,1)} %get-tuple-element.42.key_new_ref, bf16[1,1024]{1,0:T(2,128)(2,1)} %get-tuple-element.21.value_new_ref, bf16[512,1024]{1,0:T(8,128)(2,1)} %get-tuple-element.38.keys_ref, ...), custom_call_target="tpu_custom_call" | custom-call | flops 67108864 | bytes 2097152 | tf_op jit(solution)/shard_map/pallas_call | solution.py:126
  28.9 0.7 stack.20
  29.7 1.0 broadcast_in_dim.56
  30.7 7.6 %all-to-all-start = ((bf16[16,4,4096]{2,1,0:T(4,128)(2,1)}), bf16[16,4,4096]{2,1,0:T(4,128)(2,1)S(1)}, u32[]{:S(2)}, u32[]{:S(2)}) async-start(bf16[16,4,4096]{2,1,0:T(4,128)(2,1)} %broadcast_in_dim.56), calls=%async_computation | async-start | bytes 1048576 | tf_op jit(solution)/shard_map/all_to_all | solution.py:34
  39.2 9.4 %all-to-all-done = bf16[16,4,4096]{2,1,0:T(4,128)(2,1)S(1)} async-done(((bf16[16,4,4096]{2,1,0:T(4,128)(2,1)}), bf16[16,4,4096]{2,1,0:T(4,128)(2,1)S(1)}, u32[]{:S(2)}, u32[]{:S(2)}) %all-to-all-start) | async-done | bytes 524320 | tf_op jit(solution)/shard_map/all_to_all | solution.py:34
  49.5 0.7 reshape.64
  50.3 3.5 %all-to-all-start.1 = ((f32[16,1,576]{2,1,0:T(1,128)}), f32[16,1,576]{2,1,0:T(1,128)S(1)}, u32[]{:S(2)}, u32[]{:S(2)}) async-start(f32[16,1,576]{2,1,0:T(1,128)} %reshape.64), calls=%async_computation.1 | async-start | bytes 81920 | tf_op jit(solution)/shard_map/all_to_all | solution.py:34
  53.8 6.5 %all-to-all-done.1 = f32[16,1,576]{2,1,0:T(1,128)S(1)} async-done(((f32[16,1,576]{2,1,0:T(1,128)}), f32[16,1,576]{2,1,0:T(1,128)S(1)}, u32[]{:S(2)}, u32[]{:S(2)}) %all-to-all-start.1) | async-done | bytes 36896 | tf_op jit(solution)/shard_map/all_to_all | solution.py:34
  60.8 0.7 reduce.1
  62.3 39.1 %all_to_all.20 = bf16[128,32,256]{2,1,0:T(8,128)(2,1)S(1)} all-to-all(bf16[128,32,256]{2,1,0:T(8,128)(2,1)S(1)} %bitcast.63), channel_id=1, replica_groups=mesh['expert'=8,'ffn'=16] {'expert','ffn'}, dimensions={0} | all-to-all | bytes 4194304 | tf_op jit(solution)/shard_map/all_to_all | solution.py:220
  101.3 6.6 %shard_map.140 = bf16[8,16,32,256]{3,2,1,0:T(8,128)(2,1)S(1)} custom-call(bf16[8,16,32,256]{3,2,1,0:T(8,128)(2,1)S(1)} %bitcast.61, bf16[4096,512]{1,0:T(8,128)(2,1)} %bitcast.64, bf16[4096,512]{1,0:T(8,128)(2,1)} %bitcast.65, bf16[512,4096]{1,0:T(8,128)(2,1)} %bitcast.66), custom_call_target="tpu_custom_call" | custom-call | flops 3221225472 | bytes 16777216 | tf_op jit(solution)/shard_map/pallas_call | solution.py:75
  108.0 34.0 %all_to_all.21 = bf16[128,32,256]{2,1,0:T(8,128)(2,1)S(1)} all-to-all(bf16[128,32,256]{2,1,0:T(8,128)(2,1)S(1)} %bitcast.62), channel_id=1, replica_groups=mesh['expert'=8,'ffn'=16] {'expert','ffn'}, dimensions={0} | all-to-all | bytes 4194304 | tf_op jit(solution)/shard_map/all_to_all | solution.py:224
  142.4 0.8 fusion
  (42 shorter events, 5.5 us)
Async XLA Ops:
  0.0 48.8 %copy-start = (bf16[4096,256]{1,0:T(8,128)(2,1)S(1)}, bf16[4096,256]{1,0:T(8,128)(2,1)}, u32[]{:S(2)}) copy-start(bf16[4096,256]{1,0:T(8,128)(2,1)} %param.21) | copy-start | bytes 6291460
  24.0 14.2 %copy-start.2 = (s32[64,2]{0,1:T(2,128)S(1)}, s32[64,2]{0,1:T(2,128)}, u32[]{:S(2)}) copy-start(s32[64,2]{0,1:T(2,128)} %param.27) | copy-start | bytes 1540
  28.9 19.9 %copy-start.1 = (bf16[64,256]{1,0:T(8,128)(2,1)S(1)}, bf16[64,256]{1,0:T(8,128)(2,1)}, u32[]{:S(2)}) copy-start(bf16[64,256]{1,0:T(8,128)(2,1)} %param.20) | copy-start | bytes 98308
  30.7 17.9 %all-to-all-start = ((bf16[16,4,4096]{2,1,0:T(4,128)(2,1)}), bf16[16,4,4096]{2,1,0:T(4,128)(2,1)S(1)}, u32[]{:S(2)}, u32[]{:S(2)}) async-start(bf16[16,4,4096]{2,1,0:T(4,128)(2,1)} %broadcast_in_dim.56), calls=%async_computation | async-start | bytes 1048576 | tf_op jit(solution)/shard_map/all_to_all | solution.py:34
  38.3 11.1 %copy-start.3 = (f32[256,8]{0,1:T(8,128)S(1)}, f32[256,8]{0,1:T(8,128)}, u32[]{:S(2)}) copy-start(f32[256,8]{0,1:T(8,128)} %param.23) | copy-start | bytes 24580
  38.3 11.1 %copy-start.4 = (f32[256]{0:T(256)S(1)}, f32[256]{0:T(256)}, u32[]{:S(2)}) copy-start(f32[256]{0:T(256)} %param.22) | copy-start | bytes 3076
  50.3 10.0 %all-to-all-start.1 = ((f32[16,1,576]{2,1,0:T(1,128)}), f32[16,1,576]{2,1,0:T(1,128)S(1)}, u32[]{:S(2)}, u32[]{:S(2)}) async-start(f32[16,1,576]{2,1,0:T(1,128)} %reshape.64), calls=%async_computation.1 | async-start | bytes 81920 | tf_op jit(solution)/shard_map/all_to_all | solution.py:34

commit v10 on v7

--- a/solution.py
+++ b/solution.py
@@ -49,8 +49,12 @@
         for copy in trio:
             copy.start()
         copies.append(trio)
-    down_copy = pltpu.make_async_copy(down_hbm, down_v, sems.at[3, 0])
-    down_copy.start()
+    down_copies = []
+    for block in range(blocks):
+        span = pl.ds(block * width, width)
+        copy = pltpu.make_async_copy(down_hbm.at[:, span], down_v.at[:, span], sems.at[3, block])
+        copy.start()
+        down_copies.append(copy)
     gate_sum = jnp.zeros((row_count, hidden_units), jnp.float32)
     up_sum = jnp.zeros((row_count, hidden_units), jnp.float32)
     for block in range(blocks):
@@ -61,8 +65,8 @@
         gate_sum += jnp.dot(rows, gate_v[span, :], preferred_element_type=jnp.float32)
         up_sum += jnp.dot(rows, up_v[span, :], preferred_element_type=jnp.float32)
     inner = (gate_sum / (1.0 + jnp.exp(-gate_sum)) * up_sum).astype(jnp.bfloat16)
-    down_copy.wait()
-    for block in range(blocks):
+    for block in range(blocks):
+        down_copies[block].wait()
         part = jnp.dot(inner, down_v[:, pl.ds(block * width, width)], preferred_element_type=jnp.float32)
         out_ref[:, block] = part.astype(out_ref.dtype).reshape(groups, capacity, width)
 

time: 123 us -> 126 us (1.024)
  Pallas kernels: 6.62 us -> 9.53 us
    pallas_call x1, Pallas kernels: 6.62 us -> 9.53 us  [expert_block(): pl.pallas_call(expert_kernel, out_shape=jax.ShapeDtypeStruct(rows.shape,...]
where the time goes in v10:
time: 126 us; the launch traced here: 125 us
  blocking collectives  73.1 us (58%)
  waiting for transfers between devices  15.9 us (13%)
  starting transfers between devices  11.1 us (9%)
  Pallas kernels  9.53 us (8%)
  matrix products  7.53 us (6%)
  local copies, waits for them, and re-layouts  4.32 us (3%)
  other arithmetic  3.75 us (3%)
    all_to_all x1, blocking collectives, local(): incoming = lax.all_to_all(outgoing, ('expert', 'ffn'), 0, 0, tiled=True)  39.1 us
    all_to_all x1, blocking collectives, local(): pieces = lax.all_to_all(partial_out, ('expert', 'ffn'), 0, 0, tiled=True)  34 us
    all_to_all x2, waiting for transfers between devices, gather_by_exchange(): return lax.all_to_all(copies, axis_name, 0, 0, tiled=True)  15.9 us
    all_to_all x2, starting transfers between devices, gather_by_exchange(): return lax.all_to_all(copies, axis_name, 0, 0, tiled=True)  11.1 us
    pallas_call x1, Pallas kernels, expert_block(): pl.pallas_call(expert_kernel, out_shape=jax.ShapeDtypeStruct(rows.shape,...  9.53 us
    dot_general x1, matrix products, attend_local(): jnp.einsum('rhc,rpc->rhp', spread_queries, key_cache, preferred_element_t...  3.86 us
  transfers between devices with their start and end apart: 2, of which 2 were waited for; matrix products, arithmetic and copies ran while one was open for 1% of the time, Pallas kernels for 0%

profile of v10, /device:TPU:1, one launch (start us, length us, event | category | flops | bytes accessed | tf_op | source)
XLA Modules:
  0.0 125.5 jit_solution(16241798308245280909)
XLA Ops:
  0.0 0.9 iota_compare_fusion.3
  0.9 0.7 convert_element_type.73
  1.6 0.8 mul.93
  2.7 1.0 fusion.3
  3.7 3.9 %fusion.29 = (f32[4,32]{1,0:T(4,128)S(1)}, f32[4,32,512]{2,1,0:T(8,128)S(1)}) fusion(bf16[4,512,1024]{2,1,0:T(8,128)(2,1)} %param.17, bf16[4,32,1024]{2,1,0:T(8,128)(2,1)S(1)} %mul.95, bf16[32,1024]{1,0:T(8,128)(2,1)S(1)} %bitcast.50, pred[4,512]{1,0:T(4,128)(4,1)S(1)} %iota_compare_fusion.3), kind=kOutput, calls=%fused_computation.58 | convolution fusion | flops 134545280 | bytes 4786688 | tf_op jit(solution)/shard_map/rhc,rpc->rhp/dot_general | solution.py:108
  7.6 0.2 fusion.6
  7.8 0.9 fusion
  8.8 0.2 multiply_reduce_fusion
  9.1 1.0 broadcast_in_dim.81
  10.1 7.6 %all-to-all-start = ((bf16[16,4,4096]{2,1,0:T(4,128)(2,1)}), bf16[16,4,4096]{2,1,0:T(4,128)(2,1)S(1)}, u32[]{:S(2)}, u32[]{:S(2)}) async-start(bf16[16,4,4096]{2,1,0:T(4,128)(2,1)} %broadcast_in_dim.81), calls=%async_computation | async-start | bytes 1048576 | tf_op jit(solution)/shard_map/all_to_all | solution.py:34
  18.6 9.5 %all-to-all-done = bf16[16,4,4096]{2,1,0:T(4,128)(2,1)S(1)} async-done(((bf16[16,4,4096]{2,1,0:T(4,128)(2,1)}), bf16[16,4,4096]{2,1,0:T(4,128)(2,1)S(1)}, u32[]{:S(2)}, u32[]{:S(2)}) %all-to-all-start) | async-done | bytes 524320 | tf_op jit(solution)/shard_map/all_to_all | solution.py:34
  28.2 0.6 multiply_reduce_fusion.1
  29.0 0.7 reshape.90
  29.7 3.5 %all-to-all-start.1 = ((f32[16,1,576]{2,1,0:T(1,128)}), f32[16,1,576]{2,1,0:T(1,128)S(1)}, u32[]{:S(2)}, u32[]{:S(2)}) async-start(f32[16,1,576]{2,1,0:T(1,128)} %reshape.90), calls=%async_computation.1 | async-start | bytes 81920 | tf_op jit(solution)/shard_map/all_to_all | solution.py:34
  33.2 6.5 %all-to-all-done.1 = f32[16,1,576]{2,1,0:T(1,128)S(1)} async-done(((f32[16,1,576]{2,1,0:T(1,128)}), f32[16,1,576]{2,1,0:T(1,128)S(1)}, u32[]{:S(2)}, u32[]{:S(2)}) %all-to-all-start.1) | async-done | bytes 36896 | tf_op jit(solution)/shard_map/all_to_all | solution.py:34
  39.7 0.5 broadcast.41
  40.2 0.7 reduce.1
  41.2 0.2 convolution_convert_fusion
  41.4 0.3 broadcast_in_dim.89
  41.7 39.1 %all_to_all.20 = bf16[128,32,256]{2,1,0:T(8,128)(2,1)S(1)} all-to-all(bf16[128,32,256]{2,1,0:T(8,128)(2,1)S(1)} %bitcast.41), channel_id=1, replica_groups=mesh['expert'=8,'ffn'=16] {'expert','ffn'}, dimensions={0} | all-to-all | bytes 4194304 | tf_op jit(solution)/shard_map/all_to_all | solution.py:195
  80.8 9.5 %shard_map.136 = bf16[8,16,32,256]{3,2,1,0:T(8,128)(2,1)S(1)} custom-call(bf16[8,16,32,256]{3,2,1,0:T(8,128)(2,1)S(1)} %bitcast.39, bf16[4096,512]{1,0:T(8,128)(2,1)} %bitcast.42, bf16[4096,512]{1,0:T(8,128)(2,1)} %bitcast.43, bf16[512,4096]{1,0:T(8,128)(2,1)} %bitcast.44), custom_call_target="tpu_custom_call" | custom-call | flops 3221225472 | bytes 16777216 | tf_op jit(solution)/shard_map/pallas_call | solution.py:79
  90.3 34.0 %all_to_all.21 = bf16[128,32,256]{2,1,0:T(8,128)(2,1)S(1)} all-to-all(bf16[128,32,256]{2,1,0:T(8,128)(2,1)S(1)} %bitcast.40), channel_id=1, replica_groups=mesh['expert'=8,'ffn'=16] {'expert','ffn'}, dimensions={0} | all-to-all | bytes 4194304 | tf_op jit(solution)/shard_map/all_to_all | solution.py:199
  124.3 0.3 bitcast_reduce_fusion
  124.7 0.8 fusion.2
  (42 shorter events, 1.9 us)
Async XLA Ops:
  0.0 28.2 %copy-start = (bf16[4096,256]{1,0:T(8,128)(2,1)S(1)}, bf16[4096,256]{1,0:T(8,128)(2,1)}, u32[]{:S(2)}) copy-start(bf16[4096,256]{1,0:T(8,128)(2,1)} %param.21) | copy-start | bytes 6291460
  2.7 5.1 %copy-start.1 = (bf16[4,512,1024]{2,1,0:T(8,128)(2,1)S(1)}, bf16[4,512,1024]{2,1,0:T(8,128)(2,1)}, u32[]{:S(2)}) copy-start(bf16[4,512,1024]{2,1,0:T(8,128)(2,1)} %param.18) | copy-start | bytes 12582916
  7.8 9.9 %copy-start.3 = (s32[64,2]{0,1:T(2,128)S(1)}, s32[64,2]{0,1:T(2,128)}, u32[]{:S(2)}) copy-start(s32[64,2]{0,1:T(2,128)} %param.27) | copy-start | bytes 1540
  7.8 20.4 %copy-start.2 = (bf16[64,256]{1,0:T(8,128)(2,1)S(1)}, bf16[64,256]{1,0:T(8,128)(2,1)}, u32[]{:S(2)}) copy-start(bf16[64,256]{1,0:T(8,128)(2,1)} %param.20) | copy-start | bytes 98308
  8.7 20.0 %copy-start.4 = (f32[256,8]{0,1:T(8,128)S(1)}, f32[256,8]{0,1:T(8,128)}, u32[]{:S(2)}) copy-start(f32[256,8]{0,1:T(8,128)} %param.23) | copy-start | bytes 24580
  8.7 20.0 %copy-start.5 = (f32[256]{0:T(256)S(1)}, f32[256]{0:T(256)}, u32[]{:S(2)}) copy-start(f32[256]{0:T(256)} %param.22) | copy-start | bytes 3076
  10.1 17.9 %all-to-all-start = ((bf16[16,4,4096]{2,1,0:T(4,128)(2,1)}), bf16[16,4,4096]{2,1,0:T(4,128)(2,1)S(1)}, u32[]{:S(2)}, u32[]{:S(2)}) async-start(bf16[16,4,4096]{2,1,0:T(4,128)(2,1)} %broadcast_in_dim.81), calls=%async_computation | async-start | bytes 1048576 | tf_op jit(solution)/shard_map/all_to_all | solution.py:34
  29.7 10.0 %all-to-all-start.1 = ((f32[16,1,576]{2,1,0:T(1,128)}), f32[16,1,576]{2,1,0:T(1,128)S(1)}, u32[]{:S(2)}, u32[]{:S(2)}) async-start(f32[16,1,576]{2,1,0:T(1,128)} %reshape.90), calls=%async_computation.1 | async-start | bytes 81920 | tf_op jit(solution)/shard_map/all_to_all | solution.py:34

commit v11 on v7

--- a/solution.py
+++ b/solution.py
@@ -101,7 +101,7 @@
     head_eye = jnp.eye(KVH, dtype=queries.dtype)[None, :, None, :, None]
     spread_queries = (query_heads[:, :, :, None, :] * head_eye).reshape(request_count, QH, KVH * HD)
     scores = (
-        jnp.einsum("rhc,rpc->rhp", spread_queries, key_cache, preferred_element_type=jnp.float32)
+        jnp.einsum("rpc,rhc->rph", key_cache, spread_queries, preferred_element_type=jnp.float32)
         * score_scale
     )
     score_new = (
@@ -109,15 +109,15 @@
         * score_scale
     )
     positions = jnp.arange(key_cache.shape[1], dtype=jnp.int32)
-    live_mask = (positions[None, :] < lengths[:, None])[:, None, :]
+    live_mask = (positions[None, :] < lengths[:, None])[:, :, None]
     masked = jnp.where(live_mask, scores, FLOOR)
-    largest = jnp.maximum(jnp.max(masked, axis=-1), score_new)
-    weights = jnp.where(live_mask, jnp.exp(masked - largest[..., None]), 0.0)
+    largest = jnp.maximum(jnp.max(masked, axis=1), score_new)
+    weights = jnp.where(live_mask, jnp.exp(masked - largest[:, None, :]), 0.0)
     weight_new = jnp.exp(score_new - largest)
-    denoms = jnp.sum(weights, axis=-1) + weight_new
+    denoms = jnp.sum(weights, axis=1) + weight_new
     rounded_new = weight_new.astype(jnp.bfloat16).astype(jnp.float32)
     spread_totals = jnp.einsum(
-        "rhp,rpc->rhc", weights.astype(jnp.bfloat16), value_cache, preferred_element_type=jnp.float32
+        "rph,rpc->rhc", weights.astype(jnp.bfloat16), value_cache, preferred_element_type=jnp.float32
     ) + rounded_new[..., None] * new_values[:, None, :].astype(jnp.float32)
     spread_totals = spread_totals / denoms[..., None]
     totals = jnp.sum(

time: 123 us -> 123 us (level)
  no operation moved by 1% of the time
where the time goes in v11:
time: 123 us
  blocking collectives  73.1 us (59%)
  waiting for transfers between devices  15.9 us (13%)
  starting transfers between devices  11.1 us (9%)
  matrix products  7.53 us (6%)
  Pallas kernels  6.62 us (5%)
  local copies, waits for them, and re-layouts  4.32 us (4%)
  other arithmetic  3.75 us (3%)
    all_to_all x1, blocking collectives, local(): incoming = lax.all_to_all(outgoing, ('expert', 'ffn'), 0, 0, tiled=True)  39.1 us
    all_to_all x1, blocking collectives, local(): pieces = lax.all_to_all(partial_out, ('expert', 'ffn'), 0, 0, tiled=True)  34 us
    all_to_all x2, waiting for transfers between devices, gather_by_exchange(): return lax.all_to_all(copies, axis_name, 0, 0, tiled=True)  15.9 us
    all_to_all x2, starting transfers between devices, gather_by_exchange(): return lax.all_to_all(copies, axis_name, 0, 0, tiled=True)  11.1 us
    pallas_call x1, Pallas kernels, expert_block(): pl.pallas_call(expert_kernel, out_shape=jax.ShapeDtypeStruct(rows.shape,...  6.62 us
    dot_general x1, matrix products, attend_local(): jnp.einsum('rpc,rhc->rph', key_cache, spread_queries, preferred_element_t...  3.86 us
  transfers between devices with their start and end apart: 2, of which 2 were waited for; matrix products, arithmetic and copies ran while one was open for 1% of the time, Pallas kernels for 0%

profile of v11, /device:TPU:1, one launch (start us, length us, event | category | flops | bytes accessed | tf_op | source)
XLA Modules:
  0.0 122.6 jit_solution(9339086514060203166)
XLA Ops:
  0.0 0.9 iota_compare_fusion.3
  0.9 0.7 convert_element_type.73
  1.6 0.8 mul.94
  2.7 1.0 fusion.4
  3.7 3.9 %fusion.30 = (f32[4,32]{1,0:T(4,128)S(1)}, f32[4,512,32]{1,2,0:T(8,128)S(1)}) fusion(bf16[4,512,1024]{2,1,0:T(8,128)(2,1)} %param.17, bf16[4,32,1024]{2,1,0:T(8,128)(2,1)S(1)} %mul.96, bf16[32,1024]{1,0:T(8,128)(2,1)S(1)} %bitcast.52, pred[4,512]{1,0:T(4,128)(4,1)S(1)} %iota_compare_fusion.3), kind=kOutput, calls=%fused_computation.59 | convolution fusion | flops 134545280 | bytes 4786688 | tf_op jit(solution)/shard_map/rpc,rhc->rph/dot_general | solution.py:104
  7.6 0.2 fusion.7
  7.8 0.9 fusion
  8.8 0.2 multiply_reduce_fusion
  9.1 1.0 broadcast_in_dim.84
  10.1 7.6 %all-to-all-start = ((bf16[16,4,4096]{2,1,0:T(4,128)(2,1)}), bf16[16,4,4096]{2,1,0:T(4,128)(2,1)S(1)}, u32[]{:S(2)}, u32[]{:S(2)}) async-start(bf16[16,4,4096]{2,1,0:T(4,128)(2,1)} %broadcast_in_dim.84), calls=%async_computation | async-start | bytes 1048576 | tf_op jit(solution)/shard_map/all_to_all | solution.py:34
  18.6 9.5 %all-to-all-done = bf16[16,4,4096]{2,1,0:T(4,128)(2,1)S(1)} async-done(((bf16[16,4,4096]{2,1,0:T(4,128)(2,1)}), bf16[16,4,4096]{2,1,0:T(4,128)(2,1)S(1)}, u32[]{:S(2)}, u32[]{:S(2)}) %all-to-all-start) | async-done | bytes 524320 | tf_op jit(solution)/shard_map/all_to_all | solution.py:34
  28.2 0.6 multiply_reduce_fusion.1
  29.0 0.7 reshape.94
  29.7 3.5 %all-to-all-start.1 = ((f32[16,1,576]{2,1,0:T(1,128)}), f32[16,1,576]{2,1,0:T(1,128)S(1)}, u32[]{:S(2)}, u32[]{:S(2)}) async-start(f32[16,1,576]{2,1,0:T(1,128)} %reshape.94), calls=%async_computation.1 | async-start | bytes 81920 | tf_op jit(solution)/shard_map/all_to_all | solution.py:34
  33.2 6.5 %all-to-all-done.1 = f32[16,1,576]{2,1,0:T(1,128)S(1)} async-done(((f32[16,1,576]{2,1,0:T(1,128)}), f32[16,1,576]{2,1,0:T(1,128)S(1)}, u32[]{:S(2)}, u32[]{:S(2)}) %all-to-all-start.1) | async-done | bytes 36896 | tf_op jit(solution)/shard_map/all_to_all | solution.py:34
  39.7 0.5 broadcast.51
  40.2 0.7 reduce.1
  41.2 0.2 convolution_convert_fusion
  41.4 0.3 broadcast_in_dim.92
  41.7 39.1 %all_to_all.20 = bf16[128,32,256]{2,1,0:T(8,128)(2,1)S(1)} all-to-all(bf16[128,32,256]{2,1,0:T(8,128)(2,1)S(1)} %bitcast.43), channel_id=1, replica_groups=mesh['expert'=8,'ffn'=16] {'expert','ffn'}, dimensions={0} | all-to-all | bytes 4194304 | tf_op jit(solution)/shard_map/all_to_all | solution.py:191
  80.8 6.6 %shard_map.136 = bf16[8,16,32,256]{3,2,1,0:T(8,128)(2,1)S(1)} custom-call(bf16[8,16,32,256]{3,2,1,0:T(8,128)(2,1)S(1)} %bitcast.41, bf16[4096,512]{1,0:T(8,128)(2,1)} %bitcast.44, bf16[4096,512]{1,0:T(8,128)(2,1)} %bitcast.45, bf16[512,4096]{1,0:T(8,128)(2,1)} %bitcast.46), custom_call_target="tpu_custom_call" | custom-call | flops 3221225472 | bytes 16777216 | tf_op jit(solution)/shard_map/pallas_call | solution.py:75
  87.4 34.0 %all_to_all.21 = bf16[128,32,256]{2,1,0:T(8,128)(2,1)S(1)} all-to-all(bf16[128,32,256]{2,1,0:T(8,128)(2,1)S(1)} %bitcast.42), channel_id=1, replica_groups=mesh['expert'=8,'ffn'=16] {'expert','ffn'}, dimensions={0} | all-to-all | bytes 4194304 | tf_op jit(solution)/shard_map/all_to_all | solution.py:195
  121.4 0.3 bitcast_reduce_fusion
  121.8 0.8 fusion.3
  (42 shorter events, 1.9 us)
Async XLA Ops:
  0.0 28.2 %copy-start = (bf16[4096,256]{1,0:T(8,128)(2,1)S(1)}, bf16[4096,256]{1,0:T(8,128)(2,1)}, u32[]{:S(2)}) copy-start(bf16[4096,256]{1,0:T(8,128)(2,1)} %param.21) | copy-start | bytes 6291460
  2.7 5.1 %copy-start.1 = (bf16[4,512,1024]{2,1,0:T(8,128)(2,1)S(1)}, bf16[4,512,1024]{2,1,0:T(8,128)(2,1)}, u32[]{:S(2)}) copy-start(bf16[4,512,1024]{2,1,0:T(8,128)(2,1)} %param.18) | copy-start | bytes 12582916
  7.8 9.9 %copy-start.3 = (s32[64,2]{0,1:T(2,128)S(1)}, s32[64,2]{0,1:T(2,128)}, u32[]{:S(2)}) copy-start(s32[64,2]{0,1:T(2,128)} %param.27) | copy-start | bytes 1540
  7.8 20.4 %copy-start.2 = (bf16[64,256]{1,0:T(8,128)(2,1)S(1)}, bf16[64,256]{1,0:T(8,128)(2,1)}, u32[]{:S(2)}) copy-start(bf16[64,256]{1,0:T(8,128)(2,1)} %param.20) | copy-start | bytes 98308
  8.7 20.0 %copy-start.4 = (f32[256,8]{0,1:T(8,128)S(1)}, f32[256,8]{0,1:T(8,128)}, u32[]{:S(2)}) copy-start(f32[256,8]{0,1:T(8,128)} %param.23) | copy-start | bytes 24580
  8.7 20.0 %copy-start.5 = (f32[256]{0:T(256)S(1)}, f32[256]{0:T(256)}, u32[]{:S(2)}) copy-start(f32[256]{0:T(256)} %param.22) | copy-start | bytes 3076
  10.1 17.9 %all-to-all-start = ((bf16[16,4,4096]{2,1,0:T(4,128)(2,1)}), bf16[16,4,4096]{2,1,0:T(4,128)(2,1)S(1)}, u32[]{:S(2)}, u32[]{:S(2)}) async-start(bf16[16,4,4096]{2,1,0:T(4,128)(2,1)} %broadcast_in_dim.84), calls=%async_computation | async-start | bytes 1048576 | tf_op jit(solution)/shard_map/all_to_all | solution.py:34
  29.7 10.0 %all-to-all-start.1 = ((f32[16,1,576]{2,1,0:T(1,128)}), f32[16,1,576]{2,1,0:T(1,128)S(1)}, u32[]{:S(2)}, u32[]{:S(2)}) async-start(f32[16,1,576]{2,1,0:T(1,128)} %reshape.94), calls=%async_computation.1 | async-start | bytes 81920 | tf_op jit(solution)/shard_map/all_to_all | solution.py:34

commit v12 on v7

--- a/solution.py
+++ b/solution.py
@@ -38,21 +38,23 @@
     groups, blocks, capacity, width = rows_v.shape
     row_count = groups * capacity
     hidden_units = gate_v.shape[1]
+    rows_copy = pltpu.make_async_copy(rows_hbm, rows_v, sems.at[0, 0])
+    rows_copy.start()
     copies = []
     for block in range(blocks):
         span = pl.ds(block * width, width)
-        trio = (
-            pltpu.make_async_copy(rows_hbm.at[:, block], rows_v.at[:, block], sems.at[0, block]),
+        pair = (
             pltpu.make_async_copy(gate_hbm.at[span], gate_v.at[span], sems.at[1, block]),
             pltpu.make_async_copy(up_hbm.at[span], up_v.at[span], sems.at[2, block]),
         )
-        for copy in trio:
+        for copy in pair:
             copy.start()
-        copies.append(trio)
+        copies.append(pair)
     down_copy = pltpu.make_async_copy(down_hbm, down_v, sems.at[3, 0])
     down_copy.start()
     gate_sum = jnp.zeros((row_count, hidden_units), jnp.float32)
     up_sum = jnp.zeros((row_count, hidden_units), jnp.float32)
+    rows_copy.wait()
     for block in range(blocks):
         for copy in copies[block]:
             copy.wait()

time: 123 us -> 123 us (level)
  no operation moved by 1% of the time
where the time goes in v12:
time: 123 us
  blocking collectives  73.1 us (59%)
  waiting for transfers between devices  15.9 us (13%)
  starting transfers between devices  11.1 us (9%)
  matrix products  7.53 us (6%)
  Pallas kernels  6.66 us (5%)
  local copies, waits for them, and re-layouts  4.32 us (4%)
  other arithmetic  3.75 us (3%)
    all_to_all x1, blocking collectives, local(): incoming = lax.all_to_all(outgoing, ('expert', 'ffn'), 0, 0, tiled=True)  39.1 us
    all_to_all x1, blocking collectives, local(): pieces = lax.all_to_all(partial_out, ('expert', 'ffn'), 0, 0, tiled=True)  34 us
    all_to_all x2, waiting for transfers between devices, gather_by_exchange(): return lax.all_to_all(copies, axis_name, 0, 0, tiled=True)  15.9 us
    all_to_all x2, starting transfers between devices, gather_by_exchange(): return lax.all_to_all(copies, axis_name, 0, 0, tiled=True)  11.1 us
    pallas_call x1, Pallas kernels, expert_block(): pl.pallas_call(expert_kernel, out_shape=jax.ShapeDtypeStruct(rows.shape,...  6.66 us
    dot_general x1, matrix products, attend_local(): jnp.einsum('rhc,rpc->rhp', spread_queries, key_cache, preferred_element_t...  3.86 us
  transfers between devices with their start and end apart: 2, of which 2 were waited for; matrix products, arithmetic and copies ran while one was open for 1% of the time, Pallas kernels for 0%

profile of v12, /device:TPU:1, one launch (start us, length us, event | category | flops | bytes accessed | tf_op | source)
XLA Modules:
  0.0 122.6 jit_solution(5163429121444015954)
XLA Ops:
  0.0 0.9 iota_compare_fusion.3
  0.9 0.7 convert_element_type.73
  1.6 0.8 mul.93
  2.7 1.0 fusion.3
  3.7 3.9 %fusion.29 = (f32[4,32]{1,0:T(4,128)S(1)}, f32[4,32,512]{2,1,0:T(8,128)S(1)}) fusion(bf16[4,512,1024]{2,1,0:T(8,128)(2,1)} %param.17, bf16[4,32,1024]{2,1,0:T(8,128)(2,1)S(1)} %mul.95, bf16[32,1024]{1,0:T(8,128)(2,1)S(1)} %bitcast.50, pred[4,512]{1,0:T(4,128)(4,1)S(1)} %iota_compare_fusion.3), kind=kOutput, calls=%fused_computation.58 | convolution fusion | flops 134545280 | bytes 4786688 | tf_op jit(solution)/shard_map/rhc,rpc->rhp/dot_general | solution.py:106
  7.6 0.2 fusion.6
  7.8 0.9 fusion
  8.8 0.2 multiply_reduce_fusion
  9.1 1.0 broadcast_in_dim.81
  10.1 7.6 %all-to-all-start = ((bf16[16,4,4096]{2,1,0:T(4,128)(2,1)}), bf16[16,4,4096]{2,1,0:T(4,128)(2,1)S(1)}, u32[]{:S(2)}, u32[]{:S(2)}) async-start(bf16[16,4,4096]{2,1,0:T(4,128)(2,1)} %broadcast_in_dim.81), calls=%async_computation | async-start | bytes 1048576 | tf_op jit(solution)/shard_map/all_to_all | solution.py:34
  18.6 9.5 %all-to-all-done = bf16[16,4,4096]{2,1,0:T(4,128)(2,1)S(1)} async-done(((bf16[16,4,4096]{2,1,0:T(4,128)(2,1)}), bf16[16,4,4096]{2,1,0:T(4,128)(2,1)S(1)}, u32[]{:S(2)}, u32[]{:S(2)}) %all-to-all-start) | async-done | bytes 524320 | tf_op jit(solution)/shard_map/all_to_all | solution.py:34
  28.2 0.6 multiply_reduce_fusion.1
  29.0 0.7 reshape.90
  29.7 3.5 %all-to-all-start.1 = ((f32[16,1,576]{2,1,0:T(1,128)}), f32[16,1,576]{2,1,0:T(1,128)S(1)}, u32[]{:S(2)}, u32[]{:S(2)}) async-start(f32[16,1,576]{2,1,0:T(1,128)} %reshape.90), calls=%async_computation.1 | async-start | bytes 81920 | tf_op jit(solution)/shard_map/all_to_all | solution.py:34
  33.2 6.5 %all-to-all-done.1 = f32[16,1,576]{2,1,0:T(1,128)S(1)} async-done(((f32[16,1,576]{2,1,0:T(1,128)}), f32[16,1,576]{2,1,0:T(1,128)S(1)}, u32[]{:S(2)}, u32[]{:S(2)}) %all-to-all-start.1) | async-done | bytes 36896 | tf_op jit(solution)/shard_map/all_to_all | solution.py:34
  39.7 0.5 broadcast.41
  40.2 0.7 reduce.1
  41.2 0.2 convolution_convert_fusion
  41.4 0.3 broadcast_in_dim.89
  41.7 39.1 %all_to_all.20 = bf16[128,32,256]{2,1,0:T(8,128)(2,1)S(1)} all-to-all(bf16[128,32,256]{2,1,0:T(8,128)(2,1)S(1)} %bitcast.41), channel_id=1, replica_groups=mesh['expert'=8,'ffn'=16] {'expert','ffn'}, dimensions={0} | all-to-all | bytes 4194304 | tf_op jit(solution)/shard_map/all_to_all | solution.py:193
  80.8 6.7 %shard_map.136 = bf16[8,16,32,256]{3,2,1,0:T(8,128)(2,1)S(1)} custom-call(bf16[8,16,32,256]{3,2,1,0:T(8,128)(2,1)S(1)} %bitcast.39, bf16[4096,512]{1,0:T(8,128)(2,1)} %bitcast.42, bf16[4096,512]{1,0:T(8,128)(2,1)} %bitcast.43, bf16[512,4096]{1,0:T(8,128)(2,1)} %bitcast.44), custom_call_target="tpu_custom_call" | custom-call | flops 3221225472 | bytes 16777216 | tf_op jit(solution)/shard_map/pallas_call | solution.py:77
  87.4 34.0 %all_to_all.21 = bf16[128,32,256]{2,1,0:T(8,128)(2,1)S(1)} all-to-all(bf16[128,32,256]{2,1,0:T(8,128)(2,1)S(1)} %bitcast.40), channel_id=1, replica_groups=mesh['expert'=8,'ffn'=16] {'expert','ffn'}, dimensions={0} | all-to-all | bytes 4194304 | tf_op jit(solution)/shard_map/all_to_all | solution.py:197
  121.5 0.3 bitcast_reduce_fusion
  121.8 0.8 fusion.2
  (42 shorter events, 1.9 us)
Async XLA Ops:
  0.0 28.2 %copy-start = (bf16[4096,256]{1,0:T(8,128)(2,1)S(1)}, bf16[4096,256]{1,0:T(8,128)(2,1)}, u32[]{:S(2)}) copy-start(bf16[4096,256]{1,0:T(8,128)(2,1)} %param.21) | copy-start | bytes 6291460
  2.7 5.1 %copy-start.1 = (bf16[4,512,1024]{2,1,0:T(8,128)(2,1)S(1)}, bf16[4,512,1024]{2,1,0:T(8,128)(2,1)}, u32[]{:S(2)}) copy-start(bf16[4,512,1024]{2,1,0:T(8,128)(2,1)} %param.18) | copy-start | bytes 12582916
  7.8 9.9 %copy-start.3 = (s32[64,2]{0,1:T(2,128)S(1)}, s32[64,2]{0,1:T(2,128)}, u32[]{:S(2)}) copy-start(s32[64,2]{0,1:T(2,128)} %param.27) | copy-start | bytes 1540
  7.8 20.4 %copy-start.2 = (bf16[64,256]{1,0:T(8,128)(2,1)S(1)}, bf16[64,256]{1,0:T(8,128)(2,1)}, u32[]{:S(2)}) copy-start(bf16[64,256]{1,0:T(8,128)(2,1)} %param.20) | copy-start | bytes 98308
  8.7 20.0 %copy-start.4 = (f32[256,8]{0,1:T(8,128)S(1)}, f32[256,8]{0,1:T(8,128)}, u32[]{:S(2)}) copy-start(f32[256,8]{0,1:T(8,128)} %param.23) | copy-start | bytes 24580
  8.7 20.0 %copy-start.5 = (f32[256]{0:T(256)S(1)}, f32[256]{0:T(256)}, u32[]{:S(2)}) copy-start(f32[256]{0:T(256)} %param.22) | copy-start | bytes 3076
  10.1 17.9 %all-to-all-start = ((bf16[16,4,4096]{2,1,0:T(4,128)(2,1)}), bf16[16,4,4096]{2,1,0:T(4,128)(2,1)S(1)}, u32[]{:S(2)}, u32[]{:S(2)}) async-start(bf16[16,4,4096]{2,1,0:T(4,128)(2,1)} %broadcast_in_dim.81), calls=%async_computation | async-start | bytes 1048576 | tf_op jit(solution)/shard_map/all_to_all | solution.py:34
  29.7 10.0 %all-to-all-start.1 = ((f32[16,1,576]{2,1,0:T(1,128)}), f32[16,1,576]{2,1,0:T(1,128)S(1)}, u32[]{:S(2)}, u32[]{:S(2)}) async-start(f32[16,1,576]{2,1,0:T(1,128)} %reshape.90), calls=%async_computation.1 | async-start | bytes 81920 | tf_op jit(solution)/shard_map/all_to_all | solution.py:34
